TPU v7x, 512 devices: a whole 4x8x8 slice. The times are simulated.
512 devices in a mesh: section: 16 (over x_hi, y), dp: 8 (over z), mp: 4 (over x_lo, core).
Axes of the slice: x: 4 (x_hi: 2, x_lo: 2; x = x_hi * 2 + x_lo), y: 8, z: 8, core: 2. Of those that a mesh axis runs over, the one named last changes fastest.
Arguments:
- cotangent: bfloat16 [1024, 4096], P('dp', 'mp'), may hold values from -6 to 6
- saved_inputs: bfloat16 [16, 1024, 4096], P('section', 'dp', 'mp'), may hold values from -6 to 6
- pre_acts: bfloat16 [16, 1024, 4096], P('section', 'dp', 'mp'), may hold values from -8 to 8
- weights: bfloat16 [16, 4096, 4096], P('section', 'mp', 'dp'), may hold values from -0.046875 to 0.046875
- proj_in: bfloat16 [16, 4096, 64], P('section', 'mp'), may hold values from -0.09375 to 0.09375
- proj_out: bfloat16 [16, 4096, 64], P('section', 'mp'), may hold values from -0.09375 to 0.09375
- query_panels: float32 [16, 16, 4096], P('section', 'dp', 'mp'), may hold values from -4 to 4
- partners: int32 [8, 8], replicated, may hold values from 0 to 7, as said below
Outputs:
- train_panels: float32 [16, 32, 4096], P('section', 'dp', 'mp')
- scores: float32 [16, 8, 4], replicated
Inputs may be any that keep to these rules, and one draw needn't show every extreme that they name: The plan has 8 rounds: one round pairs every dp index with itself, and the others are the rounds of one round-robin plan of the 8 indices. The rows of partners hold each of these rounds once, in some order, so partners[r, partners[r, i]] = i.
All inputs are finite; a program needn't handle non-finite values.
Results may differ from a plain program's by a relative error of at most 0.02.
Values may be sent and summed in bfloat16 or wider, within the bound.
No kernel may reach another device: no remote copies, remote signals or barrier semaphores. Data moves between devices by JAX's collectives and lax.ppermute only.
A program may use at most 64 MiB of HBM per device.

v0:
```python
import math

import jax
import jax.numpy as jnp
from jax import lax
from jax.sharding import PartitionSpec as P

LEN = 32


def from_behind(block, axis, distance):
    devices = range(lax.axis_size(axis))
    route = [(i - distance, i) for i in devices if i - distance in devices]
    return lax.ppermute(block, axis, route)


def silu_slope(pre_state):
    sigma = jax.nn.sigmoid(pre_state)
    return sigma * (1.0 + pre_state * (1.0 - sigma))


def score_pair(query_rows, train_rows):
    return jnp.dot(query_rows, train_rows.T, precision=lax.Precision.HIGHEST)


def place_block(score_table, block, row_at, col_at):
    return lax.dynamic_update_slice(
        score_table,
        block[None, None],
        (jnp.asarray(row_at, jnp.int32), jnp.int32(col_at), jnp.int32(0), jnp.int32(0)),
    )


def body(cotangent, saved_inputs, pre_acts, weights, proj_in, proj_out, query_panels, partners):
    section_count = lax.axis_size("section")
    model_count = lax.axis_size("mp")
    data_count = lax.axis_size("dp")
    section_index = lax.axis_index("section")
    model_index = lax.axis_index("mp")
    data_index = lax.axis_index("dp")
    inputs = saved_inputs[0]
    pre_state = pre_acts[0]
    columns = inputs.shape[1]
    length = LEN
    examples = inputs.shape[0] // length
    low_rank = proj_in.shape[2]
    w_rows = lax.all_gather(weights[0], "dp", axis=1, tiled=True)
    step_count = examples + section_count - 1
    top_section = section_count - 1

    def advance(turn, carry):
        outgoing, stored, side_store = carry
        received = from_behind(outgoing, "section", -1)
        example_at = turn - (top_section - section_index)
        active = jnp.logical_and(example_at >= 0, example_at < examples)
        row_start = jnp.clip(example_at, 0, examples - 1) * length
        top_grad = lax.dynamic_slice_in_dim(cotangent, row_start, length, 0)
        delta_piece = jnp.where(section_index == top_section, top_grad, received)
        slopes = silu_slope(
            lax.dynamic_slice_in_dim(pre_state, row_start, length, 0).astype(jnp.float32)
        )
        grad_piece = (delta_piece.astype(jnp.float32) * slopes).astype(jnp.bfloat16)
        grad_full = lax.all_gather(grad_piece, "mp", axis=1, tiled=True)

        def through():
            back_term = lax.dot_general(
                grad_full, w_rows, (((1,), (1,)), ((), ())), preferred_element_type=jnp.float32
            )
            return (delta_piece.astype(jnp.float32) + back_term).astype(jnp.bfloat16)

        def skipped():
            return jnp.zeros_like(delta_piece)

        passed = lax.cond(active, through, skipped)
        previous = lax.dynamic_slice_in_dim(stored, row_start, length, 0)
        stored = lax.dynamic_update_slice_in_dim(
            stored, jnp.where(active, grad_piece, previous), row_start, 0
        )
        return (passed, stored, side_store)

    initial = (
        jnp.zeros((length, columns), jnp.bfloat16),
        jnp.zeros((inputs.shape[0], columns), jnp.bfloat16),
        jnp.zeros((inputs.shape[0], low_rank), jnp.float32),
    )
    final_state = lax.fori_loop(0, step_count, advance, initial)
    stored = final_state[1]
    side_store = final_state[2]
    in_part = jnp.dot(inputs, proj_in[0], preferred_element_type=jnp.float32)
    out_part = jnp.dot(stored, proj_out[0], preferred_element_type=jnp.float32)
    in_side, out_side = (
        lax.psum(in_part.astype(jnp.bfloat16), "mp").astype(jnp.float32),
        lax.psum(out_part.astype(jnp.bfloat16), "mp").astype(jnp.float32),
    )
    piece_rank = low_rank // model_count
    in_rows = lax.dynamic_slice_in_dim(in_side, model_index * piece_rank, piece_rank, 1)
    panels_here = jnp.einsum(
        "etr,etc->erc",
        in_rows.reshape(examples, length, piece_rank),
        out_side.reshape(examples, length, low_rank),
        precision=lax.Precision.HIGHEST,
    ) / math.sqrt(length)
    panels_here = panels_here.reshape(examples, piece_rank * low_rank)
    queries = query_panels[0]
    asked = queries.shape[0]
    rounds = partners.shape[0]
    score_scale = 1.0 / (low_rank * math.sqrt(section_count))
    score_table = jnp.zeros((data_count, rounds, asked, examples), jnp.float32)
    everyone = lax.all_gather(panels_here, "dp", axis=0, tiled=True).reshape(
        data_count, examples, -1
    )
    for round_at in range(rounds):
        partner = partners[round_at, data_index]
        chosen = lax.dynamic_index_in_dim(everyone, partner, 0, keepdims=False)
        score_table = place_block(score_table, score_pair(queries, chosen), data_index, round_at)
    summed = lax.psum(score_table * score_scale, ("section", "dp", "mp"))
    scores = summed.transpose(0, 2, 1, 3).reshape(data_count * asked, rounds, examples)
    return (panels_here[None], scores)


def solution(mesh):
    placed = (
        P("dp", "mp"),
        P("section", "dp", "mp"),
        P("section", "dp", "mp"),
        P("section", "mp", "dp"),
        P("section", "mp", None),
        P("section", "mp", None),
        P("section", "dp", "mp"),
        P(),
    )
    return jax.shard_map(
        body, mesh=mesh, in_specs=placed, out_specs=(P("section", "dp", "mp"), P()), check_vma=False
    )
```

profile of v0, /device:TPU:56, one launch (start us, length us, event | category | flops | bytes accessed | tf_op | source)
XLA Modules:
  0.0 633.4 jit_solution(11931362347134518088)
XLA Ops:
  25.3 86.4 %all-gather.4.cloned.1.call-done = bf16[1,1024,4096]{2,1,0:T(8,128)(2,1)} async-done(((bf16[1,1024,512]{2,1,0:T(8,128)(2,1)}), bf16[1,1024,4096]{2,1,0:T(8,128)(2,1)}) %all-gather.4.cloned.1.call-update) | async-done | bytes 8388624 | tf_op jit(solution)/shard_map/all_gather | solution.py:47
  112.4 366.9 %while.17 = (s32[]{:T(128)}, bf16[32,1024]{1,0:T(8,128)(2,1)}, bf16[128,1024]{1,0:T(8,128)(2,1)S(1)}, s32[]{:T(128)}, pred[]{:T(512)}, /*index=5*/bf16[128,1024]...) while((s32[]{:T(128)}, bf16[32,1024]{1,0:T(8,128)(2,1)}, ...), condition=%wide.region_4.5_spmd, body=%wide.region_1.4_spmd.sunk | while | flops 268959744 | bytes 9830719 | solution.py:86
  115.9 6.6 %collective-permute-done = bf16[32,1024]{1,0:T(8,128)(2,1)S(1)} collective-permute-done((bf16[32,1024]{1,0:T(8,128)(2,1)}, bf16[32,1024]{1,0:T(8,128)(2,1)S(1)}, u32[]{:S(2)}, u32[]{:S(2)}) %collective-permute-start) | collective-permute-done | bytes 65568 | tf_op jit(solution)/shard_map/while/body/eval_jaxpr/ppermute | solution.py:14
  131.8 8.1 %collective-permute-done = bf16[32,1024]{1,0:T(8,128)(2,1)S(1)} collective-permute-done((bf16[32,1024]{1,0:T(8,128)(2,1)}, bf16[32,1024]{1,0:T(8,128)(2,1)S(1)}, u32[]{:S(2)}, u32[]{:S(2)}) %collective-permute-start) | collective-permute-done | bytes 65568 | tf_op jit(solution)/shard_map/while/body/eval_jaxpr/ppermute | solution.py:14
  149.2 8.1 %collective-permute-done = bf16[32,1024]{1,0:T(8,128)(2,1)S(1)} collective-permute-done((bf16[32,1024]{1,0:T(8,128)(2,1)}, bf16[32,1024]{1,0:T(8,128)(2,1)S(1)}, u32[]{:S(2)}, u32[]{:S(2)}) %collective-permute-start) | collective-permute-done | bytes 65568 | tf_op jit(solution)/shard_map/while/body/eval_jaxpr/ppermute | solution.py:14
  166.7 8.1 %collective-permute-done = bf16[32,1024]{1,0:T(8,128)(2,1)S(1)} collective-permute-done((bf16[32,1024]{1,0:T(8,128)(2,1)}, bf16[32,1024]{1,0:T(8,128)(2,1)S(1)}, u32[]{:S(2)}, u32[]{:S(2)}) %collective-permute-start) | collective-permute-done | bytes 65568 | tf_op jit(solution)/shard_map/while/body/eval_jaxpr/ppermute | solution.py:14
  184.1 8.1 %collective-permute-done = bf16[32,1024]{1,0:T(8,128)(2,1)S(1)} collective-permute-done((bf16[32,1024]{1,0:T(8,128)(2,1)}, bf16[32,1024]{1,0:T(8,128)(2,1)S(1)}, u32[]{:S(2)}, u32[]{:S(2)}) %collective-permute-start) | collective-permute-done | bytes 65568 | tf_op jit(solution)/shard_map/while/body/eval_jaxpr/ppermute | solution.py:14
  201.5 8.1 %collective-permute-done = bf16[32,1024]{1,0:T(8,128)(2,1)S(1)} collective-permute-done((bf16[32,1024]{1,0:T(8,128)(2,1)}, bf16[32,1024]{1,0:T(8,128)(2,1)S(1)}, u32[]{:S(2)}, u32[]{:S(2)}) %collective-permute-start) | collective-permute-done | bytes 65568 | tf_op jit(solution)/shard_map/while/body/eval_jaxpr/ppermute | solution.py:14
  218.9 8.1 %collective-permute-done = bf16[32,1024]{1,0:T(8,128)(2,1)S(1)} collective-permute-done((bf16[32,1024]{1,0:T(8,128)(2,1)}, bf16[32,1024]{1,0:T(8,128)(2,1)S(1)}, u32[]{:S(2)}, u32[]{:S(2)}) %collective-permute-start) | collective-permute-done | bytes 65568 | tf_op jit(solution)/shard_map/while/body/eval_jaxpr/ppermute | solution.py:14
  236.4 8.1 %collective-permute-done = bf16[32,1024]{1,0:T(8,128)(2,1)S(1)} collective-permute-done((bf16[32,1024]{1,0:T(8,128)(2,1)}, bf16[32,1024]{1,0:T(8,128)(2,1)S(1)}, u32[]{:S(2)}, u32[]{:S(2)}) %collective-permute-start) | collective-permute-done | bytes 65568 | tf_op jit(solution)/shard_map/while/body/eval_jaxpr/ppermute | solution.py:14
  253.8 19.7 %collective-permute-done = bf16[32,1024]{1,0:T(8,128)(2,1)S(1)} collective-permute-done((bf16[32,1024]{1,0:T(8,128)(2,1)}, bf16[32,1024]{1,0:T(8,128)(2,1)S(1)}, u32[]{:S(2)}, u32[]{:S(2)}) %collective-permute-start) | collective-permute-done | bytes 65568 | tf_op jit(solution)/shard_map/while/body/eval_jaxpr/ppermute | solution.py:14
  280.3 6.6 %conditional.2 = (bf16[32,1024]{1,0:T(8,128)(2,1)}) conditional(s32[]{:T(128)} %convert_element_type.80, () %tuple.60, (bf16[32,1024]{1,0:T(8,128)(2,1)S(1)}, bf16[32,4096]{1,0:T(8,128)(2,1)S(1)}, bf16[1024,4096]{1,0:T(8,128)(2,1)}) %tuple.61), branch_computations={%region_2.2_spmd, %region_3.3_spmd} | conditional | flops 268533760 | bytes 8781832 | solution.py:74
  288.8 8.1 %collective-permute-done = bf16[32,1024]{1,0:T(8,128)(2,1)S(1)} collective-permute-done((bf16[32,1024]{1,0:T(8,128)(2,1)}, bf16[32,1024]{1,0:T(8,128)(2,1)S(1)}, u32[]{:S(2)}, u32[]{:S(2)}) %collective-permute-start) | collective-permute-done | bytes 65568 | tf_op jit(solution)/shard_map/while/body/eval_jaxpr/ppermute | solution.py:14
  312.2 8.2 %collective-permute-done = bf16[32,1024]{1,0:T(8,128)(2,1)S(1)} collective-permute-done((bf16[32,1024]{1,0:T(8,128)(2,1)}, bf16[32,1024]{1,0:T(8,128)(2,1)S(1)}, u32[]{:S(2)}, u32[]{:S(2)}) %collective-permute-start) | collective-permute-done | bytes 65568 | tf_op jit(solution)/shard_map/while/body/eval_jaxpr/ppermute | solution.py:14
  335.6 8.1 %collective-permute-done = bf16[32,1024]{1,0:T(8,128)(2,1)S(1)} collective-permute-done((bf16[32,1024]{1,0:T(8,128)(2,1)}, bf16[32,1024]{1,0:T(8,128)(2,1)S(1)}, u32[]{:S(2)}, u32[]{:S(2)}) %collective-permute-start) | collective-permute-done | bytes 65568 | tf_op jit(solution)/shard_map/while/body/eval_jaxpr/ppermute | solution.py:14
  359.0 8.2 %collective-permute-done = bf16[32,1024]{1,0:T(8,128)(2,1)S(1)} collective-permute-done((bf16[32,1024]{1,0:T(8,128)(2,1)}, bf16[32,1024]{1,0:T(8,128)(2,1)S(1)}, u32[]{:S(2)}, u32[]{:S(2)}) %collective-permute-start) | collective-permute-done | bytes 65568 | tf_op jit(solution)/shard_map/while/body/eval_jaxpr/ppermute | solution.py:14
  394.1 8.1 %collective-permute-done = bf16[32,1024]{1,0:T(8,128)(2,1)S(1)} collective-permute-done((bf16[32,1024]{1,0:T(8,128)(2,1)}, bf16[32,1024]{1,0:T(8,128)(2,1)S(1)}, u32[]{:S(2)}, u32[]{:S(2)}) %collective-permute-start) | collective-permute-done | bytes 65568 | tf_op jit(solution)/shard_map/while/body/eval_jaxpr/ppermute | solution.py:14
  411.5 8.1 %collective-permute-done = bf16[32,1024]{1,0:T(8,128)(2,1)S(1)} collective-permute-done((bf16[32,1024]{1,0:T(8,128)(2,1)}, bf16[32,1024]{1,0:T(8,128)(2,1)S(1)}, u32[]{:S(2)}, u32[]{:S(2)}) %collective-permute-start) | collective-permute-done | bytes 65568 | tf_op jit(solution)/shard_map/while/body/eval_jaxpr/ppermute | solution.py:14
  428.9 8.1 %collective-permute-done = bf16[32,1024]{1,0:T(8,128)(2,1)S(1)} collective-permute-done((bf16[32,1024]{1,0:T(8,128)(2,1)}, bf16[32,1024]{1,0:T(8,128)(2,1)S(1)}, u32[]{:S(2)}, u32[]{:S(2)}) %collective-permute-start) | collective-permute-done | bytes 65568 | tf_op jit(solution)/shard_map/while/body/eval_jaxpr/ppermute | solution.py:14
  446.4 8.1 %collective-permute-done = bf16[32,1024]{1,0:T(8,128)(2,1)S(1)} collective-permute-done((bf16[32,1024]{1,0:T(8,128)(2,1)}, bf16[32,1024]{1,0:T(8,128)(2,1)S(1)}, u32[]{:S(2)}, u32[]{:S(2)}) %collective-permute-start) | collective-permute-done | bytes 65568 | tf_op jit(solution)/shard_map/while/body/eval_jaxpr/ppermute | solution.py:14
  463.8 8.1 %collective-permute-done = bf16[32,1024]{1,0:T(8,128)(2,1)S(1)} collective-permute-done((bf16[32,1024]{1,0:T(8,128)(2,1)}, bf16[32,1024]{1,0:T(8,128)(2,1)S(1)}, u32[]{:S(2)}, u32[]{:S(2)}) %collective-permute-start) | collective-permute-done | bytes 65568 | tf_op jit(solution)/shard_map/while/body/eval_jaxpr/ppermute | solution.py:14
  479.6 11.1 %all-reduce = (bf16[4,32,64]{2,1,0:T(8,128)(2,1)S(1)}, bf16[128,64]{0,1:T(8,128)(2,1)S(1)}) all-reduce(bf16[4,32,64]{2,1,0:T(8,128)(2,1)S(1)} %bitcast.104, bf16[128,64]{0,1:T(8,128)(2,1)S(1)} %convolution_convert_fusion.1), channel_id=1, replica_groups=mesh['section'=16,'dp'=8,'mp'=4] {'mp'}, use_global_device_ids=true, to_apply=%region_5.6 | all-reduce | flops 16384 | bytes 65536 | tf_op jit(solution)/shard_map/psum | solution.py:93
  491.0 24.6 %all-gather.1 = f32[8,4,1024]{2,1,0:T(4,128)S(1)} all-gather(f32[1,4,1024]{2,1,0:T(4,128)S(1)} %broadcast_in_dim_reshape.3), channel_id=1, replica_groups=mesh['section'=16,'dp'=8,'mp'=4] {'dp'}, dimensions={0}, use_global_device_ids=true | all-gather | bytes 147456 | tf_op jit(solution)/shard_map/all_gather | solution.py:109
  520.3 105.6 %psum.23 = f32[16,8,4]{1,0,2:T(8,128)S(1)} all-reduce(f32[16,8,4]{1,0,2:T(8,128)S(1)} %bitcast.105), channel_id=1, replica_groups=mesh['section'=16,'dp'=8,'mp'=4] {'section','dp','mp'}, use_global_device_ids=true, to_apply=%region_6.7 | all-reduce | flops 512 | bytes 4096 | tf_op jit(solution)/shard_map/psum | solution.py:116
  (142 shorter events, 249.4 us)
Async XLA Ops:
  7.2 17.0 %copy-start = (bf16[1,128,1024]{2,1,0:T(8,128)(2,1)S(1)}, bf16[1,128,1024]{2,1,0:T(8,128)(2,1)}, u32[]{:S(2)}) copy-start(bf16[1,128,1024]{2,1,0:T(8,128)(2,1)} %param.13) | copy-start | bytes 786436
  7.2 104.5 %all-gather.4.cloned.1.call-start = ((), (), s32[]{:S(2)}) async-start(), calls=%async_computation | async-start | bytes 9437184 | tf_op jit(solution)/shard_map/all_gather | solution.py:47
  112.4 366.9 %copy-start.2 = (bf16[1,1024,64]{1,2,0:T(8,128)(2,1)S(1)}, bf16[1,1024,64]{1,2,0:T(8,128)(2,1)}, u32[]{:S(2)}) copy-start(bf16[1,1024,64]{1,2,0:T(8,128)(2,1)} %param.17) | copy-start | bytes 393220
  112.4 403.2 %copy-start.1 = (f32[1,2,1024]{2,1,0:T(2,128)S(1)}, f32[1,2,1024]{2,1,0:T(2,128)}, u32[]{:S(2)}) copy-start(f32[1,2,1024]{2,1,0:T(2,128)} %param.18) | copy-start | bytes 24580
  112.4 10.1 %collective-permute-start = (bf16[32,1024]{1,0:T(8,128)(2,1)}, bf16[32,1024]{1,0:T(8,128)(2,1)S(1)}, u32[]{:S(2)}, u32[]{:S(2)}) collective-permute-start(bf16[32,1024]{1,0:T(8,128)(2,1)} %get-tuple-element.299), channel_id=1, source_target_pairs={{32,0},{64,32},{96,64},{128,96},{160,128},{192,160},{224,192},{256... | collective-permute-start | bytes 196616 | tf_op jit(solution)/shard_map/while/body/eval_jaxpr/ppermute | solution.py:14
  129.9 10.0 %collective-permute-start = (bf16[32,1024]{1,0:T(8,128)(2,1)}, bf16[32,1024]{1,0:T(8,128)(2,1)S(1)}, u32[]{:S(2)}, u32[]{:S(2)}) collective-permute-start(bf16[32,1024]{1,0:T(8,128)(2,1)} %get-tuple-element.299), channel_id=1, source_target_pairs={{32,0},{64,32},{96,64},{128,96},{160,128},{192,160},{224,192},{256... | collective-permute-start | bytes 196616 | tf_op jit(solution)/shard_map/while/body/eval_jaxpr/ppermute | solution.py:14
  147.3 10.0 %collective-permute-start = (bf16[32,1024]{1,0:T(8,128)(2,1)}, bf16[32,1024]{1,0:T(8,128)(2,1)S(1)}, u32[]{:S(2)}, u32[]{:S(2)}) collective-permute-start(bf16[32,1024]{1,0:T(8,128)(2,1)} %get-tuple-element.299), channel_id=1, source_target_pairs={{32,0},{64,32},{96,64},{128,96},{160,128},{192,160},{224,192},{256... | collective-permute-start | bytes 196616 | tf_op jit(solution)/shard_map/while/body/eval_jaxpr/ppermute | solution.py:14
  164.7 10.0 %collective-permute-start = (bf16[32,1024]{1,0:T(8,128)(2,1)}, bf16[32,1024]{1,0:T(8,128)(2,1)S(1)}, u32[]{:S(2)}, u32[]{:S(2)}) collective-permute-start(bf16[32,1024]{1,0:T(8,128)(2,1)} %get-tuple-element.299), channel_id=1, source_target_pairs={{32,0},{64,32},{96,64},{128,96},{160,128},{192,160},{224,192},{256... | collective-permute-start | bytes 196616 | tf_op jit(solution)/shard_map/while/body/eval_jaxpr/ppermute | solution.py:14
  182.2 10.0 %collective-permute-start = (bf16[32,1024]{1,0:T(8,128)(2,1)}, bf16[32,1024]{1,0:T(8,128)(2,1)S(1)}, u32[]{:S(2)}, u32[]{:S(2)}) collective-permute-start(bf16[32,1024]{1,0:T(8,128)(2,1)} %get-tuple-element.299), channel_id=1, source_target_pairs={{32,0},{64,32},{96,64},{128,96},{160,128},{192,160},{224,192},{256... | collective-permute-start | bytes 196616 | tf_op jit(solution)/shard_map/while/body/eval_jaxpr/ppermute | solution.py:14
  199.6 10.0 %collective-permute-start = (bf16[32,1024]{1,0:T(8,128)(2,1)}, bf16[32,1024]{1,0:T(8,128)(2,1)S(1)}, u32[]{:S(2)}, u32[]{:S(2)}) collective-permute-start(bf16[32,1024]{1,0:T(8,128)(2,1)} %get-tuple-element.299), channel_id=1, source_target_pairs={{32,0},{64,32},{96,64},{128,96},{160,128},{192,160},{224,192},{256... | collective-permute-start | bytes 196616 | tf_op jit(solution)/shard_map/while/body/eval_jaxpr/ppermute | solution.py:14
  217.0 10.0 %collective-permute-start = (bf16[32,1024]{1,0:T(8,128)(2,1)}, bf16[32,1024]{1,0:T(8,128)(2,1)S(1)}, u32[]{:S(2)}, u32[]{:S(2)}) collective-permute-start(bf16[32,1024]{1,0:T(8,128)(2,1)} %get-tuple-element.299), channel_id=1, source_target_pairs={{32,0},{64,32},{96,64},{128,96},{160,128},{192,160},{224,192},{256... | collective-permute-start | bytes 196616 | tf_op jit(solution)/shard_map/while/body/eval_jaxpr/ppermute | solution.py:14
  234.4 10.0 %collective-permute-start = (bf16[32,1024]{1,0:T(8,128)(2,1)}, bf16[32,1024]{1,0:T(8,128)(2,1)S(1)}, u32[]{:S(2)}, u32[]{:S(2)}) collective-permute-start(bf16[32,1024]{1,0:T(8,128)(2,1)} %get-tuple-element.299), channel_id=1, source_target_pairs={{32,0},{64,32},{96,64},{128,96},{160,128},{192,160},{224,192},{256... | collective-permute-start | bytes 196616 | tf_op jit(solution)/shard_map/while/body/eval_jaxpr/ppermute | solution.py:14
  251.9 21.7 %collective-permute-start = (bf16[32,1024]{1,0:T(8,128)(2,1)}, bf16[32,1024]{1,0:T(8,128)(2,1)S(1)}, u32[]{:S(2)}, u32[]{:S(2)}) collective-permute-start(bf16[32,1024]{1,0:T(8,128)(2,1)} %get-tuple-element.299), channel_id=1, source_target_pairs={{32,0},{64,32},{96,64},{128,96},{160,128},{192,160},{224,192},{256... | collective-permute-start | bytes 196616 | tf_op jit(solution)/shard_map/while/body/eval_jaxpr/ppermute | solution.py:14
  286.9 10.0 %collective-permute-start = (bf16[32,1024]{1,0:T(8,128)(2,1)}, bf16[32,1024]{1,0:T(8,128)(2,1)S(1)}, u32[]{:S(2)}, u32[]{:S(2)}) collective-permute-start(bf16[32,1024]{1,0:T(8,128)(2,1)} %get-tuple-element.299), channel_id=1, source_target_pairs={{32,0},{64,32},{96,64},{128,96},{160,128},{192,160},{224,192},{256... | collective-permute-start | bytes 196616 | tf_op jit(solution)/shard_map/while/body/eval_jaxpr/ppermute | solution.py:14
  310.3 10.1 %collective-permute-start = (bf16[32,1024]{1,0:T(8,128)(2,1)}, bf16[32,1024]{1,0:T(8,128)(2,1)S(1)}, u32[]{:S(2)}, u32[]{:S(2)}) collective-permute-start(bf16[32,1024]{1,0:T(8,128)(2,1)} %get-tuple-element.299), channel_id=1, source_target_pairs={{32,0},{64,32},{96,64},{128,96},{160,128},{192,160},{224,192},{256... | collective-permute-start | bytes 196616 | tf_op jit(solution)/shard_map/while/body/eval_jaxpr/ppermute | solution.py:14
  333.7 10.0 %collective-permute-start = (bf16[32,1024]{1,0:T(8,128)(2,1)}, bf16[32,1024]{1,0:T(8,128)(2,1)S(1)}, u32[]{:S(2)}, u32[]{:S(2)}) collective-permute-start(bf16[32,1024]{1,0:T(8,128)(2,1)} %get-tuple-element.299), channel_id=1, source_target_pairs={{32,0},{64,32},{96,64},{128,96},{160,128},{192,160},{224,192},{256... | collective-permute-start | bytes 196616 | tf_op jit(solution)/shard_map/while/body/eval_jaxpr/ppermute | solution.py:14
  357.1 10.1 %collective-permute-start = (bf16[32,1024]{1,0:T(8,128)(2,1)}, bf16[32,1024]{1,0:T(8,128)(2,1)S(1)}, u32[]{:S(2)}, u32[]{:S(2)}) collective-permute-start(bf16[32,1024]{1,0:T(8,128)(2,1)} %get-tuple-element.299), channel_id=1, source_target_pairs={{32,0},{64,32},{96,64},{128,96},{160,128},{192,160},{224,192},{256... | collective-permute-start | bytes 196616 | tf_op jit(solution)/shard_map/while/body/eval_jaxpr/ppermute | solution.py:14
  374.6 10.2 %collective-permute-start = (bf16[32,1024]{1,0:T(8,128)(2,1)}, bf16[32,1024]{1,0:T(8,128)(2,1)S(1)}, u32[]{:S(2)}, u32[]{:S(2)}) collective-permute-start(bf16[32,1024]{1,0:T(8,128)(2,1)} %get-tuple-element.299), channel_id=1, source_target_pairs={{32,0},{64,32},{96,64},{128,96},{160,128},{192,160},{224,192},{256... | collective-permute-start | bytes 196616 | tf_op jit(solution)/shard_map/while/body/eval_jaxpr/ppermute | solution.py:14
  392.1 10.0 %collective-permute-start = (bf16[32,1024]{1,0:T(8,128)(2,1)}, bf16[32,1024]{1,0:T(8,128)(2,1)S(1)}, u32[]{:S(2)}, u32[]{:S(2)}) collective-permute-start(bf16[32,1024]{1,0:T(8,128)(2,1)} %get-tuple-element.299), channel_id=1, source_target_pairs={{32,0},{64,32},{96,64},{128,96},{160,128},{192,160},{224,192},{256... | collective-permute-start | bytes 196616 | tf_op jit(solution)/shard_map/while/body/eval_jaxpr/ppermute | solution.py:14
  409.6 10.0 %collective-permute-start = (bf16[32,1024]{1,0:T(8,128)(2,1)}, bf16[32,1024]{1,0:T(8,128)(2,1)S(1)}, u32[]{:S(2)}, u32[]{:S(2)}) collective-permute-start(bf16[32,1024]{1,0:T(8,128)(2,1)} %get-tuple-element.299), channel_id=1, source_target_pairs={{32,0},{64,32},{96,64},{128,96},{160,128},{192,160},{224,192},{256... | collective-permute-start | bytes 196616 | tf_op jit(solution)/shard_map/while/body/eval_jaxpr/ppermute | solution.py:14
  427.0 10.0 %collective-permute-start = (bf16[32,1024]{1,0:T(8,128)(2,1)}, bf16[32,1024]{1,0:T(8,128)(2,1)S(1)}, u32[]{:S(2)}, u32[]{:S(2)}) collective-permute-start(bf16[32,1024]{1,0:T(8,128)(2,1)} %get-tuple-element.299), channel_id=1, source_target_pairs={{32,0},{64,32},{96,64},{128,96},{160,128},{192,160},{224,192},{256... | collective-permute-start | bytes 196616 | tf_op jit(solution)/shard_map/while/body/eval_jaxpr/ppermute | solution.py:14
  444.4 10.0 %collective-permute-start = (bf16[32,1024]{1,0:T(8,128)(2,1)}, bf16[32,1024]{1,0:T(8,128)(2,1)S(1)}, u32[]{:S(2)}, u32[]{:S(2)}) collective-permute-start(bf16[32,1024]{1,0:T(8,128)(2,1)} %get-tuple-element.299), channel_id=1, source_target_pairs={{32,0},{64,32},{96,64},{128,96},{160,128},{192,160},{224,192},{256... | collective-permute-start | bytes 196616 | tf_op jit(solution)/shard_map/while/body/eval_jaxpr/ppermute | solution.py:14
  461.8 10.0 %collective-permute-start = (bf16[32,1024]{1,0:T(8,128)(2,1)}, bf16[32,1024]{1,0:T(8,128)(2,1)S(1)}, u32[]{:S(2)}, u32[]{:S(2)}) collective-permute-start(bf16[32,1024]{1,0:T(8,128)(2,1)} %get-tuple-element.299), channel_id=1, source_target_pairs={{32,0},{64,32},{96,64},{128,96},{160,128},{192,160},{224,192},{256... | collective-permute-start | bytes 196616 | tf_op jit(solution)/shard_map/while/body/eval_jaxpr/ppermute | solution.py:14
  491.0 135.6 %copy-start.3 = (f32[1,4,1024]{2,1,0:T(4,128)}, f32[1,4,1024]{2,1,0:T(4,128)S(1)}, u32[]{:S(2)}) copy-start(f32[1,4,1024]{2,1,0:T(4,128)S(1)} %broadcast_in_dim_reshape.3) | copy-start | bytes 49156
Sparse Core Ops, SparseCore 0:
  10.1 101.5 all-gather.3
where the time goes:
time: 638 us; the launch traced here: 633 us
  blocking collectives  251 us (39%)
  waiting for transfers between devices  249 us (39%)
  starting transfers between devices  40.4 us (6%)
  matrix products  29.3 us (5%)
  between operations  28.8 us (5%)
  other arithmetic  18.2 us (3%)
  local copies, waits for them, and re-layouts  15.9 us (2%)
    ppermute x19, waiting for transfers between devices, from_behind(): return lax.ppermute(block, axis, route)  162 us
    all_gather x19, blocking collectives, advance(): grad_full = lax.all_gather(grad_piece, 'mp', axis=1, tiled=True)  110 us
    psum x1, blocking collectives, body(): summed = lax.psum(score_table * score_scale, ('section', 'dp', 'mp'))  106 us
    all_gather x1, waiting for transfers between devices, body(): w_rows = lax.all_gather(weights[0], 'dp', axis=1, tiled=True)  86.4 us
    ppermute x19, starting transfers between devices, from_behind(): return lax.ppermute(block, axis, route)  40.4 us
    dot_general x4, matrix products, through(): lax.dot_general(grad_full, w_rows, (((1,), (1,)), ((), ())), preferred_el...  26.4 us
    all_gather x1, blocking collectives, body(): lax.all_gather(panels_here, 'dp', axis=0, tiled=True)  24.6 us
    dynamic_update_slice x19, other arithmetic, advance(): lax.dynamic_update_slice_in_dim(stored, jnp.where(active, grad_piece, pre...  18.2 us
  transfers between devices with their start and end apart: 20, of which 20 were waited for; matrix products, arithmetic and copies ran while one was open for 0% of the time, Pallas kernels for 0%

commit v1 on v0

v1 whole, which is shorter than its diff:
```python
import math

import jax
import jax.numpy as jnp
from jax import lax
from jax.sharding import PartitionSpec as P

LEN = 32
CHUNKS = 4


def silu_slope(pre_state):
    sigma = jax.nn.sigmoid(pre_state)
    return sigma * (1.0 + pre_state * (1.0 - sigma))


def to_every_width_piece_below(block, section_count, model_count, shift):
    route = [
        (s * model_count + m, (s - 1) * model_count + (m + shift) % model_count)
        for s in range(1, section_count)
        for m in range(model_count)
    ]
    return lax.ppermute(block, ("section", "mp"), route)


def body(cotangent, saved_inputs, pre_acts, weights, proj_in, proj_out, query_panels, partners):
    section_count = lax.axis_size("section")
    model_count = lax.axis_size("mp")
    data_count = lax.axis_size("dp")
    section_index = lax.axis_index("section")
    model_index = lax.axis_index("mp")
    data_index = lax.axis_index("dp")
    tokens = saved_inputs.shape[1]
    piece = saved_inputs.shape[2]
    width = piece * model_count
    length = LEN
    examples = tokens // length
    low_rank = proj_in.shape[2]
    chunk = tokens // CHUNKS
    chunk_examples = chunk // length
    top_section = section_count - 1
    piece_rank = low_rank // model_count

    w_rows = lax.all_gather(weights[0], "dp", axis=1, tiled=True)
    pre_full = lax.all_gather(pre_acts[0], "mp", axis=1, tiled=True)
    top_full = lax.all_gather(cotangent, "mp", axis=1, tiled=True)
    inputs_full = lax.all_gather(saved_inputs[0], "mp", axis=1, tiled=True)
    in_proj = lax.all_gather(proj_in[0], "mp", axis=0, tiled=True)
    out_proj = lax.all_gather(proj_out[0], "mp", axis=0, tiled=True)
    queries = lax.all_gather(query_panels[0], "dp", axis=0, tiled=True)
    slopes = silu_slope(pre_full.astype(jnp.float32))
    in_side = jnp.dot(inputs_full, in_proj, preferred_element_type=jnp.float32)
    in_rows = lax.dynamic_slice_in_dim(in_side, model_index * piece_rank, piece_rank, 1)

    panel_store = jnp.zeros((CHUNKS, chunk_examples, piece_rank * low_rank), jnp.float32)
    score_store = jnp.zeros((CHUNKS, queries.shape[0], chunk_examples), jnp.float32)
    outgoing = jnp.zeros((chunk, piece), jnp.bfloat16)
    is_top = section_index == top_section
    step_count = CHUNKS + section_count - 1
    for turn in range(step_count):
        if turn > 0:
            received = [
                to_every_width_piece_below(outgoing, section_count, model_count, shift)
                for shift in range(model_count)
            ]
            stacked = jnp.stack(received)
            order = (model_index - jnp.arange(model_count)) % model_count
            below_full = jnp.take(stacked, order, axis=0).transpose(1, 0, 2).reshape(chunk, width)
            below_mine = received[0]
        else:
            below_full = jnp.zeros((chunk, width), jnp.bfloat16)
            below_mine = jnp.zeros((chunk, piece), jnp.bfloat16)
        chunk_at = turn - (top_section - section_index)
        active = jnp.logical_and(chunk_at >= 0, chunk_at < CHUNKS)
        clipped = jnp.clip(chunk_at, 0, CHUNKS - 1)
        row_start = clipped * chunk
        top_rows = lax.dynamic_slice_in_dim(top_full, row_start, chunk, 0)
        delta_full = jnp.where(is_top, top_rows, below_full)
        top_mine = lax.dynamic_slice_in_dim(cotangent, row_start, chunk, 0)
        delta_mine = jnp.where(is_top, top_mine, below_mine)
        slope_rows = lax.dynamic_slice_in_dim(slopes, row_start, chunk, 0)
        grad = (delta_full.astype(jnp.float32) * slope_rows).astype(jnp.bfloat16)
        if turn < step_count - 1:
            back_term = lax.dot_general(
                grad, w_rows, (((1,), (1,)), ((), ())), preferred_element_type=jnp.float32
            )
            outgoing = (delta_mine.astype(jnp.float32) + back_term).astype(jnp.bfloat16)

        out_side = jnp.dot(grad, out_proj, preferred_element_type=jnp.float32)
        in_chunk = lax.dynamic_slice_in_dim(in_rows, row_start, chunk, 0)
        panels = jnp.einsum(
            "etr,etc->erc",
            in_chunk.reshape(chunk_examples, length, piece_rank),
            out_side.reshape(chunk_examples, length, low_rank),
            precision=lax.Precision.HIGHEST,
        ) / math.sqrt(length)
        panels = panels.reshape(chunk_examples, piece_rank * low_rank)
        partial = jnp.dot(queries, panels.T, precision=lax.Precision.HIGHEST)
        old_panels = lax.dynamic_index_in_dim(panel_store, clipped, 0, keepdims=False)
        panel_store = lax.dynamic_update_index_in_dim(
            panel_store, jnp.where(active, panels, old_panels), clipped, 0
        )
        old_scores = lax.dynamic_index_in_dim(score_store, clipped, 0, keepdims=False)
        score_store = lax.dynamic_update_index_in_dim(
            score_store, jnp.where(active, partial, old_scores), clipped, 0
        )

    panels_here = panel_store.reshape(examples, piece_rank * low_rank)
    asked = queries.shape[0]
    mine = score_store.transpose(1, 0, 2).reshape(asked, examples)
    table = jnp.zeros((asked, data_count * examples), jnp.float32)
    table = lax.dynamic_update_slice(table, mine, (jnp.int32(0), data_index * examples))
    score_scale = 1.0 / (low_rank * math.sqrt(section_count))
    summed = lax.psum(table * score_scale, ("section", "dp", "mp"))
    rounds = partners.shape[0]
    per_dp = asked // data_count
    owner = jnp.arange(asked) // per_dp
    chosen = partners[:, owner].T
    columns = chosen[:, :, None] * examples + jnp.arange(examples)[None, None, :]
    scores = jnp.take_along_axis(summed, columns.reshape(asked, rounds * examples), axis=1)
    scores = scores.reshape(asked, rounds, examples)
    return (panels_here[None], scores)


def solution(mesh):
    placed = (
        P("dp", "mp"),
        P("section", "dp", "mp"),
        P("section", "dp", "mp"),
        P("section", "mp", "dp"),
        P("section", "mp", None),
        P("section", "mp", None),
        P("section", "dp", "mp"),
        P(),
    )
    return jax.shard_map(
        body, mesh=mesh, in_specs=placed, out_specs=(P("section", "dp", "mp"), P()), check_vma=False
    )
```

time: 638 us -> 778 us (1.22); the launches traced: 633 us -> 764 us
  blocking collectives: 251 us -> 141 us
  starting transfers between devices: 40.4 us -> 144 us
  matrix products: 29.3 us -> 124 us
  waiting for transfers between devices: 249 us -> 270 us
  other arithmetic: 18.2 us -> 36.6 us
  local copies, waits for them, and re-layouts: 15.9 us -> 33.8 us
  between operations: 28.8 us -> 15.8 us
    ppermute x19 -> x72, starting transfers between devices: 40.4 us -> 143 us  [to_every_width_piece_below(): return lax.ppermute(block, ('section', 'mp'), route)]
    dot_general x15 -> x76, matrix products: 29.3 us -> 124 us  [the longest x18 108 us: body(): lax.dot_general(grad, w_rows, (((1,), (1,)), ((), ())), preferred_element...]
    all_gather x20 -> x3, blocking collectives: 135 us -> 45.8 us  [the longest x1 30.9 us: body(): queries = lax.all_gather(query_panels[0], 'dp', axis=0, tiled=True)]
    all_gather x0 -> x3, waiting for transfers between devices: none -> 36.8 us  [the longest x1 27.9 us: body(): inputs_full = lax.all_gather(saved_inputs[0], 'mp', axis=1, tiled=True)]
    ppermute x19 -> x72, waiting for transfers between devices: 162 us -> 132 us  [to_every_width_piece_below(): return lax.ppermute(block, ('section', 'mp'), route)]
    psum x2 -> x1, blocking collectives: 117 us -> 95.1 us  [body(): summed = lax.psum(table * score_scale, ('section', 'dp', 'mp'))]
    dynamic_update_slice x19 -> x17, other arithmetic: 18.2 us -> 0.28 us  [body(): lax.dynamic_update_index_in_dim(panel_store, jnp.where(active, panels, ol...]
    convert_element_type x0 -> x17, other arithmetic: none -> 17.8 us  [body(): grad = (delta_full.astype(jnp.float32) * slope_rows).astype(jnp.bfloat16)]
  transfers between devices with their start and end apart: 20 -> 76, of which waited for: 20 -> 74; matrix products, arithmetic and copies ran while one was open for 0% -> 2% of each run, Pallas kernels for 0% -> 0%
where the time goes in v1:
time: 778 us; the launch traced here: 764 us
  waiting for transfers between devices  270 us (35%)
  starting transfers between devices  144 us (19%)
  blocking collectives  141 us (18%)
  matrix products  124 us (16%)
  other arithmetic  36.6 us (5%)
  local copies, waits for them, and re-layouts  33.8 us (4%)
  between operations  15.8 us (2%)
    ppermute x72, starting transfers between devices, to_every_width_piece_below(): return lax.ppermute(block, ('section', 'mp'), route)  143 us
    ppermute x72, waiting for transfers between devices, to_every_width_piece_below(): return lax.ppermute(block, ('section', 'mp'), route)  132 us
    dot_general x18, matrix products, body(): lax.dot_general(grad, w_rows, (((1,), (1,)), ((), ())), preferred_element...  108 us
    all_gather x1, waiting for transfers between devices, body(): w_rows = lax.all_gather(weights[0], 'dp', axis=1, tiled=True)  98.2 us
    psum x1, blocking collectives, body(): summed = lax.psum(table * score_scale, ('section', 'dp', 'mp'))  95.1 us
    all_gather x1, blocking collectives, body(): queries = lax.all_gather(query_panels[0], 'dp', axis=0, tiled=True)  30.9 us
    all_gather x1, waiting for transfers between devices, body(): inputs_full = lax.all_gather(saved_inputs[0], 'mp', axis=1, tiled=True)  27.9 us
    convert_element_type x17, other arithmetic, body(): grad = (delta_full.astype(jnp.float32) * slope_rows).astype(jnp.bfloat16)  17.8 us
  transfers between devices with their start and end apart: 76, of which 74 were waited for; matrix products, arithmetic and copies ran while one was open for 2% of the time, Pallas kernels for 0%

profile of v1, /device:TPU:56, one launch (start us, length us, event | category | flops | bytes accessed | tf_op | source)
XLA Modules:
  0.0 764.2 jit_solution(4156540557819097658)
XLA Ops:
  12.7 30.9 %all-gather.5 = f32[1,16,1024]{2,0,1:T(1,128)S(1)} all-gather(f32[1,2,1024]{2,0,1:T(1,128)S(1)} %copy.134), channel_id=7, replica_groups=mesh['section'=16,'dp'=8,'mp'=4] {'dp'}, dimensions={1}, use_global_device_ids=true | all-gather | bytes 73728 | tf_op jit(solution)/shard_map/all_gather | solution.py:50
  43.7 7.4 all-gather.3
  51.1 7.5 all-gather.1
  60.5 8.8 %all-gather.11.cloned.1.call-done = bf16[128,4096]{1,0:T(8,128)(2,1)} async-done(((bf16[128,1024]{1,0:T(8,128)(2,1)}), bf16[128,4096]{1,0:T(8,128)(2,1)}) %all-gather.11.cloned.1.call-update) | async-done | bytes 1048592 | tf_op jit(solution)/shard_map/all_gather | solution.py:46
  70.6 27.9 %all-gather.13.cloned.1.call-done = bf16[1,128,4096]{2,1,0:T(8,128)(2,1)} async-done(((bf16[1,128,1024]{2,1,0:T(8,128)(2,1)}), bf16[1,128,4096]{2,1,0:T(8,128)(2,1)}) %all-gather.13.cloned.1.call-update) | async-done | bytes 1048592 | tf_op jit(solution)/shard_map/all_gather | solution.py:47
  100.9 98.2 %all-gather.17.cloned.1.call-done = bf16[1,1024,4096]{2,1,0:T(8,128)(2,1)} async-done(((bf16[1,1024,512]{2,1,0:T(8,128)(2,1)}), bf16[1,1024,4096]{2,1,0:T(8,128)(2,1)}) %all-gather.17.cloned.1.call-update) | async-done | bytes 8388624 | tf_op jit(solution)/shard_map/all_gather | solution.py:44
  199.1 6.1 fusion.44
  228.7 6.0 add_convert_fusion.16
  253.9 6.0 add_convert_fusion.15
  279.1 6.0 add_convert_fusion.14
  304.4 6.0 add_convert_fusion.13
  329.6 6.0 add_convert_fusion.12
  354.8 6.0 add_convert_fusion.11
  380.1 6.0 add_convert_fusion.10
  405.3 6.0 add_convert_fusion.9
  430.6 6.0 add_convert_fusion.8
  455.8 6.0 add_convert_fusion.7
  481.0 6.0 add_convert_fusion.6
  506.3 6.0 add_convert_fusion.5
  531.5 6.0 add_convert_fusion.4
  556.7 6.0 add_convert_fusion.3
  582.0 6.0 add_convert_fusion.2
  607.2 6.0 add_convert_fusion.1
  656.8 95.1 %psum.7 = f32[16,32]{0,1:T(8,128)S(1)} all-reduce(f32[16,32]{0,1:T(8,128)S(1)} %broadcast_multiply_fusion), channel_id=1, replica_groups=mesh['section'=16,'dp'=8,'mp'=4] {'section','dp','mp'}, use_global_device_ids=true, to_apply=%region_0.2 | all-reduce | flops 512 | bytes 4096 | tf_op jit(solution)/shard_map/psum | solution.py:114
  (507 shorter events, 370.3 us)
Async XLA Ops:
  7.2 51.4 %all-gather.15.cloned.1.call-start = ((), (), s32[]{:S(2)}) async-start(), calls=%async_computation.2 | async-start | bytes 1310720 | tf_op jit(solution)/shard_map/all_gather | solution.py:45
  7.9 61.5 %all-gather.11.cloned.1.call-start = ((), (), s32[]{:S(2)}) async-start(), calls=%async_computation | async-start | bytes 1310720 | tf_op jit(solution)/shard_map/all_gather | solution.py:46
  8.7 89.9 %all-gather.13.cloned.1.call-start = ((), (), s32[]{:S(2)}) async-start(), calls=%async_computation.1 | async-start | bytes 1310720 | tf_op jit(solution)/shard_map/all_gather | solution.py:47
  9.4 189.7 %all-gather.17.cloned.1.call-start = ((), (), s32[]{:S(2)}) async-start(), calls=%async_computation.3 | async-start | bytes 9437184 | tf_op jit(solution)/shard_map/all_gather | solution.py:44
  205.2 12.9 %collective-permute-start.3 = (bf16[32,1024]{1,0:T(8,128)(2,1)S(1)}, bf16[32,1024]{1,0:T(8,128)(2,1)S(1)}, u32[]{:S(2)}, u32[]{:S(2)}) collective-permute-start(bf16[32,1024]{1,0:T(8,128)(2,1)S(1)} %fusion.44), channel_id=1, source_target_pairs={{32,3},{33,0},{34,1},{35,2},{64,35},{65,32},{66,33},{67,34},{96,67... | collective-permute-start | bytes 196616 | tf_op jit(solution)/shard_map/ppermute | solution.py:23
  215.6 10.4 %collective-permute-start = (bf16[32,1024]{1,0:T(8,128)(2,1)S(1)}, bf16[32,1024]{1,0:T(8,128)(2,1)S(1)}, u32[]{:S(2)}, u32[]{:S(2)}) collective-permute-start(bf16[32,1024]{1,0:T(8,128)(2,1)S(1)} %fusion.44), channel_id=1, source_target_pairs={{32,0},{33,1},{34,2},{35,3},{64,32},{65,33},{66,34},{67,35},{96,64... | collective-permute-start | bytes 196616 | tf_op jit(solution)/shard_map/ppermute | solution.py:23
  240.5 9.9 %collective-permute-start.4 = (bf16[32,1024]{1,0:T(8,128)(2,1)S(1)}, bf16[32,1024]{1,0:T(8,128)(2,1)S(1)}, u32[]{:S(2)}, u32[]{:S(2)}) collective-permute-start(bf16[32,1024]{1,0:T(8,128)(2,1)S(1)} %add_convert_fusion.16), channel_id=1, source_target_pairs={{32,0},{33,1},{34,2},{35,3},{64,32},{65,33},{66,34},{67,35},{96,64... | collective-permute-start | bytes 196616 | tf_op jit(solution)/shard_map/ppermute | solution.py:23
  265.7 9.9 %collective-permute-start.8 = (bf16[32,1024]{1,0:T(8,128)(2,1)S(1)}, bf16[32,1024]{1,0:T(8,128)(2,1)S(1)}, u32[]{:S(2)}, u32[]{:S(2)}) collective-permute-start(bf16[32,1024]{1,0:T(8,128)(2,1)S(1)} %add_convert_fusion.15), channel_id=1, source_target_pairs={{32,0},{33,1},{34,2},{35,3},{64,32},{65,33},{66,34},{67,35},{96,64... | collective-permute-start | bytes 196616 | tf_op jit(solution)/shard_map/ppermute | solution.py:23
  290.9 9.9 %collective-permute-start.12 = (bf16[32,1024]{1,0:T(8,128)(2,1)S(1)}, bf16[32,1024]{1,0:T(8,128)(2,1)S(1)}, u32[]{:S(2)}, u32[]{:S(2)}) collective-permute-start(bf16[32,1024]{1,0:T(8,128)(2,1)S(1)} %add_convert_fusion.14), channel_id=1, source_target_pairs={{32,0},{33,1},{34,2},{35,3},{64,32},{65,33},{66,34},{67,35},{96,64... | collective-permute-start | bytes 196616 | tf_op jit(solution)/shard_map/ppermute | solution.py:23
  316.2 9.9 %collective-permute-start.16 = (bf16[32,1024]{1,0:T(8,128)(2,1)S(1)}, bf16[32,1024]{1,0:T(8,128)(2,1)S(1)}, u32[]{:S(2)}, u32[]{:S(2)}) collective-permute-start(bf16[32,1024]{1,0:T(8,128)(2,1)S(1)} %add_convert_fusion.13), channel_id=1, source_target_pairs={{32,0},{33,1},{34,2},{35,3},{64,32},{65,33},{66,34},{67,35},{96,64... | collective-permute-start | bytes 196616 | tf_op jit(solution)/shard_map/ppermute | solution.py:23
  341.4 9.9 %collective-permute-start.20 = (bf16[32,1024]{1,0:T(8,128)(2,1)S(1)}, bf16[32,1024]{1,0:T(8,128)(2,1)S(1)}, u32[]{:S(2)}, u32[]{:S(2)}) collective-permute-start(bf16[32,1024]{1,0:T(8,128)(2,1)S(1)} %add_convert_fusion.12), channel_id=1, source_target_pairs={{32,0},{33,1},{34,2},{35,3},{64,32},{65,33},{66,34},{67,35},{96,64... | collective-permute-start | bytes 196616 | tf_op jit(solution)/shard_map/ppermute | solution.py:23
  366.6 9.9 %collective-permute-start.24 = (bf16[32,1024]{1,0:T(8,128)(2,1)S(1)}, bf16[32,1024]{1,0:T(8,128)(2,1)S(1)}, u32[]{:S(2)}, u32[]{:S(2)}) collective-permute-start(bf16[32,1024]{1,0:T(8,128)(2,1)S(1)} %add_convert_fusion.11), channel_id=1, source_target_pairs={{32,0},{33,1},{34,2},{35,3},{64,32},{65,33},{66,34},{67,35},{96,64... | collective-permute-start | bytes 196616 | tf_op jit(solution)/shard_map/ppermute | solution.py:23
  391.9 9.9 %collective-permute-start.28 = (bf16[32,1024]{1,0:T(8,128)(2,1)S(1)}, bf16[32,1024]{1,0:T(8,128)(2,1)S(1)}, u32[]{:S(2)}, u32[]{:S(2)}) collective-permute-start(bf16[32,1024]{1,0:T(8,128)(2,1)S(1)} %add_convert_fusion.10), channel_id=1, source_target_pairs={{32,0},{33,1},{34,2},{35,3},{64,32},{65,33},{66,34},{67,35},{96,64... | collective-permute-start | bytes 196616 | tf_op jit(solution)/shard_map/ppermute | solution.py:23
  417.1 9.9 %collective-permute-start.32 = (bf16[32,1024]{1,0:T(8,128)(2,1)S(1)}, bf16[32,1024]{1,0:T(8,128)(2,1)S(1)}, u32[]{:S(2)}, u32[]{:S(2)}) collective-permute-start(bf16[32,1024]{1,0:T(8,128)(2,1)S(1)} %add_convert_fusion.9), channel_id=1, source_target_pairs={{32,0},{33,1},{34,2},{35,3},{64,32},{65,33},{66,34},{67,35},{96,64... | collective-permute-start | bytes 196616 | tf_op jit(solution)/shard_map/ppermute | solution.py:23
  442.4 9.9 %collective-permute-start.36 = (bf16[32,1024]{1,0:T(8,128)(2,1)S(1)}, bf16[32,1024]{1,0:T(8,128)(2,1)S(1)}, u32[]{:S(2)}, u32[]{:S(2)}) collective-permute-start(bf16[32,1024]{1,0:T(8,128)(2,1)S(1)} %add_convert_fusion.8), channel_id=1, source_target_pairs={{32,0},{33,1},{34,2},{35,3},{64,32},{65,33},{66,34},{67,35},{96,64... | collective-permute-start | bytes 196616 | tf_op jit(solution)/shard_map/ppermute | solution.py:23
  467.6 9.9 %collective-permute-start.40 = (bf16[32,1024]{1,0:T(8,128)(2,1)S(1)}, bf16[32,1024]{1,0:T(8,128)(2,1)S(1)}, u32[]{:S(2)}, u32[]{:S(2)}) collective-permute-start(bf16[32,1024]{1,0:T(8,128)(2,1)S(1)} %add_convert_fusion.7), channel_id=1, source_target_pairs={{32,0},{33,1},{34,2},{35,3},{64,32},{65,33},{66,34},{67,35},{96,64... | collective-permute-start | bytes 196616 | tf_op jit(solution)/shard_map/ppermute | solution.py:23
  492.8 9.9 %collective-permute-start.44 = (bf16[32,1024]{1,0:T(8,128)(2,1)S(1)}, bf16[32,1024]{1,0:T(8,128)(2,1)S(1)}, u32[]{:S(2)}, u32[]{:S(2)}) collective-permute-start(bf16[32,1024]{1,0:T(8,128)(2,1)S(1)} %add_convert_fusion.6), channel_id=1, source_target_pairs={{32,0},{33,1},{34,2},{35,3},{64,32},{65,33},{66,34},{67,35},{96,64... | collective-permute-start | bytes 196616 | tf_op jit(solution)/shard_map/ppermute | solution.py:23
  518.1 9.9 %collective-permute-start.48 = (bf16[32,1024]{1,0:T(8,128)(2,1)S(1)}, bf16[32,1024]{1,0:T(8,128)(2,1)S(1)}, u32[]{:S(2)}, u32[]{:S(2)}) collective-permute-start(bf16[32,1024]{1,0:T(8,128)(2,1)S(1)} %add_convert_fusion.5), channel_id=1, source_target_pairs={{32,0},{33,1},{34,2},{35,3},{64,32},{65,33},{66,34},{67,35},{96,64... | collective-permute-start | bytes 196616 | tf_op jit(solution)/shard_map/ppermute | solution.py:23
  543.3 9.9 %collective-permute-start.52 = (bf16[32,1024]{1,0:T(8,128)(2,1)S(1)}, bf16[32,1024]{1,0:T(8,128)(2,1)S(1)}, u32[]{:S(2)}, u32[]{:S(2)}) collective-permute-start(bf16[32,1024]{1,0:T(8,128)(2,1)S(1)} %add_convert_fusion.4), channel_id=1, source_target_pairs={{32,0},{33,1},{34,2},{35,3},{64,32},{65,33},{66,34},{67,35},{96,64... | collective-permute-start | bytes 196616 | tf_op jit(solution)/shard_map/ppermute | solution.py:23
  568.5 9.9 %collective-permute-start.56 = (bf16[32,1024]{1,0:T(8,128)(2,1)S(1)}, bf16[32,1024]{1,0:T(8,128)(2,1)S(1)}, u32[]{:S(2)}, u32[]{:S(2)}) collective-permute-start(bf16[32,1024]{1,0:T(8,128)(2,1)S(1)} %add_convert_fusion.3), channel_id=1, source_target_pairs={{32,0},{33,1},{34,2},{35,3},{64,32},{65,33},{66,34},{67,35},{96,64... | collective-permute-start | bytes 196616 | tf_op jit(solution)/shard_map/ppermute | solution.py:23
  593.8 9.9 %collective-permute-start.60 = (bf16[32,1024]{1,0:T(8,128)(2,1)S(1)}, bf16[32,1024]{1,0:T(8,128)(2,1)S(1)}, u32[]{:S(2)}, u32[]{:S(2)}) collective-permute-start(bf16[32,1024]{1,0:T(8,128)(2,1)S(1)} %add_convert_fusion.2), channel_id=1, source_target_pairs={{32,0},{33,1},{34,2},{35,3},{64,32},{65,33},{66,34},{67,35},{96,64... | collective-permute-start | bytes 196616 | tf_op jit(solution)/shard_map/ppermute | solution.py:23
  619.0 9.9 %collective-permute-start.64 = (bf16[32,1024]{1,0:T(8,128)(2,1)S(1)}, bf16[32,1024]{1,0:T(8,128)(2,1)S(1)}, u32[]{:S(2)}, u32[]{:S(2)}) collective-permute-start(bf16[32,1024]{1,0:T(8,128)(2,1)S(1)} %add_convert_fusion.1), channel_id=1, source_target_pairs={{32,0},{33,1},{34,2},{35,3},{64,32},{65,33},{66,34},{67,35},{96,64... | collective-permute-start | bytes 196616 | tf_op jit(solution)/shard_map/ppermute | solution.py:23
  640.4 9.6 %collective-permute-start.70 = (bf16[32,1024]{1,0:T(8,128)(2,1)S(1)}, bf16[32,1024]{1,0:T(8,128)(2,1)S(1)}, u32[]{:S(2)}, u32[]{:S(2)}) collective-permute-start(bf16[32,1024]{1,0:T(8,128)(2,1)S(1)} %add_convert_fusion), channel_id=1, source_target_pairs={{32,2},{33,3},{34,0},{35,1},{64,34},{65,35},{66,32},{67,33},{96,66... | collective-permute-start | bytes 196616 | tf_op jit(solution)/shard_map/ppermute | solution.py:23
  644.2 9.9 %collective-permute-start.68 = (bf16[32,1024]{1,0:T(8,128)(2,1)S(1)}, bf16[32,1024]{1,0:T(8,128)(2,1)S(1)}, u32[]{:S(2)}, u32[]{:S(2)}) collective-permute-start(bf16[32,1024]{1,0:T(8,128)(2,1)S(1)} %add_convert_fusion), channel_id=1, source_target_pairs={{32,0},{33,1},{34,2},{35,3},{64,32},{65,33},{66,34},{67,35},{96,64... | collective-permute-start | bytes 196616 | tf_op jit(solution)/shard_map/ppermute | solution.py:23
  (103 other events, 802.7 us)
Sparse Core Ops, SparseCore 0:
  10.1 30.0 all-gather.14
  42.3 27.0 all-gather.10
  71.5 27.0 all-gather.12
  100.5 98.5 all-gather.16

commit v2 on v1

v2 whole, which is shorter than its diff:
```python
import math

import jax
import jax.numpy as jnp
from jax import lax
from jax.sharding import PartitionSpec as P

LEN = 32
CHUNKS = 2


def from_behind(block, axis, distance):
    devices = range(lax.axis_size(axis))
    route = [(i - distance, i) for i in devices if i - distance in devices]
    return lax.ppermute(block, axis, route)


def silu_slope(pre_state):
    sigma = jax.nn.sigmoid(pre_state)
    return sigma * (1.0 + pre_state * (1.0 - sigma))


def body(cotangent, saved_inputs, pre_acts, weights, proj_in, proj_out, query_panels, partners):
    section_count = lax.axis_size("section")
    model_count = lax.axis_size("mp")
    data_count = lax.axis_size("dp")
    section_index = lax.axis_index("section")
    model_index = lax.axis_index("mp")
    data_index = lax.axis_index("dp")
    tokens = saved_inputs.shape[1]
    piece = saved_inputs.shape[2]
    length = LEN
    examples = tokens // length
    low_rank = proj_in.shape[2]
    chunk = tokens // CHUNKS
    chunk_examples = chunk // length
    top_section = section_count - 1
    piece_rank = low_rank // model_count

    w_rows = lax.all_gather(weights[0], "dp", axis=1, tiled=True)
    slopes = silu_slope(pre_acts[0].astype(jnp.float32))
    out_proj = lax.all_gather(proj_out[0], "mp", axis=0, tiled=True)
    in_part = jnp.dot(saved_inputs[0], proj_in[0], preferred_element_type=jnp.float32)
    in_side = lax.psum(in_part, "mp")
    in_rows = lax.dynamic_slice_in_dim(in_side, model_index * piece_rank, piece_rank, 1)
    queries = query_panels[0]
    asked = queries.shape[0] * data_count
    queries = lax.all_gather(queries, "dp", axis=0, tiled=True)

    panel_store = jnp.zeros((CHUNKS, chunk_examples, piece_rank * low_rank), jnp.float32)
    score_store = jnp.zeros((CHUNKS, asked, chunk_examples), jnp.float32)
    outgoing = jnp.zeros((chunk, piece), jnp.bfloat16)
    is_top = section_index == top_section
    step_count = CHUNKS + section_count - 1
    for turn in range(step_count):
        chunk_at = turn - (top_section - section_index)
        active = jnp.logical_and(chunk_at >= 0, chunk_at < CHUNKS)
        clipped = jnp.clip(chunk_at, 0, CHUNKS - 1)
        row_start = clipped * chunk
        top_rows = lax.dynamic_slice_in_dim(cotangent, row_start, chunk, 0)
        if turn > 0:
            received = from_behind(outgoing, "section", -1)
            delta_piece = jnp.where(is_top, top_rows, received)
        else:
            delta_piece = top_rows
        slope_rows = lax.dynamic_slice_in_dim(slopes, row_start, chunk, 0)
        grad_piece = (delta_piece.astype(jnp.float32) * slope_rows).astype(jnp.bfloat16)
        grad_full = lax.all_gather(grad_piece, "mp", axis=1, tiled=True)
        if turn < step_count - 1:
            back_term = lax.dot_general(
                grad_full, w_rows, (((1,), (1,)), ((), ())), preferred_element_type=jnp.float32
            )
            outgoing = (delta_piece.astype(jnp.float32) + back_term).astype(jnp.bfloat16)

        out_side = jnp.dot(grad_full, out_proj, preferred_element_type=jnp.float32)
        in_chunk = lax.dynamic_slice_in_dim(in_rows, row_start, chunk, 0)
        panels = jnp.einsum(
            "etr,etc->erc",
            in_chunk.reshape(chunk_examples, length, piece_rank),
            out_side.reshape(chunk_examples, length, low_rank),
            precision=lax.Precision.HIGHEST,
        ) / math.sqrt(length)
        panels = panels.reshape(chunk_examples, piece_rank * low_rank)
        partial = jnp.dot(queries, panels.T, precision=lax.Precision.HIGHEST)
        old_panels = lax.dynamic_index_in_dim(panel_store, clipped, 0, keepdims=False)
        panel_store = lax.dynamic_update_index_in_dim(
            panel_store, jnp.where(active, panels, old_panels), clipped, 0
        )
        old_scores = lax.dynamic_index_in_dim(score_store, clipped, 0, keepdims=False)
        score_store = lax.dynamic_update_index_in_dim(
            score_store, jnp.where(active, partial, old_scores), clipped, 0
        )

    panels_here = panel_store.reshape(examples, piece_rank * low_rank)
    mine = score_store.transpose(1, 0, 2).reshape(asked, examples)
    table = jnp.zeros((asked, data_count * examples), jnp.float32)
    table = lax.dynamic_update_slice(table, mine, (jnp.int32(0), data_index * examples))
    score_scale = 1.0 / (low_rank * math.sqrt(section_count))
    summed = lax.psum(table * score_scale, "mp")
    summed = lax.psum(summed, "dp")
    summed = lax.psum(summed, "section")
    rounds = partners.shape[0]
    per_dp = asked // data_count
    owner = jnp.arange(asked) // per_dp
    chosen = partners[:, owner].T
    columns = chosen[:, :, None] * examples + jnp.arange(examples)[None, None, :]
    scores = jnp.take_along_axis(summed, columns.reshape(asked, rounds * examples), axis=1)
    scores = scores.reshape(asked, rounds, examples)
    return (panels_here[None], scores)


def solution(mesh):
    placed = (
        P("dp", "mp"),
        P("section", "dp", "mp"),
        P("section", "dp", "mp"),
        P("section", "mp", "dp"),
        P("section", "mp", None),
        P("section", "mp", None),
        P("section", "dp", "mp"),
        P(),
    )
    return jax.shard_map(
        body, mesh=mesh, in_specs=placed, out_specs=(P("section", "dp", "mp"), P()), check_vma=False
    )
```

time: 778 us -> 645 us (0.83)
  blocking collectives: 141 us -> 276 us
  starting transfers between devices: 144 us -> 32.1 us
  waiting for transfers between devices: 270 us -> 184 us
  other arithmetic: 36.6 us -> 3.75 us
  local copies, waits for them, and re-layouts: 33.8 us -> 12.2 us
  matrix products: 124 us -> 109 us
    ppermute x72 -> x16, starting transfers between devices: 143 us -> 32.1 us  [from_behind(): return lax.ppermute(block, axis, route)]
    all_gather x2 -> x18, blocking collectives: 38.4 us -> 146 us  [the longest x17 115 us: body(): grad_full = lax.all_gather(grad_piece, 'mp', axis=1, tiled=True)]
    all_gather x1, waiting for transfers between devices: 98.2 us -> 41.3 us  [body(): w_rows = lax.all_gather(weights[0], 'dp', axis=1, tiled=True)]
    all_gather x3 -> x0, waiting for transfers between devices: 36.8 us -> none  [the longest x1 27.9 us: body(): inputs_full = lax.all_gather(saved_inputs[0], 'mp', axis=1, tiled=True)]
    psum x1 -> x4, blocking collectives: 95.1 us -> 122 us  [the longest x1 71.5 us: body(): summed = lax.psum(summed, 'section')]
    convert_element_type x17, other arithmetic: 17.8 us -> 1.69 us  [body(): (delta_piece.astype(jnp.float32) * slope_rows).astype(jnp.bfloat16)]
    another operation x18 -> x0, other arithmetic: 14.6 us -> none  [body(): stacked = jnp.stack(received)]
    dot_general x38 -> x34, matrix products: 117 us -> 104 us  [the longest x16 97 us: body(): lax.dot_general(grad_full, w_rows, (((1,), (1,)), ((), ())), preferred_el...]
  transfers between devices with their start and end apart: 76 -> 17, of which waited for: 74 -> 17; matrix products, arithmetic and copies ran while one was open for 2% -> 2% of each run, Pallas kernels for 0% -> 0%
where the time goes in v2:
time: 645 us; the launch traced here: 633 us
  blocking collectives  276 us (43%)
  waiting for transfers between devices  184 us (29%)
  matrix products  109 us (17%)
  starting transfers between devices  32.1 us (5%)
  between operations  15.4 us (2%)
  local copies, waits for them, and re-layouts  12.2 us (2%)
    ppermute x16, waiting for transfers between devices, from_behind(): return lax.ppermute(block, axis, route)  142 us
    all_gather x17, blocking collectives, body(): grad_full = lax.all_gather(grad_piece, 'mp', axis=1, tiled=True)  115 us
    dot_general x16, matrix products, body(): lax.dot_general(grad_full, w_rows, (((1,), (1,)), ((), ())), preferred_el...  97 us
    psum x1, blocking collectives, body(): summed = lax.psum(summed, 'section')  71.5 us
    all_gather x1, waiting for transfers between devices, body(): w_rows = lax.all_gather(weights[0], 'dp', axis=1, tiled=True)  41.3 us
    ppermute x16, starting transfers between devices, from_behind(): return lax.ppermute(block, axis, route)  32.1 us
    all_gather x1, blocking collectives, body(): queries = lax.all_gather(queries, 'dp', axis=0, tiled=True)  31 us
    psum x1, blocking collectives, body(): summed = lax.psum(summed, 'dp')  28.2 us
  transfers between devices with their start and end apart: 17, of which 17 were waited for; matrix products, arithmetic and copies ran while one was open for 2% of the time, Pallas kernels for 0%

profile of v2, /device:TPU:56, one launch (start us, length us, event | category | flops | bytes accessed | tf_op | source)
XLA Modules:
  0.0 632.7 jit_solution(15589204861607120687)
XLA Ops:
  9.3 11.4 %psum.28 = f32[128,64]{0,1:T(8,128)S(1)} all-reduce(f32[128,64]{0,1:T(8,128)S(1)} %fusion.233), channel_id=1, replica_groups=mesh['section'=16,'dp'=8,'mp'=4] {'mp'}, use_global_device_ids=true, to_apply=%region_0.0 | all-reduce | flops 8192 | bytes 65536 | tf_op jit(solution)/shard_map/psum | solution.py:44
  29.5 7.5 %all-gather = bf16[1,4096,64]{1,2,0:T(8,128)(2,1)S(1)} all-gather(bf16[1,1024,64]{1,2,0:T(8,128)(2,1)} %param.13), channel_id=2, replica_groups=mesh['section'=16,'dp'=8,'mp'=4] {'mp'}, dimensions={1}, use_global_device_ids=true | all-gather | bytes 655360 | tf_op jit(solution)/shard_map/all_gather | solution.py:42
  39.8 31.0 %all-gather.2 = f32[1,16,1024]{2,0,1:T(1,128)S(1)} all-gather(f32[1,2,1024]{2,0,1:T(1,128)S(1)} %copy.70), channel_id=4, replica_groups=mesh['section'=16,'dp'=8,'mp'=4] {'dp'}, dimensions={1}, use_global_device_ids=true | all-gather | bytes 73728 | tf_op jit(solution)/shard_map/all_gather | solution.py:48
  71.0 41.3 %all-gather.5.cloned.1.call-done = bf16[1,1024,4096]{2,1,0:T(8,128)(2,1)} async-done(((bf16[1,1024,512]{2,1,0:T(8,128)(2,1)}), bf16[1,1024,4096]{2,1,0:T(8,128)(2,1)}) %all-gather.5.cloned.1.call-update) | async-done | bytes 8388624 | tf_op jit(solution)/shard_map/all_gather | solution.py:40
  129.2 7.2 %all_gather.63 = bf16[64,4096]{1,0:T(8,128)(2,1)S(1)} all-gather(bf16[64,1024]{1,0:T(8,128)(2,1)S(1)} %fusion.218), channel_id=1, replica_groups=mesh['section'=16,'dp'=8,'mp'=4] {'mp'}, dimensions={1}, use_global_device_ids=true | all-gather | bytes 655360 | tf_op jit(solution)/shard_map/all_gather | solution.py:68
  145.3 9.2 %collective-permute-done.1 = bf16[64,1024]{1,0:T(8,128)(2,1)S(1)} collective-permute-done((bf16[64,1024]{1,0:T(8,128)(2,1)S(1)}, bf16[64,1024]{1,0:T(8,128)(2,1)S(1)}, u32[]{:S(2)}, u32[]{:S(2)}) %collective-permute-start.1) | collective-permute-done | bytes 131104 | tf_op jit(solution)/shard_map/ppermute | solution.py:15
  169.9 9.1 %collective-permute-done.2 = bf16[64,1024]{1,0:T(8,128)(2,1)S(1)} collective-permute-done((bf16[64,1024]{1,0:T(8,128)(2,1)S(1)}, bf16[64,1024]{1,0:T(8,128)(2,1)S(1)}, u32[]{:S(2)}, u32[]{:S(2)}) %collective-permute-start.2) | collective-permute-done | bytes 131104 | tf_op jit(solution)/shard_map/ppermute | solution.py:15
  179.0 7.4 %all_gather.65 = bf16[64,4096]{1,0:T(8,128)(2,1)S(1)} all-gather(bf16[64,1024]{1,0:T(8,128)(2,1)S(1)} %fusion.220), channel_id=1, replica_groups=mesh['section'=16,'dp'=8,'mp'=4] {'mp'}, dimensions={1}, use_global_device_ids=true | all-gather | bytes 655360 | tf_op jit(solution)/shard_map/all_gather | solution.py:68
  195.3 9.1 %collective-permute-done.3 = bf16[64,1024]{1,0:T(8,128)(2,1)S(1)} collective-permute-done((bf16[64,1024]{1,0:T(8,128)(2,1)S(1)}, bf16[64,1024]{1,0:T(8,128)(2,1)S(1)}, u32[]{:S(2)}, u32[]{:S(2)}) %collective-permute-start.3) | collective-permute-done | bytes 131104 | tf_op jit(solution)/shard_map/ppermute | solution.py:15
  219.9 9.1 %collective-permute-done.4 = bf16[64,1024]{1,0:T(8,128)(2,1)S(1)} collective-permute-done((bf16[64,1024]{1,0:T(8,128)(2,1)S(1)}, bf16[64,1024]{1,0:T(8,128)(2,1)S(1)}, u32[]{:S(2)}, u32[]{:S(2)}) %collective-permute-start.4) | collective-permute-done | bytes 131104 | tf_op jit(solution)/shard_map/ppermute | solution.py:15
  244.8 9.1 %collective-permute-done.5 = bf16[64,1024]{1,0:T(8,128)(2,1)S(1)} collective-permute-done((bf16[64,1024]{1,0:T(8,128)(2,1)S(1)}, bf16[64,1024]{1,0:T(8,128)(2,1)S(1)}, u32[]{:S(2)}, u32[]{:S(2)}) %collective-permute-start.5) | collective-permute-done | bytes 131104 | tf_op jit(solution)/shard_map/ppermute | solution.py:15
  269.3 9.1 %collective-permute-done.6 = bf16[64,1024]{1,0:T(8,128)(2,1)S(1)} collective-permute-done((bf16[64,1024]{1,0:T(8,128)(2,1)S(1)}, bf16[64,1024]{1,0:T(8,128)(2,1)S(1)}, u32[]{:S(2)}, u32[]{:S(2)}) %collective-permute-start.6) | collective-permute-done | bytes 131104 | tf_op jit(solution)/shard_map/ppermute | solution.py:15
  294.4 9.2 %collective-permute-done.7 = bf16[64,1024]{1,0:T(8,128)(2,1)S(1)} collective-permute-done((bf16[64,1024]{1,0:T(8,128)(2,1)S(1)}, bf16[64,1024]{1,0:T(8,128)(2,1)S(1)}, u32[]{:S(2)}, u32[]{:S(2)}) %collective-permute-start.7) | collective-permute-done | bytes 131104 | tf_op jit(solution)/shard_map/ppermute | solution.py:15
  319.0 9.2 %collective-permute-done.8 = bf16[64,1024]{1,0:T(8,128)(2,1)S(1)} collective-permute-done((bf16[64,1024]{1,0:T(8,128)(2,1)S(1)}, bf16[64,1024]{1,0:T(8,128)(2,1)S(1)}, u32[]{:S(2)}, u32[]{:S(2)}) %collective-permute-start.8) | collective-permute-done | bytes 131104 | tf_op jit(solution)/shard_map/ppermute | solution.py:15
  344.0 9.1 %collective-permute-done.9 = bf16[64,1024]{1,0:T(8,128)(2,1)S(1)} collective-permute-done((bf16[64,1024]{1,0:T(8,128)(2,1)S(1)}, bf16[64,1024]{1,0:T(8,128)(2,1)S(1)}, u32[]{:S(2)}, u32[]{:S(2)}) %collective-permute-start.9) | collective-permute-done | bytes 131104 | tf_op jit(solution)/shard_map/ppermute | solution.py:15
  368.6 9.1 %collective-permute-done.10 = bf16[64,1024]{1,0:T(8,128)(2,1)S(1)} collective-permute-done((bf16[64,1024]{1,0:T(8,128)(2,1)S(1)}, bf16[64,1024]{1,0:T(8,128)(2,1)S(1)}, u32[]{:S(2)}, u32[]{:S(2)}) %collective-permute-start.10) | collective-permute-done | bytes 131104 | tf_op jit(solution)/shard_map/ppermute | solution.py:15
  393.6 9.1 %collective-permute-done.11 = bf16[64,1024]{1,0:T(8,128)(2,1)S(1)} collective-permute-done((bf16[64,1024]{1,0:T(8,128)(2,1)S(1)}, bf16[64,1024]{1,0:T(8,128)(2,1)S(1)}, u32[]{:S(2)}, u32[]{:S(2)}) %collective-permute-start.11) | collective-permute-done | bytes 131104 | tf_op jit(solution)/shard_map/ppermute | solution.py:15
  418.2 9.1 %collective-permute-done.12 = bf16[64,1024]{1,0:T(8,128)(2,1)S(1)} collective-permute-done((bf16[64,1024]{1,0:T(8,128)(2,1)S(1)}, bf16[64,1024]{1,0:T(8,128)(2,1)S(1)}, u32[]{:S(2)}, u32[]{:S(2)}) %collective-permute-start.12) | collective-permute-done | bytes 131104 | tf_op jit(solution)/shard_map/ppermute | solution.py:15
  443.1 9.1 %collective-permute-done.13 = bf16[64,1024]{1,0:T(8,128)(2,1)S(1)} collective-permute-done((bf16[64,1024]{1,0:T(8,128)(2,1)S(1)}, bf16[64,1024]{1,0:T(8,128)(2,1)S(1)}, u32[]{:S(2)}, u32[]{:S(2)}) %collective-permute-start.13) | collective-permute-done | bytes 131104 | tf_op jit(solution)/shard_map/ppermute | solution.py:15
  467.6 9.1 %collective-permute-done.14 = bf16[64,1024]{1,0:T(8,128)(2,1)S(1)} collective-permute-done((bf16[64,1024]{1,0:T(8,128)(2,1)S(1)}, bf16[64,1024]{1,0:T(8,128)(2,1)S(1)}, u32[]{:S(2)}, u32[]{:S(2)}) %collective-permute-start.14) | collective-permute-done | bytes 131104 | tf_op jit(solution)/shard_map/ppermute | solution.py:15
  492.8 9.1 %collective-permute-done.15 = bf16[64,1024]{1,0:T(8,128)(2,1)S(1)} collective-permute-done((bf16[64,1024]{1,0:T(8,128)(2,1)S(1)}, bf16[64,1024]{1,0:T(8,128)(2,1)S(1)}, u32[]{:S(2)}, u32[]{:S(2)}) %collective-permute-start.15) | collective-permute-done | bytes 131104 | tf_op jit(solution)/shard_map/ppermute | solution.py:15
  509.9 11.1 %psum.29 = f32[16,32]{0,1:T(8,128)S(1)} all-reduce(f32[16,32]{0,1:T(8,128)S(1)} %broadcast_multiply_fusion), channel_id=1, replica_groups=mesh['section'=16,'dp'=8,'mp'=4] {'mp'}, use_global_device_ids=true, to_apply=%region_1.2 | all-reduce | flops 512 | bytes 4096 | tf_op jit(solution)/shard_map/psum | solution.py:99
  521.0 28.2 %psum.30 = f32[16,32]{0,1:T(8,128)S(1)} all-reduce(f32[16,32]{0,1:T(8,128)S(1)} %psum.29), channel_id=1, replica_groups=mesh['section'=16,'dp'=8,'mp'=4] {'dp'}, use_global_device_ids=true, to_apply=%region_2.3 | all-reduce | flops 512 | bytes 4096 | tf_op jit(solution)/shard_map/psum | solution.py:100
  549.2 71.5 %psum.31 = f32[16,32]{0,1:T(8,128)S(1)} all-reduce(f32[16,32]{0,1:T(8,128)S(1)} %psum.30), channel_id=1, replica_groups=mesh['section'=16,'dp'=8,'mp'=4] {'section'}, use_global_device_ids=true, to_apply=%region_3.4 | all-reduce | flops 512 | bytes 4096 | tf_op jit(solution)/shard_map/psum | solution.py:101
  (232 shorter events, 264.0 us)
Async XLA Ops:
  7.2 1.0 copy-start
  7.2 121.9 %copy-start.1 = (bf16[128,1024]{1,0:T(8,128)(2,1)S(1)}, bf16[128,1024]{1,0:T(8,128)(2,1)}, u32[]{:S(2)}) copy-start(bf16[128,1024]{1,0:T(8,128)(2,1)} %param.8) | copy-start | bytes 786436
  7.2 105.1 %all-gather.5.cloned.1.call-start = ((), (), s32[]{:S(2)}) async-start(), calls=%async_computation | async-start | bytes 9437184 | tf_op jit(solution)/shard_map/all_gather | solution.py:40
  118.4 10.7 %collective-permute-start = (bf16[64,1024]{1,0:T(8,128)(2,1)S(1)}, bf16[64,1024]{1,0:T(8,128)(2,1)S(1)}, u32[]{:S(2)}, u32[]{:S(2)}) collective-permute-start(bf16[64,1024]{1,0:T(8,128)(2,1)S(1)} %fusion.125), channel_id=1, source_target_pairs={{32,0},{64,32},{96,64},{128,96},{160,128},{192,160},{224,192},{256... | collective-permute-start | bytes 393224 | tf_op jit(solution)/shard_map/ppermute | solution.py:15
  143.1 11.4 %collective-permute-start.1 = (bf16[64,1024]{1,0:T(8,128)(2,1)S(1)}, bf16[64,1024]{1,0:T(8,128)(2,1)S(1)}, u32[]{:S(2)}, u32[]{:S(2)}) collective-permute-start(bf16[64,1024]{1,0:T(8,128)(2,1)S(1)} %fusion.122), channel_id=1, source_target_pairs={{32,0},{64,32},{96,64},{128,96},{160,128},{192,160},{224,192},{256... | collective-permute-start | bytes 393224 | tf_op jit(solution)/shard_map/ppermute | solution.py:15
  167.7 11.3 %collective-permute-start.2 = (bf16[64,1024]{1,0:T(8,128)(2,1)S(1)}, bf16[64,1024]{1,0:T(8,128)(2,1)S(1)}, u32[]{:S(2)}, u32[]{:S(2)}) collective-permute-start(bf16[64,1024]{1,0:T(8,128)(2,1)S(1)} %fusion.119), channel_id=1, source_target_pairs={{32,0},{64,32},{96,64},{128,96},{160,128},{192,160},{224,192},{256... | collective-permute-start | bytes 393224 | tf_op jit(solution)/shard_map/ppermute | solution.py:15
  193.2 11.3 %collective-permute-start.3 = (bf16[64,1024]{1,0:T(8,128)(2,1)S(1)}, bf16[64,1024]{1,0:T(8,128)(2,1)S(1)}, u32[]{:S(2)}, u32[]{:S(2)}) collective-permute-start(bf16[64,1024]{1,0:T(8,128)(2,1)S(1)} %fusion.116), channel_id=1, source_target_pairs={{32,0},{64,32},{96,64},{128,96},{160,128},{192,160},{224,192},{256... | collective-permute-start | bytes 393224 | tf_op jit(solution)/shard_map/ppermute | solution.py:15
  217.7 11.3 %collective-permute-start.4 = (bf16[64,1024]{1,0:T(8,128)(2,1)S(1)}, bf16[64,1024]{1,0:T(8,128)(2,1)S(1)}, u32[]{:S(2)}, u32[]{:S(2)}) collective-permute-start(bf16[64,1024]{1,0:T(8,128)(2,1)S(1)} %fusion.113), channel_id=1, source_target_pairs={{32,0},{64,32},{96,64},{128,96},{160,128},{192,160},{224,192},{256... | collective-permute-start | bytes 393224 | tf_op jit(solution)/shard_map/ppermute | solution.py:15
  242.6 11.3 %collective-permute-start.5 = (bf16[64,1024]{1,0:T(8,128)(2,1)S(1)}, bf16[64,1024]{1,0:T(8,128)(2,1)S(1)}, u32[]{:S(2)}, u32[]{:S(2)}) collective-permute-start(bf16[64,1024]{1,0:T(8,128)(2,1)S(1)} %fusion.110), channel_id=1, source_target_pairs={{32,0},{64,32},{96,64},{128,96},{160,128},{192,160},{224,192},{256... | collective-permute-start | bytes 393224 | tf_op jit(solution)/shard_map/ppermute | solution.py:15
  267.1 11.3 %collective-permute-start.6 = (bf16[64,1024]{1,0:T(8,128)(2,1)S(1)}, bf16[64,1024]{1,0:T(8,128)(2,1)S(1)}, u32[]{:S(2)}, u32[]{:S(2)}) collective-permute-start(bf16[64,1024]{1,0:T(8,128)(2,1)S(1)} %fusion.107), channel_id=1, source_target_pairs={{32,0},{64,32},{96,64},{128,96},{160,128},{192,160},{224,192},{256... | collective-permute-start | bytes 393224 | tf_op jit(solution)/shard_map/ppermute | solution.py:15
  292.2 11.4 %collective-permute-start.7 = (bf16[64,1024]{1,0:T(8,128)(2,1)S(1)}, bf16[64,1024]{1,0:T(8,128)(2,1)S(1)}, u32[]{:S(2)}, u32[]{:S(2)}) collective-permute-start(bf16[64,1024]{1,0:T(8,128)(2,1)S(1)} %fusion.104), channel_id=1, source_target_pairs={{32,0},{64,32},{96,64},{128,96},{160,128},{192,160},{224,192},{256... | collective-permute-start | bytes 393224 | tf_op jit(solution)/shard_map/ppermute | solution.py:15
  316.9 11.4 %collective-permute-start.8 = (bf16[64,1024]{1,0:T(8,128)(2,1)S(1)}, bf16[64,1024]{1,0:T(8,128)(2,1)S(1)}, u32[]{:S(2)}, u32[]{:S(2)}) collective-permute-start(bf16[64,1024]{1,0:T(8,128)(2,1)S(1)} %fusion.101), channel_id=1, source_target_pairs={{32,0},{64,32},{96,64},{128,96},{160,128},{192,160},{224,192},{256... | collective-permute-start | bytes 393224 | tf_op jit(solution)/shard_map/ppermute | solution.py:15
  341.8 11.3 %collective-permute-start.9 = (bf16[64,1024]{1,0:T(8,128)(2,1)S(1)}, bf16[64,1024]{1,0:T(8,128)(2,1)S(1)}, u32[]{:S(2)}, u32[]{:S(2)}) collective-permute-start(bf16[64,1024]{1,0:T(8,128)(2,1)S(1)} %fusion.98), channel_id=1, source_target_pairs={{32,0},{64,32},{96,64},{128,96},{160,128},{192,160},{224,192},{256... | collective-permute-start | bytes 393224 | tf_op jit(solution)/shard_map/ppermute | solution.py:15
  366.4 11.3 %collective-permute-start.10 = (bf16[64,1024]{1,0:T(8,128)(2,1)S(1)}, bf16[64,1024]{1,0:T(8,128)(2,1)S(1)}, u32[]{:S(2)}, u32[]{:S(2)}) collective-permute-start(bf16[64,1024]{1,0:T(8,128)(2,1)S(1)} %fusion.95), channel_id=1, source_target_pairs={{32,0},{64,32},{96,64},{128,96},{160,128},{192,160},{224,192},{256... | collective-permute-start | bytes 393224 | tf_op jit(solution)/shard_map/ppermute | solution.py:15
  391.5 11.3 %collective-permute-start.11 = (bf16[64,1024]{1,0:T(8,128)(2,1)S(1)}, bf16[64,1024]{1,0:T(8,128)(2,1)S(1)}, u32[]{:S(2)}, u32[]{:S(2)}) collective-permute-start(bf16[64,1024]{1,0:T(8,128)(2,1)S(1)} %fusion.92), channel_id=1, source_target_pairs={{32,0},{64,32},{96,64},{128,96},{160,128},{192,160},{224,192},{256... | collective-permute-start | bytes 393224 | tf_op jit(solution)/shard_map/ppermute | solution.py:15
  416.0 11.3 %collective-permute-start.12 = (bf16[64,1024]{1,0:T(8,128)(2,1)S(1)}, bf16[64,1024]{1,0:T(8,128)(2,1)S(1)}, u32[]{:S(2)}, u32[]{:S(2)}) collective-permute-start(bf16[64,1024]{1,0:T(8,128)(2,1)S(1)} %fusion.89), channel_id=1, source_target_pairs={{32,0},{64,32},{96,64},{128,96},{160,128},{192,160},{224,192},{256... | collective-permute-start | bytes 393224 | tf_op jit(solution)/shard_map/ppermute | solution.py:15
  440.9 11.3 %collective-permute-start.13 = (bf16[64,1024]{1,0:T(8,128)(2,1)S(1)}, bf16[64,1024]{1,0:T(8,128)(2,1)S(1)}, u32[]{:S(2)}, u32[]{:S(2)}) collective-permute-start(bf16[64,1024]{1,0:T(8,128)(2,1)S(1)} %fusion.86), channel_id=1, source_target_pairs={{32,0},{64,32},{96,64},{128,96},{160,128},{192,160},{224,192},{256... | collective-permute-start | bytes 393224 | tf_op jit(solution)/shard_map/ppermute | solution.py:15
  465.5 11.3 %collective-permute-start.14 = (bf16[64,1024]{1,0:T(8,128)(2,1)S(1)}, bf16[64,1024]{1,0:T(8,128)(2,1)S(1)}, u32[]{:S(2)}, u32[]{:S(2)}) collective-permute-start(bf16[64,1024]{1,0:T(8,128)(2,1)S(1)} %fusion.83), channel_id=1, source_target_pairs={{32,0},{64,32},{96,64},{128,96},{160,128},{192,160},{224,192},{256... | collective-permute-start | bytes 393224 | tf_op jit(solution)/shard_map/ppermute | solution.py:15
  490.6 11.3 %collective-permute-start.15 = (bf16[64,1024]{1,0:T(8,128)(2,1)S(1)}, bf16[64,1024]{1,0:T(8,128)(2,1)S(1)}, u32[]{:S(2)}, u32[]{:S(2)}) collective-permute-start(bf16[64,1024]{1,0:T(8,128)(2,1)S(1)} %fusion.80), channel_id=1, source_target_pairs={{32,0},{64,32},{96,64},{128,96},{160,128},{192,160},{224,192},{256... | collective-permute-start | bytes 393224 | tf_op jit(solution)/shard_map/ppermute | solution.py:15
Sparse Core Ops, SparseCore 0:
  10.1 102.1 all-gather.4

commit v3 on v2

--- a/solution.py
+++ b/solution.py
@@ -96,9 +96,12 @@
     table = jnp.zeros((asked, data_count * examples), jnp.float32)
     table = lax.dynamic_update_slice(table, mine, (jnp.int32(0), data_index * examples))
     score_scale = 1.0 / (low_rank * math.sqrt(section_count))
-    summed = lax.psum(table * score_scale, "mp")
-    summed = lax.psum(summed, "dp")
-    summed = lax.psum(summed, "section")
+    summed = table * score_scale
+    everyone = ("mp", "dp", "section")
+    total = section_count * data_count * model_count
+    for level in range(total.bit_length() - 1):
+        route = [(i, i ^ (1 << level)) for i in range(total)]
+        summed = summed + lax.ppermute(summed, everyone[::-1], route)
     rounds = partners.shape[0]
     per_dp = asked // data_count
     owner = jnp.arange(asked) // per_dp

time: 645 us -> 587 us (0.910)
  blocking collectives: 276 us -> 165 us
  waiting for transfers between devices: 184 us -> 218 us
  starting transfers between devices: 32.1 us -> 54.9 us
    psum x3 -> x0, blocking collectives: 111 us -> none  [the longest x1 71.5 us: body(): summed = lax.psum(summed, 'section')]
    ppermute x0 -> x9, waiting for transfers between devices: none -> 34.9 us  [body(): summed = summed + lax.ppermute(summed, everyone[::-1], route)]
    ppermute x0 -> x9, starting transfers between devices: none -> 22.7 us  [body(): summed = summed + lax.ppermute(summed, everyone[::-1], route)]
  transfers between devices with their start and end apart: 17 -> 26, of which waited for: 17 -> 26; matrix products, arithmetic and copies ran while one was open for 2% -> 2% of each run, Pallas kernels for 0% -> 0%
where the time goes in v3:
time: 587 us; the launch traced here: 578 us
  waiting for transfers between devices  218 us (37%)
  blocking collectives  165 us (28%)
  matrix products  109 us (19%)
  starting transfers between devices  54.9 us (9%)
  between operations  15.4 us (3%)
  local copies, waits for them, and re-layouts  12.2 us (2%)
    ppermute x16, waiting for transfers between devices, from_behind(): return lax.ppermute(block, axis, route)  141 us
    all_gather x17, blocking collectives, body(): grad_full = lax.all_gather(grad_piece, 'mp', axis=1, tiled=True)  115 us
    dot_general x16, matrix products, body(): lax.dot_general(grad_full, w_rows, (((1,), (1,)), ((), ())), preferred_el...  97 us
    all_gather x1, waiting for transfers between devices, body(): w_rows = lax.all_gather(weights[0], 'dp', axis=1, tiled=True)  41.3 us
    ppermute x9, waiting for transfers between devices, body(): summed = summed + lax.ppermute(summed, everyone[::-1], route)  34.9 us
    ppermute x16, starting transfers between devices, from_behind(): return lax.ppermute(block, axis, route)  32.1 us
    all_gather x1, blocking collectives, body(): queries = lax.all_gather(queries, 'dp', axis=0, tiled=True)  31 us
    ppermute x9, starting transfers between devices, body(): summed = summed + lax.ppermute(summed, everyone[::-1], route)  22.7 us
  transfers between devices with their start and end apart: 26, of which 26 were waited for; matrix products, arithmetic and copies ran while one was open for 2% of the time, Pallas kernels for 0%

profile of v3, /device:TPU:56, one launch (start us, length us, event | category | flops | bytes accessed | tf_op | source)
XLA Modules:
  0.0 577.8 jit_solution(618299365026330467)
XLA Ops:
  9.3 11.4 %psum.7 = f32[128,64]{0,1:T(8,128)S(1)} all-reduce(f32[128,64]{0,1:T(8,128)S(1)} %fusion.233), channel_id=1, replica_groups=mesh['section'=16,'dp'=8,'mp'=4] {'mp'}, use_global_device_ids=true, to_apply=%region_0.0 | all-reduce | flops 8192 | bytes 65536 | tf_op jit(solution)/shard_map/psum | solution.py:44
  29.5 7.5 %all-gather = bf16[1,4096,64]{1,2,0:T(8,128)(2,1)S(1)} all-gather(bf16[1,1024,64]{1,2,0:T(8,128)(2,1)} %param.13), channel_id=2, replica_groups=mesh['section'=16,'dp'=8,'mp'=4] {'mp'}, dimensions={1}, use_global_device_ids=true | all-gather | bytes 655360 | tf_op jit(solution)/shard_map/all_gather | solution.py:42
  39.8 31.0 %all-gather.2 = f32[1,16,1024]{2,0,1:T(1,128)S(1)} all-gather(f32[1,2,1024]{2,0,1:T(1,128)S(1)} %copy.70), channel_id=4, replica_groups=mesh['section'=16,'dp'=8,'mp'=4] {'dp'}, dimensions={1}, use_global_device_ids=true | all-gather | bytes 73728 | tf_op jit(solution)/shard_map/all_gather | solution.py:48
  71.0 41.3 %all-gather.5.cloned.1.call-done = bf16[1,1024,4096]{2,1,0:T(8,128)(2,1)} async-done(((bf16[1,1024,512]{2,1,0:T(8,128)(2,1)}), bf16[1,1024,4096]{2,1,0:T(8,128)(2,1)}) %all-gather.5.cloned.1.call-update) | async-done | bytes 8388624 | tf_op jit(solution)/shard_map/all_gather | solution.py:40
  129.2 7.2 %all_gather.63 = bf16[64,4096]{1,0:T(8,128)(2,1)S(1)} all-gather(bf16[64,1024]{1,0:T(8,128)(2,1)S(1)} %fusion.218), channel_id=1, replica_groups=mesh['section'=16,'dp'=8,'mp'=4] {'mp'}, dimensions={1}, use_global_device_ids=true | all-gather | bytes 655360 | tf_op jit(solution)/shard_map/all_gather | solution.py:68
  145.3 9.2 %collective-permute-done.1 = bf16[64,1024]{1,0:T(8,128)(2,1)S(1)} collective-permute-done((bf16[64,1024]{1,0:T(8,128)(2,1)S(1)}, bf16[64,1024]{1,0:T(8,128)(2,1)S(1)}, u32[]{:S(2)}, u32[]{:S(2)}) %collective-permute-start.1) | collective-permute-done | bytes 131104 | tf_op jit(solution)/shard_map/ppermute | solution.py:15
  169.9 9.1 %collective-permute-done.2 = bf16[64,1024]{1,0:T(8,128)(2,1)S(1)} collective-permute-done((bf16[64,1024]{1,0:T(8,128)(2,1)S(1)}, bf16[64,1024]{1,0:T(8,128)(2,1)S(1)}, u32[]{:S(2)}, u32[]{:S(2)}) %collective-permute-start.2) | collective-permute-done | bytes 131104 | tf_op jit(solution)/shard_map/ppermute | solution.py:15
  179.0 7.4 %all_gather.65 = bf16[64,4096]{1,0:T(8,128)(2,1)S(1)} all-gather(bf16[64,1024]{1,0:T(8,128)(2,1)S(1)} %fusion.220), channel_id=1, replica_groups=mesh['section'=16,'dp'=8,'mp'=4] {'mp'}, dimensions={1}, use_global_device_ids=true | all-gather | bytes 655360 | tf_op jit(solution)/shard_map/all_gather | solution.py:68
  195.3 9.1 %collective-permute-done.3 = bf16[64,1024]{1,0:T(8,128)(2,1)S(1)} collective-permute-done((bf16[64,1024]{1,0:T(8,128)(2,1)S(1)}, bf16[64,1024]{1,0:T(8,128)(2,1)S(1)}, u32[]{:S(2)}, u32[]{:S(2)}) %collective-permute-start.3) | collective-permute-done | bytes 131104 | tf_op jit(solution)/shard_map/ppermute | solution.py:15
  219.9 9.1 %collective-permute-done.4 = bf16[64,1024]{1,0:T(8,128)(2,1)S(1)} collective-permute-done((bf16[64,1024]{1,0:T(8,128)(2,1)S(1)}, bf16[64,1024]{1,0:T(8,128)(2,1)S(1)}, u32[]{:S(2)}, u32[]{:S(2)}) %collective-permute-start.4) | collective-permute-done | bytes 131104 | tf_op jit(solution)/shard_map/ppermute | solution.py:15
  244.8 9.1 %collective-permute-done.5 = bf16[64,1024]{1,0:T(8,128)(2,1)S(1)} collective-permute-done((bf16[64,1024]{1,0:T(8,128)(2,1)S(1)}, bf16[64,1024]{1,0:T(8,128)(2,1)S(1)}, u32[]{:S(2)}, u32[]{:S(2)}) %collective-permute-start.5) | collective-permute-done | bytes 131104 | tf_op jit(solution)/shard_map/ppermute | solution.py:15
  269.3 9.1 %collective-permute-done.6 = bf16[64,1024]{1,0:T(8,128)(2,1)S(1)} collective-permute-done((bf16[64,1024]{1,0:T(8,128)(2,1)S(1)}, bf16[64,1024]{1,0:T(8,128)(2,1)S(1)}, u32[]{:S(2)}, u32[]{:S(2)}) %collective-permute-start.6) | collective-permute-done | bytes 131104 | tf_op jit(solution)/shard_map/ppermute | solution.py:15
  278.4 7.1 %all_gather.69 = bf16[64,4096]{1,0:T(8,128)(2,1)S(1)} all-gather(bf16[64,1024]{1,0:T(8,128)(2,1)S(1)} %fusion.224), channel_id=1, replica_groups=mesh['section'=16,'dp'=8,'mp'=4] {'mp'}, dimensions={1}, use_global_device_ids=true | all-gather | bytes 655360 | tf_op jit(solution)/shard_map/all_gather | solution.py:68
  294.4 9.2 %collective-permute-done.7 = bf16[64,1024]{1,0:T(8,128)(2,1)S(1)} collective-permute-done((bf16[64,1024]{1,0:T(8,128)(2,1)S(1)}, bf16[64,1024]{1,0:T(8,128)(2,1)S(1)}, u32[]{:S(2)}, u32[]{:S(2)}) %collective-permute-start.7) | collective-permute-done | bytes 131104 | tf_op jit(solution)/shard_map/ppermute | solution.py:15
  319.0 8.9 %collective-permute-done.8 = bf16[64,1024]{1,0:T(8,128)(2,1)S(1)} collective-permute-done((bf16[64,1024]{1,0:T(8,128)(2,1)S(1)}, bf16[64,1024]{1,0:T(8,128)(2,1)S(1)}, u32[]{:S(2)}, u32[]{:S(2)}) %collective-permute-start.8) | collective-permute-done | bytes 131104 | tf_op jit(solution)/shard_map/ppermute | solution.py:15
  343.5 8.9 %collective-permute-done.9 = bf16[64,1024]{1,0:T(8,128)(2,1)S(1)} collective-permute-done((bf16[64,1024]{1,0:T(8,128)(2,1)S(1)}, bf16[64,1024]{1,0:T(8,128)(2,1)S(1)}, u32[]{:S(2)}, u32[]{:S(2)}) %collective-permute-start.9) | collective-permute-done | bytes 131104 | tf_op jit(solution)/shard_map/ppermute | solution.py:15
  367.8 8.9 %collective-permute-done.10 = bf16[64,1024]{1,0:T(8,128)(2,1)S(1)} collective-permute-done((bf16[64,1024]{1,0:T(8,128)(2,1)S(1)}, bf16[64,1024]{1,0:T(8,128)(2,1)S(1)}, u32[]{:S(2)}, u32[]{:S(2)}) %collective-permute-start.10) | collective-permute-done | bytes 131104 | tf_op jit(solution)/shard_map/ppermute | solution.py:15
  392.5 8.9 %collective-permute-done.11 = bf16[64,1024]{1,0:T(8,128)(2,1)S(1)} collective-permute-done((bf16[64,1024]{1,0:T(8,128)(2,1)S(1)}, bf16[64,1024]{1,0:T(8,128)(2,1)S(1)}, u32[]{:S(2)}, u32[]{:S(2)}) %collective-permute-start.11) | collective-permute-done | bytes 131104 | tf_op jit(solution)/shard_map/ppermute | solution.py:15
  416.8 8.9 %collective-permute-done.12 = bf16[64,1024]{1,0:T(8,128)(2,1)S(1)} collective-permute-done((bf16[64,1024]{1,0:T(8,128)(2,1)S(1)}, bf16[64,1024]{1,0:T(8,128)(2,1)S(1)}, u32[]{:S(2)}, u32[]{:S(2)}) %collective-permute-start.12) | collective-permute-done | bytes 131104 | tf_op jit(solution)/shard_map/ppermute | solution.py:15
  441.3 8.9 %collective-permute-done.13 = bf16[64,1024]{1,0:T(8,128)(2,1)S(1)} collective-permute-done((bf16[64,1024]{1,0:T(8,128)(2,1)S(1)}, bf16[64,1024]{1,0:T(8,128)(2,1)S(1)}, u32[]{:S(2)}, u32[]{:S(2)}) %collective-permute-start.13) | collective-permute-done | bytes 131104 | tf_op jit(solution)/shard_map/ppermute | solution.py:15
  465.6 8.9 %collective-permute-done.14 = bf16[64,1024]{1,0:T(8,128)(2,1)S(1)} collective-permute-done((bf16[64,1024]{1,0:T(8,128)(2,1)S(1)}, bf16[64,1024]{1,0:T(8,128)(2,1)S(1)}, u32[]{:S(2)}, u32[]{:S(2)}) %collective-permute-start.14) | collective-permute-done | bytes 131104 | tf_op jit(solution)/shard_map/ppermute | solution.py:15
  474.6 7.0 %all_gather.77 = bf16[64,4096]{1,0:T(8,128)(2,1)S(1)} all-gather(bf16[64,1024]{1,0:T(8,128)(2,1)S(1)} %fusion.232), channel_id=1, replica_groups=mesh['section'=16,'dp'=8,'mp'=4] {'mp'}, dimensions={1}, use_global_device_ids=true | all-gather | bytes 655360 | tf_op jit(solution)/shard_map/all_gather | solution.py:68
  490.3 8.9 %collective-permute-done.15 = bf16[64,1024]{1,0:T(8,128)(2,1)S(1)} collective-permute-done((bf16[64,1024]{1,0:T(8,128)(2,1)S(1)}, bf16[64,1024]{1,0:T(8,128)(2,1)S(1)}, u32[]{:S(2)}, u32[]{:S(2)}) %collective-permute-start.15) | collective-permute-done | bytes 131104 | tf_op jit(solution)/shard_map/ppermute | solution.py:15
  551.3 7.5 %collective-permute-done.23 = f32[16,32]{0,1:T(8,128)S(1)} collective-permute-done((f32[16,32]{0,1:T(8,128)S(1)}, f32[16,32]{0,1:T(8,128)S(1)}, u32[]{:S(2)}, u32[]{:S(2)}) %collective-permute-start.23) | collective-permute-done | bytes 2080 | tf_op jit(solution)/shard_map/ppermute | solution.py:104
  (256 shorter events, 299.8 us)
Async XLA Ops:
  7.2 105.1 %all-gather.5.cloned.1.call-start = ((), (), s32[]{:S(2)}) async-start(), calls=%async_computation | async-start | bytes 9437184 | tf_op jit(solution)/shard_map/all_gather | solution.py:40
  118.4 10.7 %collective-permute-start = (bf16[64,1024]{1,0:T(8,128)(2,1)S(1)}, bf16[64,1024]{1,0:T(8,128)(2,1)S(1)}, u32[]{:S(2)}, u32[]{:S(2)}) collective-permute-start(bf16[64,1024]{1,0:T(8,128)(2,1)S(1)} %fusion.125), channel_id=1, source_target_pairs={{32,0},{64,32},{96,64},{128,96},{160,128},{192,160},{224,192},{256... | collective-permute-start | bytes 393224 | tf_op jit(solution)/shard_map/ppermute | solution.py:15
  143.1 11.4 %collective-permute-start.1 = (bf16[64,1024]{1,0:T(8,128)(2,1)S(1)}, bf16[64,1024]{1,0:T(8,128)(2,1)S(1)}, u32[]{:S(2)}, u32[]{:S(2)}) collective-permute-start(bf16[64,1024]{1,0:T(8,128)(2,1)S(1)} %fusion.122), channel_id=1, source_target_pairs={{32,0},{64,32},{96,64},{128,96},{160,128},{192,160},{224,192},{256... | collective-permute-start | bytes 393224 | tf_op jit(solution)/shard_map/ppermute | solution.py:15
  167.7 11.3 %collective-permute-start.2 = (bf16[64,1024]{1,0:T(8,128)(2,1)S(1)}, bf16[64,1024]{1,0:T(8,128)(2,1)S(1)}, u32[]{:S(2)}, u32[]{:S(2)}) collective-permute-start(bf16[64,1024]{1,0:T(8,128)(2,1)S(1)} %fusion.119), channel_id=1, source_target_pairs={{32,0},{64,32},{96,64},{128,96},{160,128},{192,160},{224,192},{256... | collective-permute-start | bytes 393224 | tf_op jit(solution)/shard_map/ppermute | solution.py:15
  193.2 11.3 %collective-permute-start.3 = (bf16[64,1024]{1,0:T(8,128)(2,1)S(1)}, bf16[64,1024]{1,0:T(8,128)(2,1)S(1)}, u32[]{:S(2)}, u32[]{:S(2)}) collective-permute-start(bf16[64,1024]{1,0:T(8,128)(2,1)S(1)} %fusion.116), channel_id=1, source_target_pairs={{32,0},{64,32},{96,64},{128,96},{160,128},{192,160},{224,192},{256... | collective-permute-start | bytes 393224 | tf_op jit(solution)/shard_map/ppermute | solution.py:15
  217.7 11.3 %collective-permute-start.4 = (bf16[64,1024]{1,0:T(8,128)(2,1)S(1)}, bf16[64,1024]{1,0:T(8,128)(2,1)S(1)}, u32[]{:S(2)}, u32[]{:S(2)}) collective-permute-start(bf16[64,1024]{1,0:T(8,128)(2,1)S(1)} %fusion.113), channel_id=1, source_target_pairs={{32,0},{64,32},{96,64},{128,96},{160,128},{192,160},{224,192},{256... | collective-permute-start | bytes 393224 | tf_op jit(solution)/shard_map/ppermute | solution.py:15
  242.6 11.3 %collective-permute-start.5 = (bf16[64,1024]{1,0:T(8,128)(2,1)S(1)}, bf16[64,1024]{1,0:T(8,128)(2,1)S(1)}, u32[]{:S(2)}, u32[]{:S(2)}) collective-permute-start(bf16[64,1024]{1,0:T(8,128)(2,1)S(1)} %fusion.110), channel_id=1, source_target_pairs={{32,0},{64,32},{96,64},{128,96},{160,128},{192,160},{224,192},{256... | collective-permute-start | bytes 393224 | tf_op jit(solution)/shard_map/ppermute | solution.py:15
  267.1 11.3 %collective-permute-start.6 = (bf16[64,1024]{1,0:T(8,128)(2,1)S(1)}, bf16[64,1024]{1,0:T(8,128)(2,1)S(1)}, u32[]{:S(2)}, u32[]{:S(2)}) collective-permute-start(bf16[64,1024]{1,0:T(8,128)(2,1)S(1)} %fusion.107), channel_id=1, source_target_pairs={{32,0},{64,32},{96,64},{128,96},{160,128},{192,160},{224,192},{256... | collective-permute-start | bytes 393224 | tf_op jit(solution)/shard_map/ppermute | solution.py:15
  292.2 11.4 %collective-permute-start.7 = (bf16[64,1024]{1,0:T(8,128)(2,1)S(1)}, bf16[64,1024]{1,0:T(8,128)(2,1)S(1)}, u32[]{:S(2)}, u32[]{:S(2)}) collective-permute-start(bf16[64,1024]{1,0:T(8,128)(2,1)S(1)} %fusion.104), channel_id=1, source_target_pairs={{32,0},{64,32},{96,64},{128,96},{160,128},{192,160},{224,192},{256... | collective-permute-start | bytes 393224 | tf_op jit(solution)/shard_map/ppermute | solution.py:15
  316.6 11.4 %collective-permute-start.8 = (bf16[64,1024]{1,0:T(8,128)(2,1)S(1)}, bf16[64,1024]{1,0:T(8,128)(2,1)S(1)}, u32[]{:S(2)}, u32[]{:S(2)}) collective-permute-start(bf16[64,1024]{1,0:T(8,128)(2,1)S(1)} %fusion.101), channel_id=1, source_target_pairs={{32,0},{64,32},{96,64},{128,96},{160,128},{192,160},{224,192},{256... | collective-permute-start | bytes 393224 | tf_op jit(solution)/shard_map/ppermute | solution.py:15
  341.1 11.3 %collective-permute-start.9 = (bf16[64,1024]{1,0:T(8,128)(2,1)S(1)}, bf16[64,1024]{1,0:T(8,128)(2,1)S(1)}, u32[]{:S(2)}, u32[]{:S(2)}) collective-permute-start(bf16[64,1024]{1,0:T(8,128)(2,1)S(1)} %fusion.98), channel_id=1, source_target_pairs={{32,0},{64,32},{96,64},{128,96},{160,128},{192,160},{224,192},{256... | collective-permute-start | bytes 393224 | tf_op jit(solution)/shard_map/ppermute | solution.py:15
  365.5 11.3 %collective-permute-start.10 = (bf16[64,1024]{1,0:T(8,128)(2,1)S(1)}, bf16[64,1024]{1,0:T(8,128)(2,1)S(1)}, u32[]{:S(2)}, u32[]{:S(2)}) collective-permute-start(bf16[64,1024]{1,0:T(8,128)(2,1)S(1)} %fusion.95), channel_id=1, source_target_pairs={{32,0},{64,32},{96,64},{128,96},{160,128},{192,160},{224,192},{256... | collective-permute-start | bytes 393224 | tf_op jit(solution)/shard_map/ppermute | solution.py:15
  390.1 11.3 %collective-permute-start.11 = (bf16[64,1024]{1,0:T(8,128)(2,1)S(1)}, bf16[64,1024]{1,0:T(8,128)(2,1)S(1)}, u32[]{:S(2)}, u32[]{:S(2)}) collective-permute-start(bf16[64,1024]{1,0:T(8,128)(2,1)S(1)} %fusion.92), channel_id=1, source_target_pairs={{32,0},{64,32},{96,64},{128,96},{160,128},{192,160},{224,192},{256... | collective-permute-start | bytes 393224 | tf_op jit(solution)/shard_map/ppermute | solution.py:15
  414.5 11.3 %collective-permute-start.12 = (bf16[64,1024]{1,0:T(8,128)(2,1)S(1)}, bf16[64,1024]{1,0:T(8,128)(2,1)S(1)}, u32[]{:S(2)}, u32[]{:S(2)}) collective-permute-start(bf16[64,1024]{1,0:T(8,128)(2,1)S(1)} %fusion.89), channel_id=1, source_target_pairs={{32,0},{64,32},{96,64},{128,96},{160,128},{192,160},{224,192},{256... | collective-permute-start | bytes 393224 | tf_op jit(solution)/shard_map/ppermute | solution.py:15
  438.9 11.3 %collective-permute-start.13 = (bf16[64,1024]{1,0:T(8,128)(2,1)S(1)}, bf16[64,1024]{1,0:T(8,128)(2,1)S(1)}, u32[]{:S(2)}, u32[]{:S(2)}) collective-permute-start(bf16[64,1024]{1,0:T(8,128)(2,1)S(1)} %fusion.86), channel_id=1, source_target_pairs={{32,0},{64,32},{96,64},{128,96},{160,128},{192,160},{224,192},{256... | collective-permute-start | bytes 393224 | tf_op jit(solution)/shard_map/ppermute | solution.py:15
  463.3 11.3 %collective-permute-start.14 = (bf16[64,1024]{1,0:T(8,128)(2,1)S(1)}, bf16[64,1024]{1,0:T(8,128)(2,1)S(1)}, u32[]{:S(2)}, u32[]{:S(2)}) collective-permute-start(bf16[64,1024]{1,0:T(8,128)(2,1)S(1)} %fusion.83), channel_id=1, source_target_pairs={{32,0},{64,32},{96,64},{128,96},{160,128},{192,160},{224,192},{256... | collective-permute-start | bytes 393224 | tf_op jit(solution)/shard_map/ppermute | solution.py:15
  488.0 11.3 %collective-permute-start.15 = (bf16[64,1024]{1,0:T(8,128)(2,1)S(1)}, bf16[64,1024]{1,0:T(8,128)(2,1)S(1)}, u32[]{:S(2)}, u32[]{:S(2)}) collective-permute-start(bf16[64,1024]{1,0:T(8,128)(2,1)S(1)} %fusion.80), channel_id=1, source_target_pairs={{32,0},{64,32},{96,64},{128,96},{160,128},{192,160},{224,192},{256... | collective-permute-start | bytes 393224 | tf_op jit(solution)/shard_map/ppermute | solution.py:15
  515.4 5.6 collective-permute-start.18
  521.0 6.5 %collective-permute-start.19 = (f32[16,32]{0,1:T(8,128)S(1)}, f32[16,32]{0,1:T(8,128)S(1)}, u32[]{:S(2)}, u32[]{:S(2)}) collective-permute-start(f32[16,32]{0,1:T(8,128)S(1)} %add.399), channel_id=1, source_target_pairs={{0,8},{1,9},{2,10},{3,11},{4,12},{5,13},{6,14},{7,15},{8,0},{9,1},... | collective-permute-start | bytes 6152 | tf_op jit(solution)/shard_map/ppermute | solution.py:104
  527.5 9.5 %collective-permute-start.20 = (f32[16,32]{0,1:T(8,128)S(1)}, f32[16,32]{0,1:T(8,128)S(1)}, u32[]{:S(2)}, u32[]{:S(2)}) collective-permute-start(f32[16,32]{0,1:T(8,128)S(1)} %add.400), channel_id=1, source_target_pairs={{0,16},{1,17},{2,18},{3,19},{4,20},{5,21},{6,22},{7,23},{8,24},{9,... | collective-permute-start | bytes 6152 | tf_op jit(solution)/shard_map/ppermute | solution.py:104
  537.1 5.6 collective-permute-start.21
  542.7 6.5 %collective-permute-start.22 = (f32[16,32]{0,1:T(8,128)S(1)}, f32[16,32]{0,1:T(8,128)S(1)}, u32[]{:S(2)}, u32[]{:S(2)}) collective-permute-start(f32[16,32]{0,1:T(8,128)S(1)} %add.402), channel_id=1, source_target_pairs={{0,64},{1,65},{2,66},{3,67},{4,68},{5,69},{6,70},{7,71},{8,72},{9,... | collective-permute-start | bytes 6152 | tf_op jit(solution)/shard_map/ppermute | solution.py:104
  549.2 9.5 %collective-permute-start.23 = (f32[16,32]{0,1:T(8,128)S(1)}, f32[16,32]{0,1:T(8,128)S(1)}, u32[]{:S(2)}, u32[]{:S(2)}) collective-permute-start(f32[16,32]{0,1:T(8,128)S(1)} %add.403), channel_id=1, source_target_pairs={{0,128},{1,129},{2,130},{3,131},{4,132},{5,133},{6,134},{7,135},{8... | collective-permute-start | bytes 6152 | tf_op jit(solution)/shard_map/ppermute | solution.py:104
  558.8 7.1 %collective-permute-start.24 = (f32[16,32]{0,1:T(8,128)S(1)}, f32[16,32]{0,1:T(8,128)S(1)}, u32[]{:S(2)}, u32[]{:S(2)}) collective-permute-start(f32[16,32]{0,1:T(8,128)S(1)} %add.404), channel_id=1, source_target_pairs={{0,256},{1,257},{2,258},{3,259},{4,260},{5,261},{6,262},{7,263},{8... | collective-permute-start | bytes 6152 | tf_op jit(solution)/shard_map/ppermute | solution.py:104
  (4 other events, 131.6 us)
Sparse Core Ops, SparseCore 0:
  10.1 102.1 all-gather.4

commit v4 on v3

--- a/solution.py
+++ b/solution.py
@@ -3,6 +3,7 @@
 import jax
 import jax.numpy as jnp
 from jax import lax
+from jax.experimental.layout import Layout, with_layout_constraint
 from jax.sharding import PartitionSpec as P
 
 LEN = 32
@@ -37,7 +38,8 @@
     top_section = section_count - 1
     piece_rank = low_rank // model_count
 
-    w_rows = lax.all_gather(weights[0], "dp", axis=1, tiled=True)
+    w_cols = lax.all_gather(weights[0].T, "dp", axis=0, tiled=True)
+    w_cols = with_layout_constraint(w_cols, Layout(major_to_minor=(0, 1)))
     slopes = silu_slope(pre_acts[0].astype(jnp.float32))
     out_proj = lax.all_gather(proj_out[0], "mp", axis=0, tiled=True)
     in_part = jnp.dot(saved_inputs[0], proj_in[0], preferred_element_type=jnp.float32)
@@ -67,9 +69,7 @@
         grad_piece = (delta_piece.astype(jnp.float32) * slope_rows).astype(jnp.bfloat16)
         grad_full = lax.all_gather(grad_piece, "mp", axis=1, tiled=True)
         if turn < step_count - 1:
-            back_term = lax.dot_general(
-                grad_full, w_rows, (((1,), (1,)), ((), ())), preferred_element_type=jnp.float32
-            )
+            back_term = jnp.dot(grad_full, w_cols, preferred_element_type=jnp.float32)
             outgoing = (delta_piece.astype(jnp.float32) + back_term).astype(jnp.bfloat16)
 
         out_side = jnp.dot(grad_full, out_proj, preferred_element_type=jnp.float32)

time: 587 us -> 563 us (0.959); the launches traced: 578 us -> 561 us
  matrix products: 109 us -> 91.6 us
    dot_general x16, matrix products: 97 us -> 79.6 us  [body(): back_term = jnp.dot(grad_full, w_cols, preferred_element_type=jnp.float32)]
where the time goes in v4:
time: 563 us; the launch traced here: 561 us
  waiting for transfers between devices  217 us (39%)
  blocking collectives  164 us (29%)
  matrix products  91.6 us (16%)
  starting transfers between devices  55.1 us (10%)
  between operations  15.3 us (3%)
  local copies, waits for them, and re-layouts  14.6 us (3%)
    ppermute x16, waiting for transfers between devices, from_behind(): return lax.ppermute(block, axis, route)  143 us
    all_gather x17, blocking collectives, body(): grad_full = lax.all_gather(grad_piece, 'mp', axis=1, tiled=True)  114 us
    dot_general x16, matrix products, body(): back_term = jnp.dot(grad_full, w_cols, preferred_element_type=jnp.float32)  79.6 us
    all_gather x1, waiting for transfers between devices, body(): w_cols = lax.all_gather(weights[0].T, 'dp', axis=0, tiled=True)  39.6 us
    ppermute x9, waiting for transfers between devices, body(): summed = summed + lax.ppermute(summed, everyone[::-1], route)  34.8 us
    ppermute x16, starting transfers between devices, from_behind(): return lax.ppermute(block, axis, route)  32.3 us
    all_gather x1, blocking collectives, body(): queries = lax.all_gather(queries, 'dp', axis=0, tiled=True)  31 us
    ppermute x9, starting transfers between devices, body(): summed = summed + lax.ppermute(summed, everyone[::-1], route)  22.8 us
  transfers between devices with their start and end apart: 26, of which 26 were waited for; matrix products, arithmetic and copies ran while one was open for 2% of the time, Pallas kernels for 0%

profile of v4, /device:TPU:56, one launch (start us, length us, event | category | flops | bytes accessed | tf_op | source)
XLA Modules:
  0.0 561.5 jit_solution(10484083094636745124)
XLA Ops:
  11.0 11.4 %psum.7 = f32[128,64]{0,1:T(8,128)S(1)} all-reduce(f32[128,64]{0,1:T(8,128)S(1)} %fusion.121), channel_id=1, replica_groups=mesh['section'=16,'dp'=8,'mp'=4] {'mp'}, use_global_device_ids=true, to_apply=%region_0.0 | all-reduce | flops 8192 | bytes 65536 | tf_op jit(solution)/shard_map/psum | solution.py:46
  31.2 7.5 %all-gather = bf16[1,4096,64]{1,2,0:T(8,128)(2,1)S(1)} all-gather(bf16[1,1024,64]{1,2,0:T(8,128)(2,1)} %param.13), channel_id=2, replica_groups=mesh['section'=16,'dp'=8,'mp'=4] {'mp'}, dimensions={1}, use_global_device_ids=true | all-gather | bytes 655360 | tf_op jit(solution)/shard_map/all_gather | solution.py:44
  41.5 31.0 %all-gather.1 = f32[1,16,1024]{2,0,1:T(1,128)S(1)} all-gather(f32[1,2,1024]{2,0,1:T(1,128)S(1)} %copy.74), channel_id=3, replica_groups=mesh['section'=16,'dp'=8,'mp'=4] {'dp'}, dimensions={1}, use_global_device_ids=true | all-gather | bytes 73728 | tf_op jit(solution)/shard_map/all_gather | solution.py:50
  72.8 39.6 %all-gather.4.cloned.1.call-done = bf16[4096,1024]{1,0:T(8,128)(2,1)} async-done(((bf16[512,1024]{1,0:T(8,128)(2,1)}), bf16[4096,1024]{1,0:T(8,128)(2,1)}) %all-gather.4.cloned.1.call-update) | async-done | bytes 8388624 | tf_op jit(solution)/shard_map/all_gather | solution.py:41
  128.1 7.2 %all_gather.63 = bf16[64,4096]{1,0:T(8,128)(2,1)S(1)} all-gather(bf16[64,1024]{1,0:T(8,128)(2,1)S(1)} %fusion.106), channel_id=1, replica_groups=mesh['section'=16,'dp'=8,'mp'=4] {'mp'}, dimensions={1}, use_global_device_ids=true | all-gather | bytes 655360 | tf_op jit(solution)/shard_map/all_gather | solution.py:70
  143.1 9.2 %collective-permute-done.1 = bf16[64,1024]{1,0:T(8,128)(2,1)S(1)} collective-permute-done((bf16[64,1024]{1,0:T(8,128)(2,1)S(1)}, bf16[64,1024]{1,0:T(8,128)(2,1)S(1)}, u32[]{:S(2)}, u32[]{:S(2)}) %collective-permute-start.1) | collective-permute-done | bytes 131104 | tf_op jit(solution)/shard_map/ppermute | solution.py:16
  166.7 9.1 %collective-permute-done.2 = bf16[64,1024]{1,0:T(8,128)(2,1)S(1)} collective-permute-done((bf16[64,1024]{1,0:T(8,128)(2,1)S(1)}, bf16[64,1024]{1,0:T(8,128)(2,1)S(1)}, u32[]{:S(2)}, u32[]{:S(2)}) %collective-permute-start.2) | collective-permute-done | bytes 131104 | tf_op jit(solution)/shard_map/ppermute | solution.py:16
  175.8 6.9 %all_gather.65 = bf16[64,4096]{1,0:T(8,128)(2,1)S(1)} all-gather(bf16[64,1024]{1,0:T(8,128)(2,1)S(1)} %fusion.108), channel_id=1, replica_groups=mesh['section'=16,'dp'=8,'mp'=4] {'mp'}, dimensions={1}, use_global_device_ids=true | all-gather | bytes 655360 | tf_op jit(solution)/shard_map/all_gather | solution.py:70
  190.5 9.1 %collective-permute-done.3 = bf16[64,1024]{1,0:T(8,128)(2,1)S(1)} collective-permute-done((bf16[64,1024]{1,0:T(8,128)(2,1)S(1)}, bf16[64,1024]{1,0:T(8,128)(2,1)S(1)}, u32[]{:S(2)}, u32[]{:S(2)}) %collective-permute-start.3) | collective-permute-done | bytes 131104 | tf_op jit(solution)/shard_map/ppermute | solution.py:16
  214.2 9.1 %collective-permute-done.4 = bf16[64,1024]{1,0:T(8,128)(2,1)S(1)} collective-permute-done((bf16[64,1024]{1,0:T(8,128)(2,1)S(1)}, bf16[64,1024]{1,0:T(8,128)(2,1)S(1)}, u32[]{:S(2)}, u32[]{:S(2)}) %collective-permute-start.4) | collective-permute-done | bytes 131104 | tf_op jit(solution)/shard_map/ppermute | solution.py:16
  238.0 9.1 %collective-permute-done.5 = bf16[64,1024]{1,0:T(8,128)(2,1)S(1)} collective-permute-done((bf16[64,1024]{1,0:T(8,128)(2,1)S(1)}, bf16[64,1024]{1,0:T(8,128)(2,1)S(1)}, u32[]{:S(2)}, u32[]{:S(2)}) %collective-permute-start.5) | collective-permute-done | bytes 131104 | tf_op jit(solution)/shard_map/ppermute | solution.py:16
  261.5 9.2 %collective-permute-done.6 = bf16[64,1024]{1,0:T(8,128)(2,1)S(1)} collective-permute-done((bf16[64,1024]{1,0:T(8,128)(2,1)S(1)}, bf16[64,1024]{1,0:T(8,128)(2,1)S(1)}, u32[]{:S(2)}, u32[]{:S(2)}) %collective-permute-start.6) | collective-permute-done | bytes 131104 | tf_op jit(solution)/shard_map/ppermute | solution.py:16
  270.7 6.9 %all_gather.69 = bf16[64,4096]{1,0:T(8,128)(2,1)S(1)} all-gather(bf16[64,1024]{1,0:T(8,128)(2,1)S(1)} %fusion.112), channel_id=1, replica_groups=mesh['section'=16,'dp'=8,'mp'=4] {'mp'}, dimensions={1}, use_global_device_ids=true | all-gather | bytes 655360 | tf_op jit(solution)/shard_map/all_gather | solution.py:70
  285.4 9.2 %collective-permute-done.7 = bf16[64,1024]{1,0:T(8,128)(2,1)S(1)} collective-permute-done((bf16[64,1024]{1,0:T(8,128)(2,1)S(1)}, bf16[64,1024]{1,0:T(8,128)(2,1)S(1)}, u32[]{:S(2)}, u32[]{:S(2)}) %collective-permute-start.7) | collective-permute-done | bytes 131104 | tf_op jit(solution)/shard_map/ppermute | solution.py:16
  308.9 9.0 %collective-permute-done.8 = bf16[64,1024]{1,0:T(8,128)(2,1)S(1)} collective-permute-done((bf16[64,1024]{1,0:T(8,128)(2,1)S(1)}, bf16[64,1024]{1,0:T(8,128)(2,1)S(1)}, u32[]{:S(2)}, u32[]{:S(2)}) %collective-permute-start.8) | collective-permute-done | bytes 131104 | tf_op jit(solution)/shard_map/ppermute | solution.py:16
  332.5 9.2 %collective-permute-done.9 = bf16[64,1024]{1,0:T(8,128)(2,1)S(1)} collective-permute-done((bf16[64,1024]{1,0:T(8,128)(2,1)S(1)}, bf16[64,1024]{1,0:T(8,128)(2,1)S(1)}, u32[]{:S(2)}, u32[]{:S(2)}) %collective-permute-start.9) | collective-permute-done | bytes 131104 | tf_op jit(solution)/shard_map/ppermute | solution.py:16
  355.9 9.2 %collective-permute-done.10 = bf16[64,1024]{1,0:T(8,128)(2,1)S(1)} collective-permute-done((bf16[64,1024]{1,0:T(8,128)(2,1)S(1)}, bf16[64,1024]{1,0:T(8,128)(2,1)S(1)}, u32[]{:S(2)}, u32[]{:S(2)}) %collective-permute-start.10) | collective-permute-done | bytes 131104 | tf_op jit(solution)/shard_map/ppermute | solution.py:16
  365.1 7.1 %all_gather.73 = bf16[64,4096]{1,0:T(8,128)(2,1)S(1)} all-gather(bf16[64,1024]{1,0:T(8,128)(2,1)S(1)} %fusion.116), channel_id=1, replica_groups=mesh['section'=16,'dp'=8,'mp'=4] {'mp'}, dimensions={1}, use_global_device_ids=true | all-gather | bytes 655360 | tf_op jit(solution)/shard_map/all_gather | solution.py:70
  379.9 9.2 %collective-permute-done.11 = bf16[64,1024]{1,0:T(8,128)(2,1)S(1)} collective-permute-done((bf16[64,1024]{1,0:T(8,128)(2,1)S(1)}, bf16[64,1024]{1,0:T(8,128)(2,1)S(1)}, u32[]{:S(2)}, u32[]{:S(2)}) %collective-permute-start.11) | collective-permute-done | bytes 131104 | tf_op jit(solution)/shard_map/ppermute | solution.py:16
  403.3 9.2 %collective-permute-done.12 = bf16[64,1024]{1,0:T(8,128)(2,1)S(1)} collective-permute-done((bf16[64,1024]{1,0:T(8,128)(2,1)S(1)}, bf16[64,1024]{1,0:T(8,128)(2,1)S(1)}, u32[]{:S(2)}, u32[]{:S(2)}) %collective-permute-start.12) | collective-permute-done | bytes 131104 | tf_op jit(solution)/shard_map/ppermute | solution.py:16
  427.0 9.2 %collective-permute-done.13 = bf16[64,1024]{1,0:T(8,128)(2,1)S(1)} collective-permute-done((bf16[64,1024]{1,0:T(8,128)(2,1)S(1)}, bf16[64,1024]{1,0:T(8,128)(2,1)S(1)}, u32[]{:S(2)}, u32[]{:S(2)}) %collective-permute-start.13) | collective-permute-done | bytes 131104 | tf_op jit(solution)/shard_map/ppermute | solution.py:16
  450.4 9.2 %collective-permute-done.14 = bf16[64,1024]{1,0:T(8,128)(2,1)S(1)} collective-permute-done((bf16[64,1024]{1,0:T(8,128)(2,1)S(1)}, bf16[64,1024]{1,0:T(8,128)(2,1)S(1)}, u32[]{:S(2)}, u32[]{:S(2)}) %collective-permute-start.14) | collective-permute-done | bytes 131104 | tf_op jit(solution)/shard_map/ppermute | solution.py:16
  474.1 9.2 %collective-permute-done.15 = bf16[64,1024]{1,0:T(8,128)(2,1)S(1)} collective-permute-done((bf16[64,1024]{1,0:T(8,128)(2,1)S(1)}, bf16[64,1024]{1,0:T(8,128)(2,1)S(1)}, u32[]{:S(2)}, u32[]{:S(2)}) %collective-permute-start.15) | collective-permute-done | bytes 131104 | tf_op jit(solution)/shard_map/ppermute | solution.py:16
  535.1 7.5 %collective-permute-done.23 = f32[16,32]{0,1:T(8,128)S(1)} collective-permute-done((f32[16,32]{0,1:T(8,128)S(1)}, f32[16,32]{0,1:T(8,128)S(1)}, u32[]{:S(2)}, u32[]{:S(2)}) %collective-permute-start.23) | collective-permute-done | bytes 2080 | tf_op jit(solution)/shard_map/ppermute | solution.py:104
  (257 shorter events, 284.0 us)
Async XLA Ops:
  7.2 105.2 %all-gather.4.cloned.1.call-start = ((), (), s32[]{:S(2)}) async-start(), calls=%async_computation | async-start | bytes 9437184 | tf_op jit(solution)/shard_map/all_gather | solution.py:41
  117.3 10.7 %collective-permute-start = (bf16[64,1024]{1,0:T(8,128)(2,1)S(1)}, bf16[64,1024]{1,0:T(8,128)(2,1)S(1)}, u32[]{:S(2)}, u32[]{:S(2)}) collective-permute-start(bf16[64,1024]{1,0:T(8,128)(2,1)S(1)} %fusion), channel_id=1, source_target_pairs={{32,0},{64,32},{96,64},{128,96},{160,128},{192,160},{224,192},{256... | collective-permute-start | bytes 393224 | tf_op jit(solution)/shard_map/ppermute | solution.py:16
  141.0 11.4 %collective-permute-start.1 = (bf16[64,1024]{1,0:T(8,128)(2,1)S(1)}, bf16[64,1024]{1,0:T(8,128)(2,1)S(1)}, u32[]{:S(2)}, u32[]{:S(2)}) collective-permute-start(bf16[64,1024]{1,0:T(8,128)(2,1)S(1)} %fusion.1), channel_id=1, source_target_pairs={{32,0},{64,32},{96,64},{128,96},{160,128},{192,160},{224,192},{256... | collective-permute-start | bytes 393224 | tf_op jit(solution)/shard_map/ppermute | solution.py:16
  164.5 11.3 %collective-permute-start.2 = (bf16[64,1024]{1,0:T(8,128)(2,1)S(1)}, bf16[64,1024]{1,0:T(8,128)(2,1)S(1)}, u32[]{:S(2)}, u32[]{:S(2)}) collective-permute-start(bf16[64,1024]{1,0:T(8,128)(2,1)S(1)} %fusion.2), channel_id=1, source_target_pairs={{32,0},{64,32},{96,64},{128,96},{160,128},{192,160},{224,192},{256... | collective-permute-start | bytes 393224 | tf_op jit(solution)/shard_map/ppermute | solution.py:16
  188.4 11.3 %collective-permute-start.3 = (bf16[64,1024]{1,0:T(8,128)(2,1)S(1)}, bf16[64,1024]{1,0:T(8,128)(2,1)S(1)}, u32[]{:S(2)}, u32[]{:S(2)}) collective-permute-start(bf16[64,1024]{1,0:T(8,128)(2,1)S(1)} %fusion.3), channel_id=1, source_target_pairs={{32,0},{64,32},{96,64},{128,96},{160,128},{192,160},{224,192},{256... | collective-permute-start | bytes 393224 | tf_op jit(solution)/shard_map/ppermute | solution.py:16
  211.8 11.4 %collective-permute-start.4 = (bf16[64,1024]{1,0:T(8,128)(2,1)S(1)}, bf16[64,1024]{1,0:T(8,128)(2,1)S(1)}, u32[]{:S(2)}, u32[]{:S(2)}) collective-permute-start(bf16[64,1024]{1,0:T(8,128)(2,1)S(1)} %fusion.4), channel_id=1, source_target_pairs={{32,0},{64,32},{96,64},{128,96},{160,128},{192,160},{224,192},{256... | collective-permute-start | bytes 393224 | tf_op jit(solution)/shard_map/ppermute | solution.py:16
  235.8 11.3 %collective-permute-start.5 = (bf16[64,1024]{1,0:T(8,128)(2,1)S(1)}, bf16[64,1024]{1,0:T(8,128)(2,1)S(1)}, u32[]{:S(2)}, u32[]{:S(2)}) collective-permute-start(bf16[64,1024]{1,0:T(8,128)(2,1)S(1)} %fusion.5), channel_id=1, source_target_pairs={{32,0},{64,32},{96,64},{128,96},{160,128},{192,160},{224,192},{256... | collective-permute-start | bytes 393224 | tf_op jit(solution)/shard_map/ppermute | solution.py:16
  259.3 11.3 %collective-permute-start.6 = (bf16[64,1024]{1,0:T(8,128)(2,1)S(1)}, bf16[64,1024]{1,0:T(8,128)(2,1)S(1)}, u32[]{:S(2)}, u32[]{:S(2)}) collective-permute-start(bf16[64,1024]{1,0:T(8,128)(2,1)S(1)} %fusion.6), channel_id=1, source_target_pairs={{32,0},{64,32},{96,64},{128,96},{160,128},{192,160},{224,192},{256... | collective-permute-start | bytes 393224 | tf_op jit(solution)/shard_map/ppermute | solution.py:16
  283.2 11.4 %collective-permute-start.7 = (bf16[64,1024]{1,0:T(8,128)(2,1)S(1)}, bf16[64,1024]{1,0:T(8,128)(2,1)S(1)}, u32[]{:S(2)}, u32[]{:S(2)}) collective-permute-start(bf16[64,1024]{1,0:T(8,128)(2,1)S(1)} %fusion.7), channel_id=1, source_target_pairs={{32,0},{64,32},{96,64},{128,96},{160,128},{192,160},{224,192},{256... | collective-permute-start | bytes 393224 | tf_op jit(solution)/shard_map/ppermute | solution.py:16
  306.7 11.3 %collective-permute-start.8 = (bf16[64,1024]{1,0:T(8,128)(2,1)S(1)}, bf16[64,1024]{1,0:T(8,128)(2,1)S(1)}, u32[]{:S(2)}, u32[]{:S(2)}) collective-permute-start(bf16[64,1024]{1,0:T(8,128)(2,1)S(1)} %fusion.8), channel_id=1, source_target_pairs={{32,0},{64,32},{96,64},{128,96},{160,128},{192,160},{224,192},{256... | collective-permute-start | bytes 393224 | tf_op jit(solution)/shard_map/ppermute | solution.py:16
  330.4 11.3 %collective-permute-start.9 = (bf16[64,1024]{1,0:T(8,128)(2,1)S(1)}, bf16[64,1024]{1,0:T(8,128)(2,1)S(1)}, u32[]{:S(2)}, u32[]{:S(2)}) collective-permute-start(bf16[64,1024]{1,0:T(8,128)(2,1)S(1)} %fusion.9), channel_id=1, source_target_pairs={{32,0},{64,32},{96,64},{128,96},{160,128},{192,160},{224,192},{256... | collective-permute-start | bytes 393224 | tf_op jit(solution)/shard_map/ppermute | solution.py:16
  353.8 11.3 %collective-permute-start.10 = (bf16[64,1024]{1,0:T(8,128)(2,1)S(1)}, bf16[64,1024]{1,0:T(8,128)(2,1)S(1)}, u32[]{:S(2)}, u32[]{:S(2)}) collective-permute-start(bf16[64,1024]{1,0:T(8,128)(2,1)S(1)} %fusion.10), channel_id=1, source_target_pairs={{32,0},{64,32},{96,64},{128,96},{160,128},{192,160},{224,192},{256... | collective-permute-start | bytes 393224 | tf_op jit(solution)/shard_map/ppermute | solution.py:16
  377.8 11.3 %collective-permute-start.11 = (bf16[64,1024]{1,0:T(8,128)(2,1)S(1)}, bf16[64,1024]{1,0:T(8,128)(2,1)S(1)}, u32[]{:S(2)}, u32[]{:S(2)}) collective-permute-start(bf16[64,1024]{1,0:T(8,128)(2,1)S(1)} %fusion.11), channel_id=1, source_target_pairs={{32,0},{64,32},{96,64},{128,96},{160,128},{192,160},{224,192},{256... | collective-permute-start | bytes 393224 | tf_op jit(solution)/shard_map/ppermute | solution.py:16
  401.2 11.3 %collective-permute-start.12 = (bf16[64,1024]{1,0:T(8,128)(2,1)S(1)}, bf16[64,1024]{1,0:T(8,128)(2,1)S(1)}, u32[]{:S(2)}, u32[]{:S(2)}) collective-permute-start(bf16[64,1024]{1,0:T(8,128)(2,1)S(1)} %fusion.12), channel_id=1, source_target_pairs={{32,0},{64,32},{96,64},{128,96},{160,128},{192,160},{224,192},{256... | collective-permute-start | bytes 393224 | tf_op jit(solution)/shard_map/ppermute | solution.py:16
  424.9 11.3 %collective-permute-start.13 = (bf16[64,1024]{1,0:T(8,128)(2,1)S(1)}, bf16[64,1024]{1,0:T(8,128)(2,1)S(1)}, u32[]{:S(2)}, u32[]{:S(2)}) collective-permute-start(bf16[64,1024]{1,0:T(8,128)(2,1)S(1)} %fusion.13), channel_id=1, source_target_pairs={{32,0},{64,32},{96,64},{128,96},{160,128},{192,160},{224,192},{256... | collective-permute-start | bytes 393224 | tf_op jit(solution)/shard_map/ppermute | solution.py:16
  448.3 11.3 %collective-permute-start.14 = (bf16[64,1024]{1,0:T(8,128)(2,1)S(1)}, bf16[64,1024]{1,0:T(8,128)(2,1)S(1)}, u32[]{:S(2)}, u32[]{:S(2)}) collective-permute-start(bf16[64,1024]{1,0:T(8,128)(2,1)S(1)} %fusion.14), channel_id=1, source_target_pairs={{32,0},{64,32},{96,64},{128,96},{160,128},{192,160},{224,192},{256... | collective-permute-start | bytes 393224 | tf_op jit(solution)/shard_map/ppermute | solution.py:16
  472.0 11.3 %collective-permute-start.15 = (bf16[64,1024]{1,0:T(8,128)(2,1)S(1)}, bf16[64,1024]{1,0:T(8,128)(2,1)S(1)}, u32[]{:S(2)}, u32[]{:S(2)}) collective-permute-start(bf16[64,1024]{1,0:T(8,128)(2,1)S(1)} %fusion.15), channel_id=1, source_target_pairs={{32,0},{64,32},{96,64},{128,96},{160,128},{192,160},{224,192},{256... | collective-permute-start | bytes 393224 | tf_op jit(solution)/shard_map/ppermute | solution.py:16
  499.3 5.6 %collective-permute-start.18 = (f32[16,32]{0,1:T(8,128)S(1)}, f32[16,32]{0,1:T(8,128)S(1)}, u32[]{:S(2)}, u32[]{:S(2)}) collective-permute-start(f32[16,32]{0,1:T(8,128)S(1)} %add.398), channel_id=1, source_target_pairs={{0,4},{1,5},{2,6},{3,7},{4,0},{5,1},{6,2},{7,3},{8,12},{9,13},{10,... | collective-permute-start | bytes 6152 | tf_op jit(solution)/shard_map/ppermute | solution.py:104
  504.9 6.5 %collective-permute-start.19 = (f32[16,32]{0,1:T(8,128)S(1)}, f32[16,32]{0,1:T(8,128)S(1)}, u32[]{:S(2)}, u32[]{:S(2)}) collective-permute-start(f32[16,32]{0,1:T(8,128)S(1)} %add.399), channel_id=1, source_target_pairs={{0,8},{1,9},{2,10},{3,11},{4,12},{5,13},{6,14},{7,15},{8,0},{9,1},... | collective-permute-start | bytes 6152 | tf_op jit(solution)/shard_map/ppermute | solution.py:104
  511.4 9.5 %collective-permute-start.20 = (f32[16,32]{0,1:T(8,128)S(1)}, f32[16,32]{0,1:T(8,128)S(1)}, u32[]{:S(2)}, u32[]{:S(2)}) collective-permute-start(f32[16,32]{0,1:T(8,128)S(1)} %add.400), channel_id=1, source_target_pairs={{0,16},{1,17},{2,18},{3,19},{4,20},{5,21},{6,22},{7,23},{8,24},{9,... | collective-permute-start | bytes 6152 | tf_op jit(solution)/shard_map/ppermute | solution.py:104
  521.0 5.6 %collective-permute-start.21 = (f32[16,32]{0,1:T(8,128)S(1)}, f32[16,32]{0,1:T(8,128)S(1)}, u32[]{:S(2)}, u32[]{:S(2)}) collective-permute-start(f32[16,32]{0,1:T(8,128)S(1)} %add.401), channel_id=1, source_target_pairs={{0,32},{1,33},{2,34},{3,35},{4,36},{5,37},{6,38},{7,39},{8,40},{9,... | collective-permute-start | bytes 6152 | tf_op jit(solution)/shard_map/ppermute | solution.py:104
  526.6 6.5 %collective-permute-start.22 = (f32[16,32]{0,1:T(8,128)S(1)}, f32[16,32]{0,1:T(8,128)S(1)}, u32[]{:S(2)}, u32[]{:S(2)}) collective-permute-start(f32[16,32]{0,1:T(8,128)S(1)} %add.402), channel_id=1, source_target_pairs={{0,64},{1,65},{2,66},{3,67},{4,68},{5,69},{6,70},{7,71},{8,72},{9,... | collective-permute-start | bytes 6152 | tf_op jit(solution)/shard_map/ppermute | solution.py:104
  533.1 9.5 %collective-permute-start.23 = (f32[16,32]{0,1:T(8,128)S(1)}, f32[16,32]{0,1:T(8,128)S(1)}, u32[]{:S(2)}, u32[]{:S(2)}) collective-permute-start(f32[16,32]{0,1:T(8,128)S(1)} %add.403), channel_id=1, source_target_pairs={{0,128},{1,129},{2,130},{3,131},{4,132},{5,133},{6,134},{7,135},{8... | collective-permute-start | bytes 6152 | tf_op jit(solution)/shard_map/ppermute | solution.py:104
  542.7 7.1 %collective-permute-start.24 = (f32[16,32]{0,1:T(8,128)S(1)}, f32[16,32]{0,1:T(8,128)S(1)}, u32[]{:S(2)}, u32[]{:S(2)}) collective-permute-start(f32[16,32]{0,1:T(8,128)S(1)} %add.404), channel_id=1, source_target_pairs={{0,256},{1,257},{2,258},{3,259},{4,260},{5,261},{6,262},{7,263},{8... | collective-permute-start | bytes 6152 | tf_op jit(solution)/shard_map/ppermute | solution.py:104
  (4 other events, 116.6 us)
Sparse Core Ops, SparseCore 0:
  10.1 102.2 all-gather.3

commit v5 on v4

--- a/solution.py
+++ b/solution.py
@@ -44,8 +44,7 @@
     out_proj = lax.all_gather(proj_out[0], "mp", axis=0, tiled=True)
     in_part = jnp.dot(saved_inputs[0], proj_in[0], preferred_element_type=jnp.float32)
     in_side = lax.psum(in_part, "mp")
-    in_rows = lax.dynamic_slice_in_dim(in_side, model_index * piece_rank, piece_rank, 1)
-    queries = query_panels[0]
+    queries = lax.all_gather(query_panels[0], "mp", axis=1, tiled=True)
     asked = queries.shape[0] * data_count
     queries = lax.all_gather(queries, "dp", axis=0, tiled=True)
 
@@ -73,15 +72,18 @@
             outgoing = (delta_piece.astype(jnp.float32) + back_term).astype(jnp.bfloat16)
 
         out_side = jnp.dot(grad_full, out_proj, preferred_element_type=jnp.float32)
-        in_chunk = lax.dynamic_slice_in_dim(in_rows, row_start, chunk, 0)
-        panels = jnp.einsum(
+        in_chunk = lax.dynamic_slice_in_dim(in_side, row_start, chunk, 0)
+        whole = jnp.einsum(
             "etr,etc->erc",
-            in_chunk.reshape(chunk_examples, length, piece_rank),
+            in_chunk.reshape(chunk_examples, length, low_rank),
             out_side.reshape(chunk_examples, length, low_rank),
             precision=lax.Precision.HIGHEST,
         ) / math.sqrt(length)
+        partial = jnp.dot(
+            queries, whole.reshape(chunk_examples, low_rank * low_rank).T, precision=lax.Precision.HIGHEST
+        )
+        panels = lax.dynamic_slice_in_dim(whole, model_index * piece_rank, piece_rank, 1)
         panels = panels.reshape(chunk_examples, piece_rank * low_rank)
-        partial = jnp.dot(queries, panels.T, precision=lax.Precision.HIGHEST)
         old_panels = lax.dynamic_index_in_dim(panel_store, clipped, 0, keepdims=False)
         panel_store = lax.dynamic_update_index_in_dim(
             panel_store, jnp.where(active, panels, old_panels), clipped, 0
@@ -93,22 +95,16 @@
 
     panels_here = panel_store.reshape(examples, piece_rank * low_rank)
     mine = score_store.transpose(1, 0, 2).reshape(asked, examples)
-    table = jnp.zeros((asked, data_count * examples), jnp.float32)
-    table = lax.dynamic_update_slice(table, mine, (jnp.int32(0), data_index * examples))
     score_scale = 1.0 / (low_rank * math.sqrt(section_count))
-    summed = table * score_scale
-    everyone = ("mp", "dp", "section")
-    total = section_count * data_count * model_count
+    per_dp = asked // data_count
+    owner = jnp.arange(asked) // per_dp
+    meets = partners[:, owner].T == data_index
+    scores = jnp.where(meets[:, :, None], mine[:, None, :] * score_scale, 0.0)
+    everyone = ("dp", "section")
+    total = section_count * data_count
     for level in range(total.bit_length() - 1):
         route = [(i, i ^ (1 << level)) for i in range(total)]
-        summed = summed + lax.ppermute(summed, everyone[::-1], route)
-    rounds = partners.shape[0]
-    per_dp = asked // data_count
-    owner = jnp.arange(asked) // per_dp
-    chosen = partners[:, owner].T
-    columns = chosen[:, :, None] * examples + jnp.arange(examples)[None, None, :]
-    scores = jnp.take_along_axis(summed, columns.reshape(asked, rounds * examples), axis=1)
-    scores = scores.reshape(asked, rounds, examples)
+        scores = scores + lax.ppermute(scores, everyone[::-1], route)
     return (panels_here[None], scores)
 
 

time: 563 us -> 562 us (level); the launches traced: 561 us -> 552 us
  waiting for transfers between devices: 217 us -> 205 us
  matrix products: 91.6 us -> 98.5 us
  local copies, waits for them, and re-layouts: 14.6 us -> 8.58 us
  blocking collectives: 164 us -> 170 us
    dot_general x34, matrix products: 5.34 us -> 13.2 us  [the longest x17 8.21 us: body(): jnp.dot(queries, whole.reshape(chunk_examples, low_rank * low_rank).T, pr...]
    ppermute x16, waiting for transfers between devices: 143 us -> 136 us  [from_behind(): return lax.ppermute(block, axis, route)]
    ppermute x9 -> x7, starting transfers between devices: 22.8 us -> 17.5 us  [body(): scores = scores + lax.ppermute(scores, everyone[::-1], route)]
    ppermute x9 -> x7, waiting for transfers between devices: 34.8 us -> 31.9 us  [body(): scores = scores + lax.ppermute(scores, everyone[::-1], route)]
  transfers between devices with their start and end apart: 26 -> 24, of which waited for: 26 -> 24; matrix products, arithmetic and copies ran while one was open for 2% -> 3% of each run, Pallas kernels for 0% -> 0%
where the time goes in v5:
time: 562 us; the launch traced here: 552 us
  waiting for transfers between devices  205 us (36%)
  blocking collectives  170 us (30%)
  matrix products  98.5 us (18%)
  starting transfers between devices  50.5 us (9%)
  between operations  15.5 us (3%)
  local copies, waits for them, and re-layouts  8.58 us (2%)
    ppermute x16, waiting for transfers between devices, from_behind(): return lax.ppermute(block, axis, route)  136 us
    all_gather x17, blocking collectives, body(): grad_full = lax.all_gather(grad_piece, 'mp', axis=1, tiled=True)  114 us
    dot_general x16, matrix products, body(): back_term = jnp.dot(grad_full, w_cols, preferred_element_type=jnp.float32)  79.3 us
    all_gather x1, waiting for transfers between devices, body(): w_cols = lax.all_gather(weights[0].T, 'dp', axis=0, tiled=True)  36.5 us
    ppermute x16, starting transfers between devices, from_behind(): return lax.ppermute(block, axis, route)  33 us
    ppermute x7, waiting for transfers between devices, body(): scores = scores + lax.ppermute(scores, everyone[::-1], route)  31.9 us
    all_gather x1, blocking collectives, body(): queries = lax.all_gather(queries, 'dp', axis=0, tiled=True)  31.8 us
    ppermute x7, starting transfers between devices, body(): scores = scores + lax.ppermute(scores, everyone[::-1], route)  17.5 us
  transfers between devices with their start and end apart: 24, of which 24 were waited for; matrix products, arithmetic and copies ran while one was open for 3% of the time, Pallas kernels for 0%

profile of v5, /device:TPU:56, one launch (start us, length us, event | category | flops | bytes accessed | tf_op | source)
XLA Modules:
  0.0 551.8 jit_solution(10130247364867890146)
XLA Ops:
  10.9 11.4 %psum.7 = f32[128,64]{0,1:T(8,128)S(1)} all-reduce(f32[128,64]{0,1:T(8,128)S(1)} %fusion.138), channel_id=1, replica_groups=mesh['section'=16,'dp'=8,'mp'=4] {'mp'}, use_global_device_ids=true, to_apply=%region_0.0 | all-reduce | flops 8192 | bytes 65536 | tf_op jit(solution)/shard_map/psum | solution.py:46
  31.3 7.5 %all-gather = bf16[1,4096,64]{1,2,0:T(8,128)(2,1)S(1)} all-gather(bf16[1,1024,64]{1,2,0:T(8,128)(2,1)} %param.13), channel_id=2, replica_groups=mesh['section'=16,'dp'=8,'mp'=4] {'mp'}, dimensions={1}, use_global_device_ids=true | all-gather | bytes 655360 | tf_op jit(solution)/shard_map/all_gather | solution.py:44
  45.4 31.8 %all-gather.2 = f32[1,16,4096]{2,0,1:T(1,128)S(1)} all-gather(f32[1,2,4096]{2,0,1:T(1,128)S(1)} %all-gather.1), channel_id=4, replica_groups=mesh['section'=16,'dp'=8,'mp'=4] {'dp'}, dimensions={1}, use_global_device_ids=true | all-gather | bytes 294912 | tf_op jit(solution)/shard_map/all_gather | solution.py:49
  77.7 36.5 %all-gather.5.cloned.1.call-done = bf16[4096,1024]{1,0:T(8,128)(2,1)} async-done(((bf16[512,1024]{1,0:T(8,128)(2,1)}), bf16[4096,1024]{1,0:T(8,128)(2,1)}) %all-gather.5.cloned.1.call-update) | async-done | bytes 8388624 | tf_op jit(solution)/shard_map/all_gather | solution.py:41
  130.0 7.2 %all_gather.66 = bf16[64,4096]{1,0:T(8,128)(2,1)S(1)} all-gather(bf16[64,1024]{1,0:T(8,128)(2,1)S(1)} %fusion.106), channel_id=1, replica_groups=mesh['section'=16,'dp'=8,'mp'=4] {'mp'}, dimensions={1}, use_global_device_ids=true | all-gather | bytes 655360 | tf_op jit(solution)/shard_map/all_gather | solution.py:69
  145.3 8.9 %collective-permute-done.1 = bf16[64,1024]{1,0:T(8,128)(2,1)S(1)} collective-permute-done((bf16[64,1024]{1,0:T(8,128)(2,1)S(1)}, bf16[64,1024]{1,0:T(8,128)(2,1)S(1)}, u32[]{:S(2)}, u32[]{:S(2)}) %collective-permute-start.1) | collective-permute-done | bytes 131104 | tf_op jit(solution)/shard_map/ppermute | solution.py:16
  169.1 8.6 %collective-permute-done.2 = bf16[64,1024]{1,0:T(8,128)(2,1)S(1)} collective-permute-done((bf16[64,1024]{1,0:T(8,128)(2,1)S(1)}, bf16[64,1024]{1,0:T(8,128)(2,1)S(1)}, u32[]{:S(2)}, u32[]{:S(2)}) %collective-permute-start.2) | collective-permute-done | bytes 131104 | tf_op jit(solution)/shard_map/ppermute | solution.py:16
  193.2 8.4 %collective-permute-done.3 = bf16[64,1024]{1,0:T(8,128)(2,1)S(1)} collective-permute-done((bf16[64,1024]{1,0:T(8,128)(2,1)S(1)}, bf16[64,1024]{1,0:T(8,128)(2,1)S(1)}, u32[]{:S(2)}, u32[]{:S(2)}) %collective-permute-start.3) | collective-permute-done | bytes 131104 | tf_op jit(solution)/shard_map/ppermute | solution.py:16
  216.4 8.6 %collective-permute-done.4 = bf16[64,1024]{1,0:T(8,128)(2,1)S(1)} collective-permute-done((bf16[64,1024]{1,0:T(8,128)(2,1)S(1)}, bf16[64,1024]{1,0:T(8,128)(2,1)S(1)}, u32[]{:S(2)}, u32[]{:S(2)}) %collective-permute-start.4) | collective-permute-done | bytes 131104 | tf_op jit(solution)/shard_map/ppermute | solution.py:16
  240.0 8.8 %collective-permute-done.5 = bf16[64,1024]{1,0:T(8,128)(2,1)S(1)} collective-permute-done((bf16[64,1024]{1,0:T(8,128)(2,1)S(1)}, bf16[64,1024]{1,0:T(8,128)(2,1)S(1)}, u32[]{:S(2)}, u32[]{:S(2)}) %collective-permute-start.5) | collective-permute-done | bytes 131104 | tf_op jit(solution)/shard_map/ppermute | solution.py:16
  263.8 8.7 %collective-permute-done.6 = bf16[64,1024]{1,0:T(8,128)(2,1)S(1)} collective-permute-done((bf16[64,1024]{1,0:T(8,128)(2,1)S(1)}, bf16[64,1024]{1,0:T(8,128)(2,1)S(1)}, u32[]{:S(2)}, u32[]{:S(2)}) %collective-permute-start.6) | collective-permute-done | bytes 131104 | tf_op jit(solution)/shard_map/ppermute | solution.py:16
  272.5 6.9 %all_gather.72 = bf16[64,4096]{1,0:T(8,128)(2,1)S(1)} all-gather(bf16[64,1024]{1,0:T(8,128)(2,1)S(1)} %fusion.112), channel_id=1, replica_groups=mesh['section'=16,'dp'=8,'mp'=4] {'mp'}, dimensions={1}, use_global_device_ids=true | all-gather | bytes 655360 | tf_op jit(solution)/shard_map/all_gather | solution.py:69
  287.5 8.9 %collective-permute-done.7 = bf16[64,1024]{1,0:T(8,128)(2,1)S(1)} collective-permute-done((bf16[64,1024]{1,0:T(8,128)(2,1)S(1)}, bf16[64,1024]{1,0:T(8,128)(2,1)S(1)}, u32[]{:S(2)}, u32[]{:S(2)}) %collective-permute-start.7) | collective-permute-done | bytes 131104 | tf_op jit(solution)/shard_map/ppermute | solution.py:16
  311.5 8.4 %collective-permute-done.8 = bf16[64,1024]{1,0:T(8,128)(2,1)S(1)} collective-permute-done((bf16[64,1024]{1,0:T(8,128)(2,1)S(1)}, bf16[64,1024]{1,0:T(8,128)(2,1)S(1)}, u32[]{:S(2)}, u32[]{:S(2)}) %collective-permute-start.8) | collective-permute-done | bytes 131104 | tf_op jit(solution)/shard_map/ppermute | solution.py:16
  334.9 8.8 %collective-permute-done.9 = bf16[64,1024]{1,0:T(8,128)(2,1)S(1)} collective-permute-done((bf16[64,1024]{1,0:T(8,128)(2,1)S(1)}, bf16[64,1024]{1,0:T(8,128)(2,1)S(1)}, u32[]{:S(2)}, u32[]{:S(2)}) %collective-permute-start.9) | collective-permute-done | bytes 131104 | tf_op jit(solution)/shard_map/ppermute | solution.py:16
  358.7 8.6 %collective-permute-done.10 = bf16[64,1024]{1,0:T(8,128)(2,1)S(1)} collective-permute-done((bf16[64,1024]{1,0:T(8,128)(2,1)S(1)}, bf16[64,1024]{1,0:T(8,128)(2,1)S(1)}, u32[]{:S(2)}, u32[]{:S(2)}) %collective-permute-start.10) | collective-permute-done | bytes 131104 | tf_op jit(solution)/shard_map/ppermute | solution.py:16
  367.3 6.9 %all_gather.76 = bf16[64,4096]{1,0:T(8,128)(2,1)S(1)} all-gather(bf16[64,1024]{1,0:T(8,128)(2,1)S(1)} %fusion.116), channel_id=1, replica_groups=mesh['section'=16,'dp'=8,'mp'=4] {'mp'}, dimensions={1}, use_global_device_ids=true | all-gather | bytes 655360 | tf_op jit(solution)/shard_map/all_gather | solution.py:69
  382.3 8.8 %collective-permute-done.11 = bf16[64,1024]{1,0:T(8,128)(2,1)S(1)} collective-permute-done((bf16[64,1024]{1,0:T(8,128)(2,1)S(1)}, bf16[64,1024]{1,0:T(8,128)(2,1)S(1)}, u32[]{:S(2)}, u32[]{:S(2)}) %collective-permute-start.11) | collective-permute-done | bytes 131104 | tf_op jit(solution)/shard_map/ppermute | solution.py:16
  406.0 8.6 %collective-permute-done.12 = bf16[64,1024]{1,0:T(8,128)(2,1)S(1)} collective-permute-done((bf16[64,1024]{1,0:T(8,128)(2,1)S(1)}, bf16[64,1024]{1,0:T(8,128)(2,1)S(1)}, u32[]{:S(2)}, u32[]{:S(2)}) %collective-permute-start.12) | collective-permute-done | bytes 131104 | tf_op jit(solution)/shard_map/ppermute | solution.py:16
  429.8 8.6 %collective-permute-done.13 = bf16[64,1024]{1,0:T(8,128)(2,1)S(1)} collective-permute-done((bf16[64,1024]{1,0:T(8,128)(2,1)S(1)}, bf16[64,1024]{1,0:T(8,128)(2,1)S(1)}, u32[]{:S(2)}, u32[]{:S(2)}) %collective-permute-start.13) | collective-permute-done | bytes 131104 | tf_op jit(solution)/shard_map/ppermute | solution.py:16
  453.1 8.8 %collective-permute-done.14 = bf16[64,1024]{1,0:T(8,128)(2,1)S(1)} collective-permute-done((bf16[64,1024]{1,0:T(8,128)(2,1)S(1)}, bf16[64,1024]{1,0:T(8,128)(2,1)S(1)}, u32[]{:S(2)}, u32[]{:S(2)}) %collective-permute-start.14) | collective-permute-done | bytes 131104 | tf_op jit(solution)/shard_map/ppermute | solution.py:16
  462.0 6.9 %all_gather.80 = bf16[64,4096]{1,0:T(8,128)(2,1)S(1)} all-gather(bf16[64,1024]{1,0:T(8,128)(2,1)S(1)} %fusion.120), channel_id=1, replica_groups=mesh['section'=16,'dp'=8,'mp'=4] {'mp'}, dimensions={1}, use_global_device_ids=true | all-gather | bytes 655360 | tf_op jit(solution)/shard_map/all_gather | solution.py:69
  476.9 8.8 %collective-permute-done.15 = bf16[64,1024]{1,0:T(8,128)(2,1)S(1)} collective-permute-done((bf16[64,1024]{1,0:T(8,128)(2,1)S(1)}, bf16[64,1024]{1,0:T(8,128)(2,1)S(1)}, u32[]{:S(2)}, u32[]{:S(2)}) %collective-permute-start.15) | collective-permute-done | bytes 131104 | tf_op jit(solution)/shard_map/ppermute | solution.py:16
  529.5 7.5 %collective-permute-done.21 = f32[16,8,4]{0,2,1:T(4,128)S(1)} collective-permute-done((f32[16,8,4]{0,2,1:T(4,128)S(1)}, f32[16,8,4]{0,2,1:T(4,128)S(1)}, u32[]{:S(2)}, u32[]{:S(2)}) %collective-permute-start.21) | collective-permute-done | bytes 2080 | tf_op jit(solution)/shard_map/ppermute | solution.py:107
  (254 shorter events, 283.0 us)
Async XLA Ops:
  7.2 107.0 %all-gather.5.cloned.1.call-start = ((), (), s32[]{:S(2)}) async-start(), calls=%async_computation | async-start | bytes 9437184 | tf_op jit(solution)/shard_map/all_gather | solution.py:41
  119.2 10.7 %collective-permute-start = (bf16[64,1024]{1,0:T(8,128)(2,1)S(1)}, bf16[64,1024]{1,0:T(8,128)(2,1)S(1)}, u32[]{:S(2)}, u32[]{:S(2)}) collective-permute-start(bf16[64,1024]{1,0:T(8,128)(2,1)S(1)} %fusion), channel_id=1, source_target_pairs={{32,0},{64,32},{96,64},{128,96},{160,128},{192,160},{224,192},{256... | collective-permute-start | bytes 393224 | tf_op jit(solution)/shard_map/ppermute | solution.py:16
  142.8 11.4 %collective-permute-start.1 = (bf16[64,1024]{1,0:T(8,128)(2,1)S(1)}, bf16[64,1024]{1,0:T(8,128)(2,1)S(1)}, u32[]{:S(2)}, u32[]{:S(2)}) collective-permute-start(bf16[64,1024]{1,0:T(8,128)(2,1)S(1)} %fusion.1), channel_id=1, source_target_pairs={{32,0},{64,32},{96,64},{128,96},{160,128},{192,160},{224,192},{256... | collective-permute-start | bytes 393224 | tf_op jit(solution)/shard_map/ppermute | solution.py:16
  166.4 11.3 %collective-permute-start.2 = (bf16[64,1024]{1,0:T(8,128)(2,1)S(1)}, bf16[64,1024]{1,0:T(8,128)(2,1)S(1)}, u32[]{:S(2)}, u32[]{:S(2)}) collective-permute-start(bf16[64,1024]{1,0:T(8,128)(2,1)S(1)} %fusion.2), channel_id=1, source_target_pairs={{32,0},{64,32},{96,64},{128,96},{160,128},{192,160},{224,192},{256... | collective-permute-start | bytes 393224 | tf_op jit(solution)/shard_map/ppermute | solution.py:16
  190.3 11.3 %collective-permute-start.3 = (bf16[64,1024]{1,0:T(8,128)(2,1)S(1)}, bf16[64,1024]{1,0:T(8,128)(2,1)S(1)}, u32[]{:S(2)}, u32[]{:S(2)}) collective-permute-start(bf16[64,1024]{1,0:T(8,128)(2,1)S(1)} %fusion.3), channel_id=1, source_target_pairs={{32,0},{64,32},{96,64},{128,96},{160,128},{192,160},{224,192},{256... | collective-permute-start | bytes 393224 | tf_op jit(solution)/shard_map/ppermute | solution.py:16
  213.8 11.3 %collective-permute-start.4 = (bf16[64,1024]{1,0:T(8,128)(2,1)S(1)}, bf16[64,1024]{1,0:T(8,128)(2,1)S(1)}, u32[]{:S(2)}, u32[]{:S(2)}) collective-permute-start(bf16[64,1024]{1,0:T(8,128)(2,1)S(1)} %fusion.4), channel_id=1, source_target_pairs={{32,0},{64,32},{96,64},{128,96},{160,128},{192,160},{224,192},{256... | collective-permute-start | bytes 393224 | tf_op jit(solution)/shard_map/ppermute | solution.py:16
  237.6 11.3 %collective-permute-start.5 = (bf16[64,1024]{1,0:T(8,128)(2,1)S(1)}, bf16[64,1024]{1,0:T(8,128)(2,1)S(1)}, u32[]{:S(2)}, u32[]{:S(2)}) collective-permute-start(bf16[64,1024]{1,0:T(8,128)(2,1)S(1)} %fusion.5), channel_id=1, source_target_pairs={{32,0},{64,32},{96,64},{128,96},{160,128},{192,160},{224,192},{256... | collective-permute-start | bytes 393224 | tf_op jit(solution)/shard_map/ppermute | solution.py:16
  261.1 11.3 %collective-permute-start.6 = (bf16[64,1024]{1,0:T(8,128)(2,1)S(1)}, bf16[64,1024]{1,0:T(8,128)(2,1)S(1)}, u32[]{:S(2)}, u32[]{:S(2)}) collective-permute-start(bf16[64,1024]{1,0:T(8,128)(2,1)S(1)} %fusion.6), channel_id=1, source_target_pairs={{32,0},{64,32},{96,64},{128,96},{160,128},{192,160},{224,192},{256... | collective-permute-start | bytes 393224 | tf_op jit(solution)/shard_map/ppermute | solution.py:16
  285.1 11.4 %collective-permute-start.7 = (bf16[64,1024]{1,0:T(8,128)(2,1)S(1)}, bf16[64,1024]{1,0:T(8,128)(2,1)S(1)}, u32[]{:S(2)}, u32[]{:S(2)}) collective-permute-start(bf16[64,1024]{1,0:T(8,128)(2,1)S(1)} %fusion.7), channel_id=1, source_target_pairs={{32,0},{64,32},{96,64},{128,96},{160,128},{192,160},{224,192},{256... | collective-permute-start | bytes 393224 | tf_op jit(solution)/shard_map/ppermute | solution.py:16
  308.7 11.3 %collective-permute-start.8 = (bf16[64,1024]{1,0:T(8,128)(2,1)S(1)}, bf16[64,1024]{1,0:T(8,128)(2,1)S(1)}, u32[]{:S(2)}, u32[]{:S(2)}) collective-permute-start(bf16[64,1024]{1,0:T(8,128)(2,1)S(1)} %fusion.8), channel_id=1, source_target_pairs={{32,0},{64,32},{96,64},{128,96},{160,128},{192,160},{224,192},{256... | collective-permute-start | bytes 393224 | tf_op jit(solution)/shard_map/ppermute | solution.py:16
  332.5 11.3 %collective-permute-start.9 = (bf16[64,1024]{1,0:T(8,128)(2,1)S(1)}, bf16[64,1024]{1,0:T(8,128)(2,1)S(1)}, u32[]{:S(2)}, u32[]{:S(2)}) collective-permute-start(bf16[64,1024]{1,0:T(8,128)(2,1)S(1)} %fusion.9), channel_id=1, source_target_pairs={{32,0},{64,32},{96,64},{128,96},{160,128},{192,160},{224,192},{256... | collective-permute-start | bytes 393224 | tf_op jit(solution)/shard_map/ppermute | solution.py:16
  356.0 11.3 %collective-permute-start.10 = (bf16[64,1024]{1,0:T(8,128)(2,1)S(1)}, bf16[64,1024]{1,0:T(8,128)(2,1)S(1)}, u32[]{:S(2)}, u32[]{:S(2)}) collective-permute-start(bf16[64,1024]{1,0:T(8,128)(2,1)S(1)} %fusion.10), channel_id=1, source_target_pairs={{32,0},{64,32},{96,64},{128,96},{160,128},{192,160},{224,192},{256... | collective-permute-start | bytes 393224 | tf_op jit(solution)/shard_map/ppermute | solution.py:16
  379.9 11.3 %collective-permute-start.11 = (bf16[64,1024]{1,0:T(8,128)(2,1)S(1)}, bf16[64,1024]{1,0:T(8,128)(2,1)S(1)}, u32[]{:S(2)}, u32[]{:S(2)}) collective-permute-start(bf16[64,1024]{1,0:T(8,128)(2,1)S(1)} %fusion.11), channel_id=1, source_target_pairs={{32,0},{64,32},{96,64},{128,96},{160,128},{192,160},{224,192},{256... | collective-permute-start | bytes 393224 | tf_op jit(solution)/shard_map/ppermute | solution.py:16
  403.3 11.3 %collective-permute-start.12 = (bf16[64,1024]{1,0:T(8,128)(2,1)S(1)}, bf16[64,1024]{1,0:T(8,128)(2,1)S(1)}, u32[]{:S(2)}, u32[]{:S(2)}) collective-permute-start(bf16[64,1024]{1,0:T(8,128)(2,1)S(1)} %fusion.12), channel_id=1, source_target_pairs={{32,0},{64,32},{96,64},{128,96},{160,128},{192,160},{224,192},{256... | collective-permute-start | bytes 393224 | tf_op jit(solution)/shard_map/ppermute | solution.py:16
  427.2 11.3 %collective-permute-start.13 = (bf16[64,1024]{1,0:T(8,128)(2,1)S(1)}, bf16[64,1024]{1,0:T(8,128)(2,1)S(1)}, u32[]{:S(2)}, u32[]{:S(2)}) collective-permute-start(bf16[64,1024]{1,0:T(8,128)(2,1)S(1)} %fusion.13), channel_id=1, source_target_pairs={{32,0},{64,32},{96,64},{128,96},{160,128},{192,160},{224,192},{256... | collective-permute-start | bytes 393224 | tf_op jit(solution)/shard_map/ppermute | solution.py:16
  450.7 11.3 %collective-permute-start.14 = (bf16[64,1024]{1,0:T(8,128)(2,1)S(1)}, bf16[64,1024]{1,0:T(8,128)(2,1)S(1)}, u32[]{:S(2)}, u32[]{:S(2)}) collective-permute-start(bf16[64,1024]{1,0:T(8,128)(2,1)S(1)} %fusion.14), channel_id=1, source_target_pairs={{32,0},{64,32},{96,64},{128,96},{160,128},{192,160},{224,192},{256... | collective-permute-start | bytes 393224 | tf_op jit(solution)/shard_map/ppermute | solution.py:16
  474.5 11.3 %collective-permute-start.15 = (bf16[64,1024]{1,0:T(8,128)(2,1)S(1)}, bf16[64,1024]{1,0:T(8,128)(2,1)S(1)}, u32[]{:S(2)}, u32[]{:S(2)}) collective-permute-start(bf16[64,1024]{1,0:T(8,128)(2,1)S(1)} %fusion.15), channel_id=1, source_target_pairs={{32,0},{64,32},{96,64},{128,96},{160,128},{192,160},{224,192},{256... | collective-permute-start | bytes 393224 | tf_op jit(solution)/shard_map/ppermute | solution.py:16
  493.6 5.6 %collective-permute-start.16 = (f32[16,8,4]{0,2,1:T(4,128)S(1)}, f32[16,8,4]{0,2,1:T(4,128)S(1)}, u32[]{:S(2)}, u32[]{:S(2)}) collective-permute-start(f32[16,8,4]{0,2,1:T(4,128)S(1)} %broadcast_select_fusion), channel_id=1, source_target_pairs={{0,4},{4,0},{8,12},{12,8},{16,20},{20,16},{24,28},{28,24},{32,36},... | collective-permute-start | bytes 6152 | tf_op jit(solution)/shard_map/ppermute | solution.py:107
  499.2 6.5 %collective-permute-start.17 = (f32[16,8,4]{0,2,1:T(4,128)S(1)}, f32[16,8,4]{0,2,1:T(4,128)S(1)}, u32[]{:S(2)}, u32[]{:S(2)}) collective-permute-start(f32[16,8,4]{0,2,1:T(4,128)S(1)} %fusion.191), channel_id=1, source_target_pairs={{0,8},{4,12},{8,0},{12,4},{16,24},{20,28},{24,16},{28,20},{32,40},... | collective-permute-start | bytes 6152 | tf_op jit(solution)/shard_map/ppermute | solution.py:107
  505.8 9.5 %collective-permute-start.18 = (f32[16,8,4]{0,2,1:T(4,128)S(1)}, f32[16,8,4]{0,2,1:T(4,128)S(1)}, u32[]{:S(2)}, u32[]{:S(2)}) collective-permute-start(f32[16,8,4]{0,2,1:T(4,128)S(1)} %fusion.293), channel_id=1, source_target_pairs={{0,16},{4,20},{8,24},{12,28},{16,0},{20,4},{24,8},{28,12},{32,48},... | collective-permute-start | bytes 6152 | tf_op jit(solution)/shard_map/ppermute | solution.py:107
  515.3 5.6 %collective-permute-start.19 = (f32[16,8,4]{0,2,1:T(4,128)S(1)}, f32[16,8,4]{0,2,1:T(4,128)S(1)}, u32[]{:S(2)}, u32[]{:S(2)}) collective-permute-start(f32[16,8,4]{0,2,1:T(4,128)S(1)} %add.310), channel_id=1, source_target_pairs={{0,32},{4,36},{8,40},{12,44},{16,48},{20,52},{24,56},{28,60},{32,0... | collective-permute-start | bytes 6152 | tf_op jit(solution)/shard_map/ppermute | solution.py:107
  521.0 6.5 %collective-permute-start.20 = (f32[16,8,4]{0,2,1:T(4,128)S(1)}, f32[16,8,4]{0,2,1:T(4,128)S(1)}, u32[]{:S(2)}, u32[]{:S(2)}) collective-permute-start(f32[16,8,4]{0,2,1:T(4,128)S(1)} %add.311), channel_id=1, source_target_pairs={{0,64},{4,68},{8,72},{12,76},{16,80},{20,84},{24,88},{28,92},{32,9... | collective-permute-start | bytes 6152 | tf_op jit(solution)/shard_map/ppermute | solution.py:107
  527.5 9.5 %collective-permute-start.21 = (f32[16,8,4]{0,2,1:T(4,128)S(1)}, f32[16,8,4]{0,2,1:T(4,128)S(1)}, u32[]{:S(2)}, u32[]{:S(2)}) collective-permute-start(f32[16,8,4]{0,2,1:T(4,128)S(1)} %add.312), channel_id=1, source_target_pairs={{0,128},{4,132},{8,136},{12,140},{16,144},{20,148},{24,152},{28,15... | collective-permute-start | bytes 6152 | tf_op jit(solution)/shard_map/ppermute | solution.py:107
  537.0 7.1 %collective-permute-start.22 = (f32[16,8,4]{0,2,1:T(4,128)S(1)}, f32[16,8,4]{0,2,1:T(4,128)S(1)}, u32[]{:S(2)}, u32[]{:S(2)}) collective-permute-start(f32[16,8,4]{0,2,1:T(4,128)S(1)} %add.313), channel_id=1, source_target_pairs={{0,256},{4,260},{8,264},{12,268},{16,272},{20,276},{24,280},{28,28... | collective-permute-start | bytes 6152 | tf_op jit(solution)/shard_map/ppermute | solution.py:107
  (4 other events, 174.2 us)
Sparse Core Ops, SparseCore 0:
  10.1 104.0 all-gather.4

commit v6 on v5

--- a/solution.py
+++ b/solution.py
@@ -8,12 +8,6 @@
 
 LEN = 32
 CHUNKS = 2
-
-
-def from_behind(block, axis, distance):
-    devices = range(lax.axis_size(axis))
-    route = [(i - distance, i) for i in devices if i - distance in devices]
-    return lax.ppermute(block, axis, route)
 
 
 def silu_slope(pre_state):
@@ -60,7 +54,11 @@
         row_start = clipped * chunk
         top_rows = lax.dynamic_slice_in_dim(cotangent, row_start, chunk, 0)
         if turn > 0:
-            received = from_behind(outgoing, "section", -1)
+            senders = [
+                k for k in range(top_section + 1 - turn, top_section + 1 - turn + CHUNKS)
+                if 1 <= k <= top_section
+            ]
+            received = lax.ppermute(outgoing, "section", [(k, k - 1) for k in senders])
             delta_piece = jnp.where(is_top, top_rows, received)
         else:
             delta_piece = top_rows
@@ -100,11 +98,12 @@
     owner = jnp.arange(asked) // per_dp
     meets = partners[:, owner].T == data_index
     scores = jnp.where(meets[:, :, None], mine[:, None, :] * score_scale, 0.0)
-    everyone = ("dp", "section")
     total = section_count * data_count
-    for level in range(total.bit_length() - 1):
+    levels = list(range(total.bit_length() - 1))
+    dp_levels = data_count.bit_length() - 1
+    for level in levels[dp_levels:] + levels[:dp_levels]:
         route = [(i, i ^ (1 << level)) for i in range(total)]
-        scores = scores + lax.ppermute(scores, everyone[::-1], route)
+        scores = scores + lax.ppermute(scores, ("section", "dp"), route)
     return (panels_here[None], scores)
 
 

time: 562 us -> 500 us (0.89)
  the two profiles are of different devices: /device:TPU:56 before, /device:TPU:2 now
where the time goes in v6:
time: 500 us; the launch traced here: 490 us
  blocking collectives  177 us (35%)
  waiting for transfers between devices  156 us (31%)
  matrix products  98.5 us (20%)
  starting transfers between devices  30.3 us (6%)
  between operations  15.7 us (3%)
  local copies, waits for them, and re-layouts  8.57 us (2%)
    all_gather x17, blocking collectives, body(): grad_full = lax.all_gather(grad_piece, 'mp', axis=1, tiled=True)  123 us
    ppermute x16, waiting for transfers between devices, body(): received = lax.ppermute(outgoing, 'section', [(k, k - 1) for k in senders])  86.7 us
    dot_general x16, matrix products, body(): back_term = jnp.dot(grad_full, w_cols, preferred_element_type=jnp.float32)  79.3 us
    all_gather x1, waiting for transfers between devices, body(): w_cols = lax.all_gather(weights[0].T, 'dp', axis=0, tiled=True)  37.5 us
    ppermute x7, waiting for transfers between devices, body(): scores = scores + lax.ppermute(scores, ('section', 'dp'), route)  31.9 us
    all_gather x1, blocking collectives, body(): queries = lax.all_gather(queries, 'dp', axis=0, tiled=True)  27.6 us
    ppermute x7, starting transfers between devices, body(): scores = scores + lax.ppermute(scores, ('section', 'dp'), route)  17.4 us
    psum x1, blocking collectives, body(): in_side = lax.psum(in_part, 'mp')  13.9 us
  transfers between devices with their start and end apart: 24, of which 10 were waited for; matrix products, arithmetic and copies ran while one was open for 3% of the time, Pallas kernels for 0%

profile of v6, /device:TPU:2, one launch (start us, length us, event | category | flops | bytes accessed | tf_op | source)
XLA Modules:
  0.0 490.3 jit_solution(15573031993672210974)
XLA Ops:
  10.9 13.9 %psum.7 = f32[128,64]{0,1:T(8,128)S(1)} all-reduce(f32[128,64]{0,1:T(8,128)S(1)} %fusion.138), channel_id=1, replica_groups=mesh['section'=16,'dp'=8,'mp'=4] {'mp'}, use_global_device_ids=true, to_apply=%region_0.0 | all-reduce | flops 8192 | bytes 65536 | tf_op jit(solution)/shard_map/psum | solution.py:40
  27.3 7.9 %all_gather.63 = bf16[64,4096]{1,0:T(8,128)(2,1)S(1)} all-gather(bf16[64,1024]{1,0:T(8,128)(2,1)S(1)} %fusion.105), channel_id=1, replica_groups=mesh['section'=16,'dp'=8,'mp'=4] {'mp'}, dimensions={1}, use_global_device_ids=true | all-gather | bytes 655360 | tf_op jit(solution)/shard_map/all_gather | solution.py:67
  35.2 7.5 %all-gather = bf16[1,4096,64]{1,2,0:T(8,128)(2,1)S(1)} all-gather(bf16[1,1024,64]{1,2,0:T(8,128)(2,1)} %param.13), channel_id=2, replica_groups=mesh['section'=16,'dp'=8,'mp'=4] {'mp'}, dimensions={1}, use_global_device_ids=true | all-gather | bytes 655360 | tf_op jit(solution)/shard_map/all_gather | solution.py:38
  49.3 27.6 %all-gather.2 = f32[1,16,4096]{2,0,1:T(1,128)S(1)} all-gather(f32[1,2,4096]{2,0,1:T(1,128)S(1)} %all-gather.1), channel_id=4, replica_groups=mesh['section'=16,'dp'=8,'mp'=4] {'dp'}, dimensions={1}, use_global_device_ids=true | all-gather | bytes 294912 | tf_op jit(solution)/shard_map/all_gather | solution.py:43
  77.4 37.5 %all-gather.5.cloned.1.call-done = bf16[4096,1024]{1,0:T(8,128)(2,1)} async-done(((bf16[512,1024]{1,0:T(8,128)(2,1)}), bf16[4096,1024]{1,0:T(8,128)(2,1)}) %all-gather.5.cloned.1.call-update) | async-done | bytes 8388624 | tf_op jit(solution)/shard_map/all_gather | solution.py:35
  122.2 6.8 %all_gather.66 = bf16[64,4096]{1,0:T(8,128)(2,1)S(1)} all-gather(bf16[64,1024]{1,0:T(8,128)(2,1)S(1)} %fusion.106), channel_id=1, replica_groups=mesh['section'=16,'dp'=8,'mp'=4] {'mp'}, dimensions={1}, use_global_device_ids=true | all-gather | bytes 655360 | tf_op jit(solution)/shard_map/all_gather | solution.py:67
  135.8 7.3 %all_gather.67 = bf16[64,4096]{1,0:T(8,128)(2,1)S(1)} all-gather(bf16[64,1024]{1,0:T(8,128)(2,1)S(1)} %fusion.107), channel_id=1, replica_groups=mesh['section'=16,'dp'=8,'mp'=4] {'mp'}, dimensions={1}, use_global_device_ids=true | all-gather | bytes 655360 | tf_op jit(solution)/shard_map/all_gather | solution.py:67
  150.3 7.3 %all_gather.68 = bf16[64,4096]{1,0:T(8,128)(2,1)S(1)} all-gather(bf16[64,1024]{1,0:T(8,128)(2,1)S(1)} %fusion.108), channel_id=1, replica_groups=mesh['section'=16,'dp'=8,'mp'=4] {'mp'}, dimensions={1}, use_global_device_ids=true | all-gather | bytes 655360 | tf_op jit(solution)/shard_map/all_gather | solution.py:67
  164.9 7.3 %all_gather.69 = bf16[64,4096]{1,0:T(8,128)(2,1)S(1)} all-gather(bf16[64,1024]{1,0:T(8,128)(2,1)S(1)} %fusion.109), channel_id=1, replica_groups=mesh['section'=16,'dp'=8,'mp'=4] {'mp'}, dimensions={1}, use_global_device_ids=true | all-gather | bytes 655360 | tf_op jit(solution)/shard_map/all_gather | solution.py:67
  179.4 7.3 %all_gather.70 = bf16[64,4096]{1,0:T(8,128)(2,1)S(1)} all-gather(bf16[64,1024]{1,0:T(8,128)(2,1)S(1)} %fusion.110), channel_id=1, replica_groups=mesh['section'=16,'dp'=8,'mp'=4] {'mp'}, dimensions={1}, use_global_device_ids=true | all-gather | bytes 655360 | tf_op jit(solution)/shard_map/all_gather | solution.py:67
  193.6 7.3 %all_gather.71 = bf16[64,4096]{1,0:T(8,128)(2,1)S(1)} all-gather(bf16[64,1024]{1,0:T(8,128)(2,1)S(1)} %fusion.111), channel_id=1, replica_groups=mesh['section'=16,'dp'=8,'mp'=4] {'mp'}, dimensions={1}, use_global_device_ids=true | all-gather | bytes 655360 | tf_op jit(solution)/shard_map/all_gather | solution.py:67
  208.0 7.3 %all_gather.72 = bf16[64,4096]{1,0:T(8,128)(2,1)S(1)} all-gather(bf16[64,1024]{1,0:T(8,128)(2,1)S(1)} %fusion.112), channel_id=1, replica_groups=mesh['section'=16,'dp'=8,'mp'=4] {'mp'}, dimensions={1}, use_global_device_ids=true | all-gather | bytes 655360 | tf_op jit(solution)/shard_map/all_gather | solution.py:67
  222.2 7.3 %all_gather.73 = bf16[64,4096]{1,0:T(8,128)(2,1)S(1)} all-gather(bf16[64,1024]{1,0:T(8,128)(2,1)S(1)} %fusion.113), channel_id=1, replica_groups=mesh['section'=16,'dp'=8,'mp'=4] {'mp'}, dimensions={1}, use_global_device_ids=true | all-gather | bytes 655360 | tf_op jit(solution)/shard_map/all_gather | solution.py:67
  236.8 7.3 %all_gather.74 = bf16[64,4096]{1,0:T(8,128)(2,1)S(1)} all-gather(bf16[64,1024]{1,0:T(8,128)(2,1)S(1)} %fusion.114), channel_id=1, replica_groups=mesh['section'=16,'dp'=8,'mp'=4] {'mp'}, dimensions={1}, use_global_device_ids=true | all-gather | bytes 655360 | tf_op jit(solution)/shard_map/all_gather | solution.py:67
  251.0 7.3 %all_gather.75 = bf16[64,4096]{1,0:T(8,128)(2,1)S(1)} all-gather(bf16[64,1024]{1,0:T(8,128)(2,1)S(1)} %fusion.115), channel_id=1, replica_groups=mesh['section'=16,'dp'=8,'mp'=4] {'mp'}, dimensions={1}, use_global_device_ids=true | all-gather | bytes 655360 | tf_op jit(solution)/shard_map/all_gather | solution.py:67
  265.5 7.3 %all_gather.76 = bf16[64,4096]{1,0:T(8,128)(2,1)S(1)} all-gather(bf16[64,1024]{1,0:T(8,128)(2,1)S(1)} %fusion.116), channel_id=1, replica_groups=mesh['section'=16,'dp'=8,'mp'=4] {'mp'}, dimensions={1}, use_global_device_ids=true | all-gather | bytes 655360 | tf_op jit(solution)/shard_map/all_gather | solution.py:67
  279.7 7.3 %all_gather.77 = bf16[64,4096]{1,0:T(8,128)(2,1)S(1)} all-gather(bf16[64,1024]{1,0:T(8,128)(2,1)S(1)} %fusion.117), channel_id=1, replica_groups=mesh['section'=16,'dp'=8,'mp'=4] {'mp'}, dimensions={1}, use_global_device_ids=true | all-gather | bytes 655360 | tf_op jit(solution)/shard_map/all_gather | solution.py:67
  294.1 7.3 %all_gather.78 = bf16[64,4096]{1,0:T(8,128)(2,1)S(1)} all-gather(bf16[64,1024]{1,0:T(8,128)(2,1)S(1)} %fusion.118), channel_id=1, replica_groups=mesh['section'=16,'dp'=8,'mp'=4] {'mp'}, dimensions={1}, use_global_device_ids=true | all-gather | bytes 655360 | tf_op jit(solution)/shard_map/all_gather | solution.py:67
  308.5 7.3 %all_gather.79 = bf16[64,4096]{1,0:T(8,128)(2,1)S(1)} all-gather(bf16[64,1024]{1,0:T(8,128)(2,1)S(1)} %fusion.119), channel_id=1, replica_groups=mesh['section'=16,'dp'=8,'mp'=4] {'mp'}, dimensions={1}, use_global_device_ids=true | all-gather | bytes 655360 | tf_op jit(solution)/shard_map/all_gather | solution.py:67
  323.2 80.7 %collective-permute-done.14 = bf16[64,1024]{1,0:T(8,128)(2,1)S(1)} collective-permute-done((bf16[64,1024]{1,0:T(8,128)(2,1)S(1)}, bf16[64,1024]{1,0:T(8,128)(2,1)S(1)}, u32[]{:S(2)}, u32[]{:S(2)}) %collective-permute-start.14) | collective-permute-done | bytes 131104 | tf_op jit(solution)/shard_map/ppermute | solution.py:61
  404.0 6.7 %all_gather.80 = bf16[64,4096]{1,0:T(8,128)(2,1)S(1)} all-gather(bf16[64,1024]{1,0:T(8,128)(2,1)S(1)} %fusion.120), channel_id=1, replica_groups=mesh['section'=16,'dp'=8,'mp'=4] {'mp'}, dimensions={1}, use_global_device_ids=true | all-gather | bytes 655360 | tf_op jit(solution)/shard_map/all_gather | solution.py:67
  418.1 5.9 %collective-permute-done.15 = bf16[64,1024]{1,0:T(8,128)(2,1)S(1)} collective-permute-done((bf16[64,1024]{1,0:T(8,128)(2,1)S(1)}, bf16[64,1024]{1,0:T(8,128)(2,1)S(1)}, u32[]{:S(2)}, u32[]{:S(2)}) %collective-permute-start.15) | collective-permute-done | bytes 131104 | tf_op jit(solution)/shard_map/ppermute | solution.py:61
  424.1 6.7 %all_gather.81 = bf16[64,4096]{1,0:T(8,128)(2,1)S(1)} all-gather(bf16[64,1024]{1,0:T(8,128)(2,1)S(1)} %multiply_convert_fusion), channel_id=1, replica_groups=mesh['section'=16,'dp'=8,'mp'=4] {'mp'}, dimensions={1}, use_global_device_ids=true | all-gather | bytes 655360 | tf_op jit(solution)/shard_map/all_gather | solution.py:67
  446.3 7.5 %collective-permute-done.18 = f32[16,8,4]{0,2,1:T(4,128)S(1)} collective-permute-done((f32[16,8,4]{0,2,1:T(4,128)S(1)}, f32[16,8,4]{0,2,1:T(4,128)S(1)}, u32[]{:S(2)}, u32[]{:S(2)}) %collective-permute-start.18) | collective-permute-done | bytes 2080 | tf_op jit(solution)/shard_map/ppermute | solution.py:106
  (254 shorter events, 171.1 us)
Async XLA Ops:
  7.2 107.6 %all-gather.5.cloned.1.call-start = ((), (), s32[]{:S(2)}) async-start(), calls=%async_computation | async-start | bytes 9437184 | tf_op jit(solution)/shard_map/all_gather | solution.py:35
  119.8 2.3 collective-permute-start
  134.6 1.2 collective-permute-start.1
  148.8 1.4 collective-permute-start.2
  163.2 1.7 collective-permute-start.3
  177.9 1.4 collective-permute-start.4
  192.3 1.2 collective-permute-start.5
  206.6 1.4 collective-permute-start.6
  221.0 1.2 collective-permute-start.7
  235.2 1.6 collective-permute-start.8
  249.8 1.2 collective-permute-start.9
  264.0 1.4 collective-permute-start.10
  278.4 1.2 collective-permute-start.11
  292.7 1.4 collective-permute-start.12
  307.0 1.4 collective-permute-start.13
  321.5 82.5 %collective-permute-start.14 = (bf16[64,1024]{1,0:T(8,128)(2,1)S(1)}, bf16[64,1024]{1,0:T(8,128)(2,1)S(1)}, u32[]{:S(2)}, u32[]{:S(2)}) collective-permute-start(bf16[64,1024]{1,0:T(8,128)(2,1)S(1)} %fusion.14), channel_id=1, source_target_pairs={{32,0},{64,32},{33,1},{65,33},{34,2},{66,34},{35,3},{67,35},{36,4}... | collective-permute-start | bytes 393224 | tf_op jit(solution)/shard_map/ppermute | solution.py:61
  416.4 7.6 %collective-permute-start.15 = (bf16[64,1024]{1,0:T(8,128)(2,1)S(1)}, bf16[64,1024]{1,0:T(8,128)(2,1)S(1)}, u32[]{:S(2)}, u32[]{:S(2)}) collective-permute-start(bf16[64,1024]{1,0:T(8,128)(2,1)S(1)} %fusion.15), channel_id=1, source_target_pairs={{32,0},{33,1},{34,2},{35,3},{36,4},{37,5},{38,6},{39,7},{40,8},{41... | collective-permute-start | bytes 393224 | tf_op jit(solution)/shard_map/ppermute | solution.py:61
  432.0 5.6 %collective-permute-start.16 = (f32[16,8,4]{0,2,1:T(4,128)S(1)}, f32[16,8,4]{0,2,1:T(4,128)S(1)}, u32[]{:S(2)}, u32[]{:S(2)}) collective-permute-start(f32[16,8,4]{0,2,1:T(4,128)S(1)} %broadcast_select_fusion), channel_id=1, source_target_pairs={{0,32},{4,36},{8,40},{12,44},{16,48},{20,52},{24,56},{28,60},{32,0... | collective-permute-start | bytes 6152 | tf_op jit(solution)/shard_map/ppermute | solution.py:106
  437.7 6.5 %collective-permute-start.17 = (f32[16,8,4]{0,2,1:T(4,128)S(1)}, f32[16,8,4]{0,2,1:T(4,128)S(1)}, u32[]{:S(2)}, u32[]{:S(2)}) collective-permute-start(f32[16,8,4]{0,2,1:T(4,128)S(1)} %fusion.191), channel_id=1, source_target_pairs={{0,64},{4,68},{8,72},{12,76},{16,80},{20,84},{24,88},{28,92},{32,9... | collective-permute-start | bytes 6152 | tf_op jit(solution)/shard_map/ppermute | solution.py:106
  444.2 9.5 %collective-permute-start.18 = (f32[16,8,4]{0,2,1:T(4,128)S(1)}, f32[16,8,4]{0,2,1:T(4,128)S(1)}, u32[]{:S(2)}, u32[]{:S(2)}) collective-permute-start(f32[16,8,4]{0,2,1:T(4,128)S(1)} %fusion.293), channel_id=1, source_target_pairs={{0,128},{4,132},{8,136},{12,140},{16,144},{20,148},{24,152},{28,15... | collective-permute-start | bytes 6152 | tf_op jit(solution)/shard_map/ppermute | solution.py:106
  453.8 7.1 %collective-permute-start.19 = (f32[16,8,4]{0,2,1:T(4,128)S(1)}, f32[16,8,4]{0,2,1:T(4,128)S(1)}, u32[]{:S(2)}, u32[]{:S(2)}) collective-permute-start(f32[16,8,4]{0,2,1:T(4,128)S(1)} %add.310), channel_id=1, source_target_pairs={{0,256},{4,260},{8,264},{12,268},{16,272},{20,276},{24,280},{28,28... | collective-permute-start | bytes 6152 | tf_op jit(solution)/shard_map/ppermute | solution.py:106
  460.9 5.6 %collective-permute-start.20 = (f32[16,8,4]{0,2,1:T(4,128)S(1)}, f32[16,8,4]{0,2,1:T(4,128)S(1)}, u32[]{:S(2)}, u32[]{:S(2)}) collective-permute-start(f32[16,8,4]{0,2,1:T(4,128)S(1)} %add.311), channel_id=1, source_target_pairs={{0,4},{4,0},{8,12},{12,8},{16,20},{20,16},{24,28},{28,24},{32,36},... | collective-permute-start | bytes 6152 | tf_op jit(solution)/shard_map/ppermute | solution.py:106
  466.5 6.5 %collective-permute-start.21 = (f32[16,8,4]{0,2,1:T(4,128)S(1)}, f32[16,8,4]{0,2,1:T(4,128)S(1)}, u32[]{:S(2)}, u32[]{:S(2)}) collective-permute-start(f32[16,8,4]{0,2,1:T(4,128)S(1)} %add.312), channel_id=1, source_target_pairs={{0,8},{4,12},{8,0},{12,4},{16,24},{20,28},{24,16},{28,20},{32,40},... | collective-permute-start | bytes 6152 | tf_op jit(solution)/shard_map/ppermute | solution.py:106
  473.1 9.5 %collective-permute-start.22 = (f32[16,8,4]{0,2,1:T(4,128)S(1)}, f32[16,8,4]{0,2,1:T(4,128)S(1)}, u32[]{:S(2)}, u32[]{:S(2)}) collective-permute-start(f32[16,8,4]{0,2,1:T(4,128)S(1)} %add.313), channel_id=1, source_target_pairs={{0,16},{4,20},{8,24},{12,28},{16,0},{20,4},{24,8},{28,12},{32,48},... | collective-permute-start | bytes 6152 | tf_op jit(solution)/shard_map/ppermute | solution.py:106
  (4 other events, 182.6 us)
Sparse Core Ops, SparseCore 0:
  10.1 104.6 all-gather.4

commit v7 on v6

--- a/solution.py
+++ b/solution.py
@@ -13,6 +13,22 @@
 def silu_slope(pre_state):
     sigma = jax.nn.sigmoid(pre_state)
     return sigma * (1.0 + pre_state * (1.0 - sigma))
+
+
+def group_sum(block, place, total, stride, ways):
+    sent = [block]
+    for shift in range(1, ways):
+        route = []
+        for i in range(total):
+            here = (i // stride) % ways
+            route.append((i, i + (((here + shift) % ways) - here) * stride))
+        sent.append(lax.ppermute(block, ("section", "dp"), route))
+    here = (place // stride) % ways
+    ordered = jnp.take(jnp.stack(sent), (here - jnp.arange(ways)) % ways, axis=0)
+    summed = ordered[0]
+    for position in range(1, ways):
+        summed = summed + ordered[position]
+    return summed
 
 
 def body(cotangent, saved_inputs, pre_acts, weights, proj_in, proj_out, query_panels, partners):
@@ -98,12 +114,18 @@
     owner = jnp.arange(asked) // per_dp
     meets = partners[:, owner].T == data_index
     scores = jnp.where(meets[:, :, None], mine[:, None, :] * score_scale, 0.0)
+    place = section_index * data_count + data_index
     total = section_count * data_count
-    levels = list(range(total.bit_length() - 1))
-    dp_levels = data_count.bit_length() - 1
-    for level in levels[dp_levels:] + levels[:dp_levels]:
-        route = [(i, i ^ (1 << level)) for i in range(total)]
-        scores = scores + lax.ppermute(scores, ("section", "dp"), route)
+    stride = 1
+    for ways in (4, 2) if data_count == 8 else (data_count,):
+        scores = group_sum(scores, place, total, stride, ways)
+        stride *= ways
+    left = section_count
+    while left > 1:
+        ways = 4 if left % 4 == 0 else 2
+        scores = group_sum(scores, place, total, stride, ways)
+        stride *= ways
+        left //= ways
     return (panels_here[None], scores)
 
 

time: 500 us -> 507 us (1.014)
  the two profiles are of different devices: /device:TPU:2 before, /device:TPU:56 now
where the time goes in v7:
time: 507 us; the launch traced here: 499 us
  blocking collectives  178 us (35%)
  waiting for transfers between devices  115 us (23%)
  matrix products  98.5 us (19%)
  starting transfers between devices  75.9 us (15%)
  between operations  15.9 us (3%)
  local copies, waits for them, and re-layouts  11.4 us (2%)
    all_gather x17, blocking collectives, body(): grad_full = lax.all_gather(grad_piece, 'mp', axis=1, tiled=True)  122 us
    dot_general x16, matrix products, body(): back_term = jnp.dot(grad_full, w_cols, preferred_element_type=jnp.float32)  79.3 us
    ppermute x10, starting transfers between devices, group_sum(): sent.append(lax.ppermute(block, ('section', 'dp'), route))  62.7 us
    ppermute x16, waiting for transfers between devices, body(): received = lax.ppermute(outgoing, 'section', [(k, k - 1) for k in senders])  56 us
    all_gather x1, waiting for transfers between devices, body(): w_cols = lax.all_gather(weights[0].T, 'dp', axis=0, tiled=True)  36.3 us
    all_gather x1, blocking collectives, body(): queries = lax.all_gather(queries, 'dp', axis=0, tiled=True)  31.8 us
    ppermute x10, waiting for transfers between devices, group_sum(): sent.append(lax.ppermute(block, ('section', 'dp'), route))  22.8 us
    ppermute x16, starting transfers between devices, body(): received = lax.ppermute(outgoing, 'section', [(k, k - 1) for k in senders])  13.2 us
  transfers between devices with their start and end apart: 27, of which 9 were waited for; matrix products, arithmetic and copies ran while one was open for 3% of the time, Pallas kernels for 0%

profile of v7, /device:TPU:56, one launch (start us, length us, event | category | flops | bytes accessed | tf_op | source)
XLA Modules:
  0.0 498.8 jit_solution(2373537880441093370)
XLA Ops:
  11.0 11.4 %psum.7 = f32[128,64]{0,1:T(8,128)S(1)} all-reduce(f32[128,64]{0,1:T(8,128)S(1)} %fusion.138), channel_id=1, replica_groups=mesh['section'=16,'dp'=8,'mp'=4] {'mp'}, use_global_device_ids=true, to_apply=%region_0.0 | all-reduce | flops 8192 | bytes 65536 | tf_op jit(solution)/shard_map/psum | solution.py:56
  31.3 7.5 %all-gather = bf16[1,4096,64]{1,2,0:T(8,128)(2,1)S(1)} all-gather(bf16[1,1024,64]{1,2,0:T(8,128)(2,1)} %param.15), channel_id=2, replica_groups=mesh['section'=16,'dp'=8,'mp'=4] {'mp'}, dimensions={1}, use_global_device_ids=true | all-gather | bytes 655360 | tf_op jit(solution)/shard_map/all_gather | solution.py:54
  45.5 31.8 %all-gather.2 = f32[1,16,4096]{2,0,1:T(1,128)S(1)} all-gather(f32[1,2,4096]{2,0,1:T(1,128)S(1)} %all-gather.1), channel_id=4, replica_groups=mesh['section'=16,'dp'=8,'mp'=4] {'dp'}, dimensions={1}, use_global_device_ids=true | all-gather | bytes 294912 | tf_op jit(solution)/shard_map/all_gather | solution.py:59
  78.0 36.3 %all-gather.5.cloned.1.call-done = bf16[4096,1024]{1,0:T(8,128)(2,1)} async-done(((bf16[512,1024]{1,0:T(8,128)(2,1)}), bf16[4096,1024]{1,0:T(8,128)(2,1)}) %all-gather.5.cloned.1.call-update) | async-done | bytes 8388624 | tf_op jit(solution)/shard_map/all_gather | solution.py:51
  121.6 7.2 %all_gather.66 = bf16[64,4096]{1,0:T(8,128)(2,1)S(1)} all-gather(bf16[64,1024]{1,0:T(8,128)(2,1)S(1)} %fusion.106), channel_id=1, replica_groups=mesh['section'=16,'dp'=8,'mp'=4] {'mp'}, dimensions={1}, use_global_device_ids=true | all-gather | bytes 655360 | tf_op jit(solution)/shard_map/all_gather | solution.py:83
  135.7 7.3 %all_gather.67 = bf16[64,4096]{1,0:T(8,128)(2,1)S(1)} all-gather(bf16[64,1024]{1,0:T(8,128)(2,1)S(1)} %fusion.107), channel_id=1, replica_groups=mesh['section'=16,'dp'=8,'mp'=4] {'mp'}, dimensions={1}, use_global_device_ids=true | all-gather | bytes 655360 | tf_op jit(solution)/shard_map/all_gather | solution.py:83
  150.1 7.8 %all_gather.68 = bf16[64,4096]{1,0:T(8,128)(2,1)S(1)} all-gather(bf16[64,1024]{1,0:T(8,128)(2,1)S(1)} %fusion.108), channel_id=1, replica_groups=mesh['section'=16,'dp'=8,'mp'=4] {'mp'}, dimensions={1}, use_global_device_ids=true | all-gather | bytes 655360 | tf_op jit(solution)/shard_map/all_gather | solution.py:83
  164.8 7.3 %all_gather.69 = bf16[64,4096]{1,0:T(8,128)(2,1)S(1)} all-gather(bf16[64,1024]{1,0:T(8,128)(2,1)S(1)} %fusion.109), channel_id=1, replica_groups=mesh['section'=16,'dp'=8,'mp'=4] {'mp'}, dimensions={1}, use_global_device_ids=true | all-gather | bytes 655360 | tf_op jit(solution)/shard_map/all_gather | solution.py:83
  179.2 7.3 %all_gather.70 = bf16[64,4096]{1,0:T(8,128)(2,1)S(1)} all-gather(bf16[64,1024]{1,0:T(8,128)(2,1)S(1)} %fusion.110), channel_id=1, replica_groups=mesh['section'=16,'dp'=8,'mp'=4] {'mp'}, dimensions={1}, use_global_device_ids=true | all-gather | bytes 655360 | tf_op jit(solution)/shard_map/all_gather | solution.py:83
  193.4 7.3 %all_gather.71 = bf16[64,4096]{1,0:T(8,128)(2,1)S(1)} all-gather(bf16[64,1024]{1,0:T(8,128)(2,1)S(1)} %fusion.111), channel_id=1, replica_groups=mesh['section'=16,'dp'=8,'mp'=4] {'mp'}, dimensions={1}, use_global_device_ids=true | all-gather | bytes 655360 | tf_op jit(solution)/shard_map/all_gather | solution.py:83
  207.9 7.3 %all_gather.72 = bf16[64,4096]{1,0:T(8,128)(2,1)S(1)} all-gather(bf16[64,1024]{1,0:T(8,128)(2,1)S(1)} %fusion.112), channel_id=1, replica_groups=mesh['section'=16,'dp'=8,'mp'=4] {'mp'}, dimensions={1}, use_global_device_ids=true | all-gather | bytes 655360 | tf_op jit(solution)/shard_map/all_gather | solution.py:83
  222.6 44.3 %collective-permute-done.7 = bf16[64,1024]{1,0:T(8,128)(2,1)S(1)} collective-permute-done((bf16[64,1024]{1,0:T(8,128)(2,1)S(1)}, bf16[64,1024]{1,0:T(8,128)(2,1)S(1)}, u32[]{:S(2)}, u32[]{:S(2)}) %collective-permute-start.7) | collective-permute-done | bytes 131104 | tf_op jit(solution)/shard_map/ppermute | solution.py:77
  266.9 6.9 %all_gather.73 = bf16[64,4096]{1,0:T(8,128)(2,1)S(1)} all-gather(bf16[64,1024]{1,0:T(8,128)(2,1)S(1)} %fusion.113), channel_id=1, replica_groups=mesh['section'=16,'dp'=8,'mp'=4] {'mp'}, dimensions={1}, use_global_device_ids=true | all-gather | bytes 655360 | tf_op jit(solution)/shard_map/all_gather | solution.py:83
  282.1 8.6 %collective-permute-done.8 = bf16[64,1024]{1,0:T(8,128)(2,1)S(1)} collective-permute-done((bf16[64,1024]{1,0:T(8,128)(2,1)S(1)}, bf16[64,1024]{1,0:T(8,128)(2,1)S(1)}, u32[]{:S(2)}, u32[]{:S(2)}) %collective-permute-start.8) | collective-permute-done | bytes 131104 | tf_op jit(solution)/shard_map/ppermute | solution.py:77
  308.0 6.7 %all_gather.75 = bf16[64,4096]{1,0:T(8,128)(2,1)S(1)} all-gather(bf16[64,1024]{1,0:T(8,128)(2,1)S(1)} %fusion.115), channel_id=1, replica_groups=mesh['section'=16,'dp'=8,'mp'=4] {'mp'}, dimensions={1}, use_global_device_ids=true | all-gather | bytes 655360 | tf_op jit(solution)/shard_map/all_gather | solution.py:83
  321.8 7.3 %all_gather.76 = bf16[64,4096]{1,0:T(8,128)(2,1)S(1)} all-gather(bf16[64,1024]{1,0:T(8,128)(2,1)S(1)} %fusion.116), channel_id=1, replica_groups=mesh['section'=16,'dp'=8,'mp'=4] {'mp'}, dimensions={1}, use_global_device_ids=true | all-gather | bytes 655360 | tf_op jit(solution)/shard_map/all_gather | solution.py:83
  336.0 7.3 %all_gather.77 = bf16[64,4096]{1,0:T(8,128)(2,1)S(1)} all-gather(bf16[64,1024]{1,0:T(8,128)(2,1)S(1)} %fusion.117), channel_id=1, replica_groups=mesh['section'=16,'dp'=8,'mp'=4] {'mp'}, dimensions={1}, use_global_device_ids=true | all-gather | bytes 655360 | tf_op jit(solution)/shard_map/all_gather | solution.py:83
  350.5 7.5 %all_gather.78 = bf16[64,4096]{1,0:T(8,128)(2,1)S(1)} all-gather(bf16[64,1024]{1,0:T(8,128)(2,1)S(1)} %fusion.118), channel_id=1, replica_groups=mesh['section'=16,'dp'=8,'mp'=4] {'mp'}, dimensions={1}, use_global_device_ids=true | all-gather | bytes 655360 | tf_op jit(solution)/shard_map/all_gather | solution.py:83
  364.9 7.3 %all_gather.79 = bf16[64,4096]{1,0:T(8,128)(2,1)S(1)} all-gather(bf16[64,1024]{1,0:T(8,128)(2,1)S(1)} %fusion.119), channel_id=1, replica_groups=mesh['section'=16,'dp'=8,'mp'=4] {'mp'}, dimensions={1}, use_global_device_ids=true | all-gather | bytes 655360 | tf_op jit(solution)/shard_map/all_gather | solution.py:83
  379.3 7.3 %all_gather.80 = bf16[64,4096]{1,0:T(8,128)(2,1)S(1)} all-gather(bf16[64,1024]{1,0:T(8,128)(2,1)S(1)} %fusion.120), channel_id=1, replica_groups=mesh['section'=16,'dp'=8,'mp'=4] {'mp'}, dimensions={1}, use_global_device_ids=true | all-gather | bytes 655360 | tf_op jit(solution)/shard_map/all_gather | solution.py:83
  393.6 7.3 %all_gather.81 = bf16[64,4096]{1,0:T(8,128)(2,1)S(1)} all-gather(bf16[64,1024]{1,0:T(8,128)(2,1)S(1)} %multiply_convert_fusion), channel_id=1, replica_groups=mesh['section'=16,'dp'=8,'mp'=4] {'mp'}, dimensions={1}, use_global_device_ids=true | all-gather | bytes 655360 | tf_op jit(solution)/shard_map/all_gather | solution.py:83
  425.6 17.0 %collective-permute-start.20 = (f32[16,8,4]{0,1,2:T(8,128)S(1)}, f32[16,8,4]{0,1,2:T(8,128)S(1)}, u32[]{:S(2)}, u32[]{:S(2)}) collective-permute-start(f32[16,8,4]{0,1,2:T(8,128)S(1)} %fusion.300), channel_id=1, source_target_pairs={{0,32},{4,36},{8,40},{12,44},{16,48},{20,52},{24,56},{28,60},{32,6... | collective-permute-start | bytes 6152 | tf_op jit(solution)/shard_map/ppermute | solution.py:25
  454.6 23.9 %collective-permute-start.24 = (f32[16,8,4]{0,1,2:T(8,128)S(1)}, f32[16,8,4]{0,1,2:T(8,128)S(1)}, u32[]{:S(2)}, u32[]{:S(2)}) collective-permute-start(f32[16,8,4]{0,1,2:T(8,128)S(1)} %fusion.299), channel_id=1, source_target_pairs={{0,256},{4,260},{8,264},{12,268},{16,272},{20,276},{24,280},{28,28... | collective-permute-start | bytes 6152 | tf_op jit(solution)/shard_map/ppermute | solution.py:25
  480.5 10.0 %collective-permute-done.25 = f32[16,8,4]{0,1,2:T(8,128)S(1)} collective-permute-done((f32[16,8,4]{0,1,2:T(8,128)S(1)}, f32[16,8,4]{0,1,2:T(8,128)S(1)}, u32[]{:S(2)}, u32[]{:S(2)}) %collective-permute-start.25) | collective-permute-done | bytes 2080 | tf_op jit(solution)/shard_map/ppermute | solution.py:25
  (285 shorter events, 183.1 us)
Async XLA Ops:
  7.2 107.1 %all-gather.5.cloned.1.call-start = ((), (), s32[]{:S(2)}) async-start(), calls=%async_computation | async-start | bytes 9437184 | tf_op jit(solution)/shard_map/all_gather | solution.py:51
  119.2 2.3 collective-permute-start
  148.6 1.4 collective-permute-start.2
  163.5 1.2 collective-permute-start.3
  177.7 1.4 collective-permute-start.4
  206.4 1.4 collective-permute-start.6
  220.8 46.0 %collective-permute-start.7 = (bf16[64,1024]{1,0:T(8,128)(2,1)S(1)}, bf16[64,1024]{1,0:T(8,128)(2,1)S(1)}, u32[]{:S(2)}, u32[]{:S(2)}) collective-permute-start(bf16[64,1024]{1,0:T(8,128)(2,1)S(1)} %fusion.7), channel_id=1, source_target_pairs={{256,224},{288,256},{257,225},{289,257},{258,226},{290,258},{259,2... | collective-permute-start | bytes 393224 | tf_op jit(solution)/shard_map/ppermute | solution.py:77
  279.4 11.3 %collective-permute-start.8 = (bf16[64,1024]{1,0:T(8,128)(2,1)S(1)}, bf16[64,1024]{1,0:T(8,128)(2,1)S(1)}, u32[]{:S(2)}, u32[]{:S(2)}) collective-permute-start(bf16[64,1024]{1,0:T(8,128)(2,1)S(1)} %fusion.8), channel_id=1, source_target_pairs={{224,192},{256,224},{225,193},{257,225},{226,194},{258,226},{227,1... | collective-permute-start | bytes 393224 | tf_op jit(solution)/shard_map/ppermute | solution.py:77
  303.1 4.8 collective-permute-start.9
  320.4 1.4 collective-permute-start.10
  334.8 1.2 collective-permute-start.11
  349.0 1.4 collective-permute-start.12
  363.6 1.2 collective-permute-start.13
  377.9 1.4 collective-permute-start.14
  402.1 10.4 %collective-permute-start.16 = (f32[16,8,4]{0,1,2:T(8,128)S(1)}, f32[16,8,4]{0,1,2:T(8,128)S(1)}, u32[]{:S(2)}, u32[]{:S(2)}) collective-permute-start(f32[16,8,4]{0,1,2:T(8,128)S(1)} %broadcast_select_fusion.4), channel_id=1, source_target_pairs={{0,4},{4,8},{8,12},{12,0},{16,20},{20,24},{24,28},{28,16},{32,36},... | collective-permute-start | bytes 6152 | tf_op jit(solution)/shard_map/ppermute | solution.py:25
  404.0 8.5 %collective-permute-start.17 = (f32[16,8,4]{0,1,2:T(8,128)S(1)}, f32[16,8,4]{0,1,2:T(8,128)S(1)}, u32[]{:S(2)}, u32[]{:S(2)}) collective-permute-start(f32[16,8,4]{0,1,2:T(8,128)S(1)} %broadcast_select_fusion.4), channel_id=1, source_target_pairs={{0,8},{4,12},{8,0},{12,4},{16,24},{20,28},{24,16},{28,20},{32,40},... | collective-permute-start | bytes 6152 | tf_op jit(solution)/shard_map/ppermute | solution.py:25
  409.2 5.6 %collective-permute-start.18 = (f32[16,8,4]{0,1,2:T(8,128)S(1)}, f32[16,8,4]{0,1,2:T(8,128)S(1)}, u32[]{:S(2)}, u32[]{:S(2)}) collective-permute-start(f32[16,8,4]{0,1,2:T(8,128)S(1)} %broadcast_select_fusion.4), channel_id=1, source_target_pairs={{0,12},{4,0},{8,4},{12,8},{16,28},{20,16},{24,20},{28,24},{32,44},... | collective-permute-start | bytes 6152 | tf_op jit(solution)/shard_map/ppermute | solution.py:25
  415.5 9.5 %collective-permute-start.19 = (f32[16,8,4]{0,1,2:T(8,128)S(1)}, f32[16,8,4]{0,1,2:T(8,128)S(1)}, u32[]{:S(2)}, u32[]{:S(2)}) collective-permute-start(f32[16,8,4]{0,1,2:T(8,128)S(1)} %fusion.301), channel_id=1, source_target_pairs={{0,16},{4,20},{8,24},{12,28},{16,0},{20,4},{24,8},{28,12},{32,48},... | collective-permute-start | bytes 6152 | tf_op jit(solution)/shard_map/ppermute | solution.py:25
  425.6 21.5 %collective-permute-start.20 = (f32[16,8,4]{0,1,2:T(8,128)S(1)}, f32[16,8,4]{0,1,2:T(8,128)S(1)}, u32[]{:S(2)}, u32[]{:S(2)}) collective-permute-start(f32[16,8,4]{0,1,2:T(8,128)S(1)} %fusion.300), channel_id=1, source_target_pairs={{0,32},{4,36},{8,40},{12,44},{16,48},{20,52},{24,56},{28,60},{32,6... | collective-permute-start | bytes 6152 | tf_op jit(solution)/shard_map/ppermute | solution.py:25
  442.7 6.5 %collective-permute-start.21 = (f32[16,8,4]{0,1,2:T(8,128)S(1)}, f32[16,8,4]{0,1,2:T(8,128)S(1)}, u32[]{:S(2)}, u32[]{:S(2)}) collective-permute-start(f32[16,8,4]{0,1,2:T(8,128)S(1)} %fusion.300), channel_id=1, source_target_pairs={{0,64},{4,68},{8,72},{12,76},{16,80},{20,84},{24,88},{28,92},{32,9... | collective-permute-start | bytes 6152 | tf_op jit(solution)/shard_map/ppermute | solution.py:25
  444.6 7.4 %collective-permute-start.22 = (f32[16,8,4]{0,1,2:T(8,128)S(1)}, f32[16,8,4]{0,1,2:T(8,128)S(1)}, u32[]{:S(2)}, u32[]{:S(2)}) collective-permute-start(f32[16,8,4]{0,1,2:T(8,128)S(1)} %fusion.300), channel_id=1, source_target_pairs={{0,96},{4,100},{8,104},{12,108},{16,112},{20,116},{24,120},{28,124... | collective-permute-start | bytes 6152 | tf_op jit(solution)/shard_map/ppermute | solution.py:25
  452.7 27.8 %collective-permute-start.23 = (f32[16,8,4]{0,1,2:T(8,128)S(1)}, f32[16,8,4]{0,1,2:T(8,128)S(1)}, u32[]{:S(2)}, u32[]{:S(2)}) collective-permute-start(f32[16,8,4]{0,1,2:T(8,128)S(1)} %fusion.299), channel_id=1, source_target_pairs={{0,128},{4,132},{8,136},{12,140},{16,144},{20,148},{24,152},{28,15... | collective-permute-start | bytes 6152 | tf_op jit(solution)/shard_map/ppermute | solution.py:25
  454.6 25.9 %collective-permute-start.24 = (f32[16,8,4]{0,1,2:T(8,128)S(1)}, f32[16,8,4]{0,1,2:T(8,128)S(1)}, u32[]{:S(2)}, u32[]{:S(2)}) collective-permute-start(f32[16,8,4]{0,1,2:T(8,128)S(1)} %fusion.299), channel_id=1, source_target_pairs={{0,256},{4,260},{8,264},{12,268},{16,272},{20,276},{24,280},{28,28... | collective-permute-start | bytes 6152 | tf_op jit(solution)/shard_map/ppermute | solution.py:25
  478.6 11.9 %collective-permute-start.25 = (f32[16,8,4]{0,1,2:T(8,128)S(1)}, f32[16,8,4]{0,1,2:T(8,128)S(1)}, u32[]{:S(2)}, u32[]{:S(2)}) collective-permute-start(f32[16,8,4]{0,1,2:T(8,128)S(1)} %fusion.299), channel_id=1, source_target_pairs={{0,384},{4,388},{8,392},{12,396},{16,400},{20,404},{24,408},{28,41... | collective-permute-start | bytes 6152 | tf_op jit(solution)/shard_map/ppermute | solution.py:25
  (7 other events, 178.0 us)
Sparse Core Ops, SparseCore 0:
  10.1 104.1 all-gather.4

commit v8 on v6

--- a/solution.py
+++ b/solution.py
@@ -7,7 +7,7 @@
 from jax.sharding import PartitionSpec as P
 
 LEN = 32
-CHUNKS = 2
+CHUNKS = 4
 
 
 def silu_slope(pre_state):

time: 500 us -> 503 us (level)
  blocking collectives: 177 us -> 167 us
  matrix products: 98.5 us -> 108 us
    all_gather x17 -> x19, blocking collectives: 123 us -> 113 us  [body(): grad_full = lax.all_gather(grad_piece, 'mp', axis=1, tiled=True)]
    dot_general x16 -> x18, matrix products: 79.3 us -> 88.8 us  [body(): back_term = jnp.dot(grad_full, w_cols, preferred_element_type=jnp.float32)]
    ppermute x16 -> x18, waiting for transfers between devices: 86.7 us -> 88.7 us  [body(): received = lax.ppermute(outgoing, 'section', [(k, k - 1) for k in senders])]
    ppermute x16 -> x18, starting transfers between devices: 12.8 us -> 14.5 us  [body(): received = lax.ppermute(outgoing, 'section', [(k, k - 1) for k in senders])]
  transfers between devices with their start and end apart: 24 -> 26, of which waited for: 10 -> 12; matrix products, arithmetic and copies ran while one was open for 3% -> 3% of each run, Pallas kernels for 0% -> 0%
where the time goes in v8:
time: 503 us; the launch traced here: 494 us
  blocking collectives  167 us (33%)
  waiting for transfers between devices  159 us (32%)
  matrix products  108 us (21%)
  starting transfers between devices  32 us (6%)
  between operations  15.7 us (3%)
  local copies, waits for them, and re-layouts  8.78 us (2%)
    all_gather x19, blocking collectives, body(): grad_full = lax.all_gather(grad_piece, 'mp', axis=1, tiled=True)  113 us
    dot_general x18, matrix products, body(): back_term = jnp.dot(grad_full, w_cols, preferred_element_type=jnp.float32)  88.8 us
    ppermute x18, waiting for transfers between devices, body(): received = lax.ppermute(outgoing, 'section', [(k, k - 1) for k in senders])  88.7 us
    all_gather x1, waiting for transfers between devices, body(): w_cols = lax.all_gather(weights[0].T, 'dp', axis=0, tiled=True)  37.8 us
    ppermute x7, waiting for transfers between devices, body(): scores = scores + lax.ppermute(scores, ('section', 'dp'), route)  32.5 us
    all_gather x1, blocking collectives, body(): queries = lax.all_gather(queries, 'dp', axis=0, tiled=True)  27.6 us
    ppermute x7, starting transfers between devices, body(): scores = scores + lax.ppermute(scores, ('section', 'dp'), route)  17.5 us
    ppermute x18, starting transfers between devices, body(): received = lax.ppermute(outgoing, 'section', [(k, k - 1) for k in senders])  14.5 us
  transfers between devices with their start and end apart: 26, of which 12 were waited for; matrix products, arithmetic and copies ran while one was open for 3% of the time, Pallas kernels for 0%

profile of v8, /device:TPU:2, one launch (start us, length us, event | category | flops | bytes accessed | tf_op | source)
XLA Modules:
  0.0 494.1 jit_solution(9853588407153997199)
XLA Ops:
  10.9 13.9 %psum.7 = f32[128,64]{0,1:T(8,128)S(1)} all-reduce(f32[128,64]{0,1:T(8,128)S(1)} %fusion.118), channel_id=1, replica_groups=mesh['section'=16,'dp'=8,'mp'=4] {'mp'}, use_global_device_ids=true, to_apply=%region_0.0 | all-reduce | flops 8192 | bytes 65536 | tf_op jit(solution)/shard_map/psum | solution.py:40
  26.8 6.5 %all_gather.69 = bf16[32,4096]{1,0:T(8,128)(2,1)S(1)} all-gather(bf16[32,1024]{1,0:T(8,128)(2,1)S(1)} %fusion.120), channel_id=1, replica_groups=mesh['section'=16,'dp'=8,'mp'=4] {'mp'}, dimensions={1}, use_global_device_ids=true | all-gather | bytes 327680 | tf_op jit(solution)/shard_map/all_gather | solution.py:67
  33.3 7.5 %all-gather = bf16[1,4096,64]{1,2,0:T(8,128)(2,1)S(1)} all-gather(bf16[1,1024,64]{1,2,0:T(8,128)(2,1)} %param.13), channel_id=2, replica_groups=mesh['section'=16,'dp'=8,'mp'=4] {'mp'}, dimensions={1}, use_global_device_ids=true | all-gather | bytes 655360 | tf_op jit(solution)/shard_map/all_gather | solution.py:38
  48.8 27.6 %all-gather.2 = f32[1,16,4096]{2,0,1:T(1,128)S(1)} all-gather(f32[1,2,4096]{2,0,1:T(1,128)S(1)} %all-gather.1), channel_id=4, replica_groups=mesh['section'=16,'dp'=8,'mp'=4] {'dp'}, dimensions={1}, use_global_device_ids=true | all-gather | bytes 294912 | tf_op jit(solution)/shard_map/all_gather | solution.py:43
  77.0 37.8 %all-gather.5.cloned.1.call-done = bf16[4096,1024]{1,0:T(8,128)(2,1)} async-done(((bf16[512,1024]{1,0:T(8,128)(2,1)}), bf16[4096,1024]{1,0:T(8,128)(2,1)}) %all-gather.5.cloned.1.call-update) | async-done | bytes 8388624 | tf_op jit(solution)/shard_map/all_gather | solution.py:35
  120.5 5.8 %all_gather.72 = bf16[32,4096]{1,0:T(8,128)(2,1)S(1)} all-gather(bf16[32,1024]{1,0:T(8,128)(2,1)S(1)} %fusion.121), channel_id=1, replica_groups=mesh['section'=16,'dp'=8,'mp'=4] {'mp'}, dimensions={1}, use_global_device_ids=true | all-gather | bytes 327680 | tf_op jit(solution)/shard_map/all_gather | solution.py:67
  133.2 5.9 %all_gather.73 = bf16[32,4096]{1,0:T(8,128)(2,1)S(1)} all-gather(bf16[32,1024]{1,0:T(8,128)(2,1)S(1)} %fusion.122), channel_id=1, replica_groups=mesh['section'=16,'dp'=8,'mp'=4] {'mp'}, dimensions={1}, use_global_device_ids=true | all-gather | bytes 327680 | tf_op jit(solution)/shard_map/all_gather | solution.py:67
  146.0 5.9 %all_gather.74 = bf16[32,4096]{1,0:T(8,128)(2,1)S(1)} all-gather(bf16[32,1024]{1,0:T(8,128)(2,1)S(1)} %fusion.123), channel_id=1, replica_groups=mesh['section'=16,'dp'=8,'mp'=4] {'mp'}, dimensions={1}, use_global_device_ids=true | all-gather | bytes 327680 | tf_op jit(solution)/shard_map/all_gather | solution.py:67
  158.8 6.3 %all_gather.75 = bf16[32,4096]{1,0:T(8,128)(2,1)S(1)} all-gather(bf16[32,1024]{1,0:T(8,128)(2,1)S(1)} %fusion.124), channel_id=1, replica_groups=mesh['section'=16,'dp'=8,'mp'=4] {'mp'}, dimensions={1}, use_global_device_ids=true | all-gather | bytes 327680 | tf_op jit(solution)/shard_map/all_gather | solution.py:67
  172.0 5.9 %all_gather.76 = bf16[32,4096]{1,0:T(8,128)(2,1)S(1)} all-gather(bf16[32,1024]{1,0:T(8,128)(2,1)S(1)} %fusion.125), channel_id=1, replica_groups=mesh['section'=16,'dp'=8,'mp'=4] {'mp'}, dimensions={1}, use_global_device_ids=true | all-gather | bytes 327680 | tf_op jit(solution)/shard_map/all_gather | solution.py:67
  184.7 5.9 %all_gather.77 = bf16[32,4096]{1,0:T(8,128)(2,1)S(1)} all-gather(bf16[32,1024]{1,0:T(8,128)(2,1)S(1)} %fusion.126), channel_id=1, replica_groups=mesh['section'=16,'dp'=8,'mp'=4] {'mp'}, dimensions={1}, use_global_device_ids=true | all-gather | bytes 327680 | tf_op jit(solution)/shard_map/all_gather | solution.py:67
  197.5 5.9 %all_gather.78 = bf16[32,4096]{1,0:T(8,128)(2,1)S(1)} all-gather(bf16[32,1024]{1,0:T(8,128)(2,1)S(1)} %fusion.127), channel_id=1, replica_groups=mesh['section'=16,'dp'=8,'mp'=4] {'mp'}, dimensions={1}, use_global_device_ids=true | all-gather | bytes 327680 | tf_op jit(solution)/shard_map/all_gather | solution.py:67
  210.3 5.9 %all_gather.79 = bf16[32,4096]{1,0:T(8,128)(2,1)S(1)} all-gather(bf16[32,1024]{1,0:T(8,128)(2,1)S(1)} %fusion.128), channel_id=1, replica_groups=mesh['section'=16,'dp'=8,'mp'=4] {'mp'}, dimensions={1}, use_global_device_ids=true | all-gather | bytes 327680 | tf_op jit(solution)/shard_map/all_gather | solution.py:67
  223.0 6.0 %all_gather.80 = bf16[32,4096]{1,0:T(8,128)(2,1)S(1)} all-gather(bf16[32,1024]{1,0:T(8,128)(2,1)S(1)} %fusion.129), channel_id=1, replica_groups=mesh['section'=16,'dp'=8,'mp'=4] {'mp'}, dimensions={1}, use_global_device_ids=true | all-gather | bytes 327680 | tf_op jit(solution)/shard_map/all_gather | solution.py:67
  236.0 5.9 %all_gather.81 = bf16[32,4096]{1,0:T(8,128)(2,1)S(1)} all-gather(bf16[32,1024]{1,0:T(8,128)(2,1)S(1)} %fusion.130), channel_id=1, replica_groups=mesh['section'=16,'dp'=8,'mp'=4] {'mp'}, dimensions={1}, use_global_device_ids=true | all-gather | bytes 327680 | tf_op jit(solution)/shard_map/all_gather | solution.py:67
  248.7 5.9 %all_gather.82 = bf16[32,4096]{1,0:T(8,128)(2,1)S(1)} all-gather(bf16[32,1024]{1,0:T(8,128)(2,1)S(1)} %fusion.131), channel_id=1, replica_groups=mesh['section'=16,'dp'=8,'mp'=4] {'mp'}, dimensions={1}, use_global_device_ids=true | all-gather | bytes 327680 | tf_op jit(solution)/shard_map/all_gather | solution.py:67
  261.5 5.9 %all_gather.83 = bf16[32,4096]{1,0:T(8,128)(2,1)S(1)} all-gather(bf16[32,1024]{1,0:T(8,128)(2,1)S(1)} %fusion.132), channel_id=1, replica_groups=mesh['section'=16,'dp'=8,'mp'=4] {'mp'}, dimensions={1}, use_global_device_ids=true | all-gather | bytes 327680 | tf_op jit(solution)/shard_map/all_gather | solution.py:67
  274.2 5.9 %all_gather.84 = bf16[32,4096]{1,0:T(8,128)(2,1)S(1)} all-gather(bf16[32,1024]{1,0:T(8,128)(2,1)S(1)} %fusion.133), channel_id=1, replica_groups=mesh['section'=16,'dp'=8,'mp'=4] {'mp'}, dimensions={1}, use_global_device_ids=true | all-gather | bytes 327680 | tf_op jit(solution)/shard_map/all_gather | solution.py:67
  287.0 6.1 %all_gather.85 = bf16[32,4096]{1,0:T(8,128)(2,1)S(1)} all-gather(bf16[32,1024]{1,0:T(8,128)(2,1)S(1)} %fusion.134), channel_id=1, replica_groups=mesh['section'=16,'dp'=8,'mp'=4] {'mp'}, dimensions={1}, use_global_device_ids=true | all-gather | bytes 327680 | tf_op jit(solution)/shard_map/all_gather | solution.py:67
  300.6 67.8 %collective-permute-done.14 = bf16[32,1024]{1,0:T(8,128)(2,1)S(1)} collective-permute-done((bf16[32,1024]{1,0:T(8,128)(2,1)S(1)}, bf16[32,1024]{1,0:T(8,128)(2,1)S(1)}, u32[]{:S(2)}, u32[]{:S(2)}) %collective-permute-start.14) | collective-permute-done | bytes 65568 | tf_op jit(solution)/shard_map/ppermute | solution.py:61
  368.4 5.8 %all_gather.86 = bf16[32,4096]{1,0:T(8,128)(2,1)S(1)} all-gather(bf16[32,1024]{1,0:T(8,128)(2,1)S(1)} %fusion.135), channel_id=1, replica_groups=mesh['section'=16,'dp'=8,'mp'=4] {'mp'}, dimensions={1}, use_global_device_ids=true | all-gather | bytes 327680 | tf_op jit(solution)/shard_map/all_gather | solution.py:67
  381.7 8.4 %collective-permute-done.15 = bf16[32,1024]{1,0:T(8,128)(2,1)S(1)} collective-permute-done((bf16[32,1024]{1,0:T(8,128)(2,1)S(1)}, bf16[32,1024]{1,0:T(8,128)(2,1)S(1)}, u32[]{:S(2)}, u32[]{:S(2)}) %collective-permute-start.15) | collective-permute-done | bytes 65568 | tf_op jit(solution)/shard_map/ppermute | solution.py:61
  403.3 8.0 %collective-permute-done.16 = bf16[32,1024]{1,0:T(8,128)(2,1)S(1)} collective-permute-done((bf16[32,1024]{1,0:T(8,128)(2,1)S(1)}, bf16[32,1024]{1,0:T(8,128)(2,1)S(1)}, u32[]{:S(2)}, u32[]{:S(2)}) %collective-permute-start.16) | collective-permute-done | bytes 65568 | tf_op jit(solution)/shard_map/ppermute | solution.py:61
  450.0 7.6 %collective-permute-done.20 = f32[16,8,4]{0,2,1:T(4,128)S(1)} collective-permute-done((f32[16,8,4]{0,2,1:T(4,128)S(1)}, f32[16,8,4]{0,2,1:T(4,128)S(1)}, u32[]{:S(2)}, u32[]{:S(2)}) %collective-permute-start.20) | collective-permute-done | bytes 2080 | tf_op jit(solution)/shard_map/ppermute | solution.py:106
  (270 shorter events, 204.6 us)
Async XLA Ops:
  7.2 107.7 %all-gather.5.cloned.1.call-start = ((), (), s32[]{:S(2)}) async-start(), calls=%async_computation | async-start | bytes 9437184 | tf_op jit(solution)/shard_map/all_gather | solution.py:35
  131.9 1.3 collective-permute-start.1
  144.7 1.3 collective-permute-start.2
  170.6 1.3 collective-permute-start.4
  183.4 1.3 collective-permute-start.5
  196.2 1.3 collective-permute-start.6
  208.9 1.3 collective-permute-start.7
  221.7 1.3 collective-permute-start.8
  234.6 1.3 collective-permute-start.9
  247.4 1.3 collective-permute-start.10
  260.1 1.3 collective-permute-start.11
  272.9 1.3 collective-permute-start.12
  285.7 1.3 collective-permute-start.13
  298.6 69.7 %collective-permute-start.14 = (bf16[32,1024]{1,0:T(8,128)(2,1)S(1)}, bf16[32,1024]{1,0:T(8,128)(2,1)S(1)}, u32[]{:S(2)}, u32[]{:S(2)}) collective-permute-start(bf16[32,1024]{1,0:T(8,128)(2,1)S(1)} %fusion.14), channel_id=1, source_target_pairs={{32,0},{64,32},{96,64},{128,96},{33,1},{65,33},{97,65},{129,97},{3... | collective-permute-start | bytes 196616 | tf_op jit(solution)/shard_map/ppermute | solution.py:61
  380.3 9.8 %collective-permute-start.15 = (bf16[32,1024]{1,0:T(8,128)(2,1)S(1)}, bf16[32,1024]{1,0:T(8,128)(2,1)S(1)}, u32[]{:S(2)}, u32[]{:S(2)}) collective-permute-start(bf16[32,1024]{1,0:T(8,128)(2,1)S(1)} %fusion.15), channel_id=1, source_target_pairs={{32,0},{64,32},{96,64},{33,1},{65,33},{97,65},{34,2},{66,34},{98,6... | collective-permute-start | bytes 196616 | tf_op jit(solution)/shard_map/ppermute | solution.py:61
  401.5 9.8 %collective-permute-start.16 = (bf16[32,1024]{1,0:T(8,128)(2,1)S(1)}, bf16[32,1024]{1,0:T(8,128)(2,1)S(1)}, u32[]{:S(2)}, u32[]{:S(2)}) collective-permute-start(bf16[32,1024]{1,0:T(8,128)(2,1)S(1)} %fusion.16), channel_id=1, source_target_pairs={{32,0},{64,32},{33,1},{65,33},{34,2},{66,34},{35,3},{67,35},{36,4}... | collective-permute-start | bytes 196616 | tf_op jit(solution)/shard_map/ppermute | solution.py:61
  422.7 6.2 %collective-permute-start.17 = (bf16[32,1024]{1,0:T(8,128)(2,1)S(1)}, bf16[32,1024]{1,0:T(8,128)(2,1)S(1)}, u32[]{:S(2)}, u32[]{:S(2)}) collective-permute-start(bf16[32,1024]{1,0:T(8,128)(2,1)S(1)} %fusion.17), channel_id=1, source_target_pairs={{32,0},{33,1},{34,2},{35,3},{36,4},{37,5},{38,6},{39,7},{40,8},{41... | collective-permute-start | bytes 196616 | tf_op jit(solution)/shard_map/ppermute | solution.py:61
  435.9 5.6 %collective-permute-start.18 = (f32[16,8,4]{0,2,1:T(4,128)S(1)}, f32[16,8,4]{0,2,1:T(4,128)S(1)}, u32[]{:S(2)}, u32[]{:S(2)}) collective-permute-start(f32[16,8,4]{0,2,1:T(4,128)S(1)} %broadcast_select_fusion), channel_id=1, source_target_pairs={{0,32},{4,36},{8,40},{12,44},{16,48},{20,52},{24,56},{28,60},{32,0... | collective-permute-start | bytes 6152 | tf_op jit(solution)/shard_map/ppermute | solution.py:106
  441.5 6.5 %collective-permute-start.19 = (f32[16,8,4]{0,2,1:T(4,128)S(1)}, f32[16,8,4]{0,2,1:T(4,128)S(1)}, u32[]{:S(2)}, u32[]{:S(2)}) collective-permute-start(f32[16,8,4]{0,2,1:T(4,128)S(1)} %fusion.140), channel_id=1, source_target_pairs={{0,64},{4,68},{8,72},{12,76},{16,80},{20,84},{24,88},{28,92},{32,9... | collective-permute-start | bytes 6152 | tf_op jit(solution)/shard_map/ppermute | solution.py:106
  448.1 9.5 %collective-permute-start.20 = (f32[16,8,4]{0,2,1:T(4,128)S(1)}, f32[16,8,4]{0,2,1:T(4,128)S(1)}, u32[]{:S(2)}, u32[]{:S(2)}) collective-permute-start(f32[16,8,4]{0,2,1:T(4,128)S(1)} %fusion.272), channel_id=1, source_target_pairs={{0,128},{4,132},{8,136},{12,140},{16,144},{20,148},{24,152},{28,15... | collective-permute-start | bytes 6152 | tf_op jit(solution)/shard_map/ppermute | solution.py:106
  457.6 7.1 %collective-permute-start.21 = (f32[16,8,4]{0,2,1:T(4,128)S(1)}, f32[16,8,4]{0,2,1:T(4,128)S(1)}, u32[]{:S(2)}, u32[]{:S(2)}) collective-permute-start(f32[16,8,4]{0,2,1:T(4,128)S(1)} %add.340), channel_id=1, source_target_pairs={{0,256},{4,260},{8,264},{12,268},{16,272},{20,276},{24,280},{28,28... | collective-permute-start | bytes 6152 | tf_op jit(solution)/shard_map/ppermute | solution.py:106
  464.8 5.6 %collective-permute-start.22 = (f32[16,8,4]{0,2,1:T(4,128)S(1)}, f32[16,8,4]{0,2,1:T(4,128)S(1)}, u32[]{:S(2)}, u32[]{:S(2)}) collective-permute-start(f32[16,8,4]{0,2,1:T(4,128)S(1)} %add.341), channel_id=1, source_target_pairs={{0,4},{4,0},{8,12},{12,8},{16,20},{20,16},{24,28},{28,24},{32,36},... | collective-permute-start | bytes 6152 | tf_op jit(solution)/shard_map/ppermute | solution.py:106
  470.4 6.5 %collective-permute-start.23 = (f32[16,8,4]{0,2,1:T(4,128)S(1)}, f32[16,8,4]{0,2,1:T(4,128)S(1)}, u32[]{:S(2)}, u32[]{:S(2)}) collective-permute-start(f32[16,8,4]{0,2,1:T(4,128)S(1)} %add.342), channel_id=1, source_target_pairs={{0,8},{4,12},{8,0},{12,4},{16,24},{20,28},{24,16},{28,20},{32,40},... | collective-permute-start | bytes 6152 | tf_op jit(solution)/shard_map/ppermute | solution.py:106
  476.9 9.5 %collective-permute-start.24 = (f32[16,8,4]{0,2,1:T(4,128)S(1)}, f32[16,8,4]{0,2,1:T(4,128)S(1)}, u32[]{:S(2)}, u32[]{:S(2)}) collective-permute-start(f32[16,8,4]{0,2,1:T(4,128)S(1)} %add.343), channel_id=1, source_target_pairs={{0,16},{4,20},{8,24},{12,28},{16,0},{20,4},{24,8},{28,12},{32,48},... | collective-permute-start | bytes 6152 | tf_op jit(solution)/shard_map/ppermute | solution.py:106
  (5 other events, 89.3 us)
Sparse Core Ops, SparseCore 0:
  10.1 104.7 all-gather.4

commit v9 on v6

--- a/solution.py
+++ b/solution.py
@@ -42,8 +42,7 @@
     asked = queries.shape[0] * data_count
     queries = lax.all_gather(queries, "dp", axis=0, tiled=True)
 
-    panel_store = jnp.zeros((CHUNKS, chunk_examples, piece_rank * low_rank), jnp.float32)
-    score_store = jnp.zeros((CHUNKS, asked, chunk_examples), jnp.float32)
+    grad_store = jnp.zeros((CHUNKS, chunk, piece * model_count), jnp.bfloat16)
     outgoing = jnp.zeros((chunk, piece), jnp.bfloat16)
     is_top = section_index == top_section
     step_count = CHUNKS + section_count - 1
@@ -69,30 +68,24 @@
             back_term = jnp.dot(grad_full, w_cols, preferred_element_type=jnp.float32)
             outgoing = (delta_piece.astype(jnp.float32) + back_term).astype(jnp.bfloat16)
 
-        out_side = jnp.dot(grad_full, out_proj, preferred_element_type=jnp.float32)
-        in_chunk = lax.dynamic_slice_in_dim(in_side, row_start, chunk, 0)
-        whole = jnp.einsum(
-            "etr,etc->erc",
-            in_chunk.reshape(chunk_examples, length, low_rank),
-            out_side.reshape(chunk_examples, length, low_rank),
-            precision=lax.Precision.HIGHEST,
-        ) / math.sqrt(length)
-        partial = jnp.dot(
-            queries, whole.reshape(chunk_examples, low_rank * low_rank).T, precision=lax.Precision.HIGHEST
-        )
-        panels = lax.dynamic_slice_in_dim(whole, model_index * piece_rank, piece_rank, 1)
-        panels = panels.reshape(chunk_examples, piece_rank * low_rank)
-        old_panels = lax.dynamic_index_in_dim(panel_store, clipped, 0, keepdims=False)
-        panel_store = lax.dynamic_update_index_in_dim(
-            panel_store, jnp.where(active, panels, old_panels), clipped, 0
-        )
-        old_scores = lax.dynamic_index_in_dim(score_store, clipped, 0, keepdims=False)
-        score_store = lax.dynamic_update_index_in_dim(
-            score_store, jnp.where(active, partial, old_scores), clipped, 0
+        previous = lax.dynamic_index_in_dim(grad_store, clipped, 0, keepdims=False)
+        grad_store = lax.dynamic_update_index_in_dim(
+            grad_store, jnp.where(active, grad_full, previous), clipped, 0
         )
 
-    panels_here = panel_store.reshape(examples, piece_rank * low_rank)
-    mine = score_store.transpose(1, 0, 2).reshape(asked, examples)
+    grads = grad_store.reshape(tokens, piece * model_count)
+    out_side = jnp.dot(grads, out_proj, preferred_element_type=jnp.float32)
+    whole = jnp.einsum(
+        "etr,etc->erc",
+        in_side.reshape(examples, length, low_rank),
+        out_side.reshape(examples, length, low_rank),
+        precision=lax.Precision.HIGHEST,
+    ) / math.sqrt(length)
+    mine = jnp.dot(
+        queries, whole.reshape(examples, low_rank * low_rank).T, precision=lax.Precision.HIGHEST
+    )
+    panels_here = lax.dynamic_slice_in_dim(whole, model_index * piece_rank, piece_rank, 1)
+    panels_here = panels_here.reshape(examples, piece_rank * low_rank)
     score_scale = 1.0 / (low_rank * math.sqrt(section_count))
     per_dp = asked // data_count
     owner = jnp.arange(asked) // per_dp

time: 500 us -> 457 us (0.914)
  the two profiles are of different devices: /device:TPU:2 before, /device:TPU:56 now
where the time goes in v9:
time: 457 us; the launch traced here: 449 us
  blocking collectives  172 us (38%)
  waiting for transfers between devices  146 us (32%)
  starting transfers between devices  68.8 us (15%)
  matrix products  35.4 us (8%)
  between operations  15.1 us (3%)
  local copies, waits for them, and re-layouts  6.17 us (1%)
  other arithmetic  5.9 us (1%)
    all_gather x17, blocking collectives, body(): grad_full = lax.all_gather(grad_piece, 'mp', axis=1, tiled=True)  122 us
    all_gather x1, waiting for transfers between devices, body(): w_cols = lax.all_gather(weights[0].T, 'dp', axis=0, tiled=True)  69.9 us
    ppermute x16, waiting for transfers between devices, body(): received = lax.ppermute(outgoing, 'section', [(k, k - 1) for k in senders])  55.6 us
    ppermute x7, starting transfers between devices, body(): scores = scores + lax.ppermute(scores, ('section', 'dp'), route)  55.6 us
    dot_general x16, matrix products, body(): back_term = jnp.dot(grad_full, w_cols, preferred_element_type=jnp.float32)  33 us
    all_gather x1, blocking collectives, body(): queries = lax.all_gather(queries, 'dp', axis=0, tiled=True)  24.8 us
    ppermute x7, waiting for transfers between devices, body(): scores = scores + lax.ppermute(scores, ('section', 'dp'), route)  20.7 us
    ppermute x16, starting transfers between devices, body(): received = lax.ppermute(outgoing, 'section', [(k, k - 1) for k in senders])  13.2 us
  transfers between devices with their start and end apart: 24, of which 11 were waited for; matrix products, arithmetic and copies ran while one was open for 2% of the time, Pallas kernels for 0%

profile of v9, /device:TPU:56, one launch (start us, length us, event | category | flops | bytes accessed | tf_op | source)
XLA Modules:
  0.0 449.4 jit_solution(187343591266637994)
XLA Ops:
  12.2 12.5 %psum.7 = f32[4,32,64]{2,1,0:T(8,128)} all-reduce(f32[4,32,64]{2,1,0:T(8,128)S(1)} %bitcast.163), channel_id=1, replica_groups=mesh['section'=16,'dp'=8,'mp'=4] {'mp'}, use_global_device_ids=true, to_apply=%region_0.0 | all-reduce | flops 8192 | bytes 65536 | tf_op jit(solution)/shard_map/psum | solution.py:40
  33.4 7.5 %all-gather = bf16[1,4096,64]{1,2,0:T(8,128)(2,1)S(1)} all-gather(bf16[1,1024,64]{1,2,0:T(8,128)(2,1)} %param.13), channel_id=2, replica_groups=mesh['section'=16,'dp'=8,'mp'=4] {'mp'}, dimensions={1}, use_global_device_ids=true | all-gather | bytes 655360 | tf_op jit(solution)/shard_map/all_gather | solution.py:38
  41.9 69.9 %all-gather.5.cloned.1.call-done = bf16[4096,1024]{1,0:T(8,128)(2,1)} async-done(((bf16[512,1024]{1,0:T(8,128)(2,1)}), bf16[4096,1024]{1,0:T(8,128)(2,1)}) %all-gather.5.cloned.1.call-update) | async-done | bytes 8388624 | tf_op jit(solution)/shard_map/all_gather | solution.py:35
  123.4 24.8 %all-gather.2 = f32[1,16,4096]{2,0,1:T(1,128)S(1)} all-gather(f32[1,2,4096]{2,0,1:T(1,128)S(1)} %all-gather.1), channel_id=4, replica_groups=mesh['section'=16,'dp'=8,'mp'=4] {'dp'}, dimensions={1}, use_global_device_ids=true | all-gather | bytes 294912 | tf_op jit(solution)/shard_map/all_gather | solution.py:43
  148.2 7.3 %all_gather.65 = bf16[64,4096]{1,0:T(8,128)(2,1)S(1)} all-gather(bf16[64,1024]{1,0:T(8,128)(2,1)S(1)} %fusion.25), channel_id=1, replica_groups=mesh['section'=16,'dp'=8,'mp'=4] {'mp'}, dimensions={1}, use_global_device_ids=true | all-gather | bytes 655360 | tf_op jit(solution)/shard_map/all_gather | solution.py:66
  161.6 7.3 %all_gather.66 = bf16[64,4096]{1,0:T(8,128)(2,1)S(1)} all-gather(bf16[64,1024]{1,0:T(8,128)(2,1)S(1)} %fusion.26), channel_id=1, replica_groups=mesh['section'=16,'dp'=8,'mp'=4] {'mp'}, dimensions={1}, use_global_device_ids=true | all-gather | bytes 655360 | tf_op jit(solution)/shard_map/all_gather | solution.py:66
  171.4 7.3 %all_gather.67 = bf16[64,4096]{1,0:T(8,128)(2,1)S(1)} all-gather(bf16[64,1024]{1,0:T(8,128)(2,1)S(1)} %fusion.27), channel_id=1, replica_groups=mesh['section'=16,'dp'=8,'mp'=4] {'mp'}, dimensions={1}, use_global_device_ids=true | all-gather | bytes 655360 | tf_op jit(solution)/shard_map/all_gather | solution.py:66
  181.2 7.3 %all_gather.68 = bf16[64,4096]{1,0:T(8,128)(2,1)S(1)} all-gather(bf16[64,1024]{1,0:T(8,128)(2,1)S(1)} %fusion.28), channel_id=1, replica_groups=mesh['section'=16,'dp'=8,'mp'=4] {'mp'}, dimensions={1}, use_global_device_ids=true | all-gather | bytes 655360 | tf_op jit(solution)/shard_map/all_gather | solution.py:66
  191.1 7.5 %all_gather.69 = bf16[64,4096]{1,0:T(8,128)(2,1)S(1)} all-gather(bf16[64,1024]{1,0:T(8,128)(2,1)S(1)} %fusion.29), channel_id=1, replica_groups=mesh['section'=16,'dp'=8,'mp'=4] {'mp'}, dimensions={1}, use_global_device_ids=true | all-gather | bytes 655360 | tf_op jit(solution)/shard_map/all_gather | solution.py:66
  201.1 7.3 %all_gather.70 = bf16[64,4096]{1,0:T(8,128)(2,1)S(1)} all-gather(bf16[64,1024]{1,0:T(8,128)(2,1)S(1)} %fusion.30), channel_id=1, replica_groups=mesh['section'=16,'dp'=8,'mp'=4] {'mp'}, dimensions={1}, use_global_device_ids=true | all-gather | bytes 655360 | tf_op jit(solution)/shard_map/all_gather | solution.py:66
  210.9 7.3 %all_gather.71 = bf16[64,4096]{1,0:T(8,128)(2,1)S(1)} all-gather(bf16[64,1024]{1,0:T(8,128)(2,1)S(1)} %fusion.31), channel_id=1, replica_groups=mesh['section'=16,'dp'=8,'mp'=4] {'mp'}, dimensions={1}, use_global_device_ids=true | all-gather | bytes 655360 | tf_op jit(solution)/shard_map/all_gather | solution.py:66
  221.3 43.1 %collective-permute-done.7 = bf16[64,1024]{1,0:T(8,128)(2,1)S(1)} collective-permute-done((bf16[64,1024]{1,0:T(8,128)(2,1)S(1)}, bf16[64,1024]{1,0:T(8,128)(2,1)S(1)}, u32[]{:S(2)}, u32[]{:S(2)}) %collective-permute-start.7) | collective-permute-done | bytes 131104 | tf_op jit(solution)/shard_map/ppermute | solution.py:60
  274.8 9.1 %collective-permute-done.8 = bf16[64,1024]{1,0:T(8,128)(2,1)S(1)} collective-permute-done((bf16[64,1024]{1,0:T(8,128)(2,1)S(1)}, bf16[64,1024]{1,0:T(8,128)(2,1)S(1)}, u32[]{:S(2)}, u32[]{:S(2)}) %collective-permute-start.8) | collective-permute-done | bytes 131104 | tf_op jit(solution)/shard_map/ppermute | solution.py:60
  284.0 6.8 %all_gather.73 = bf16[64,4096]{1,0:T(8,128)(2,1)S(1)} all-gather(bf16[64,1024]{1,0:T(8,128)(2,1)S(1)} %fusion.33), channel_id=1, replica_groups=mesh['section'=16,'dp'=8,'mp'=4] {'mp'}, dimensions={1}, use_global_device_ids=true | all-gather | bytes 655360 | tf_op jit(solution)/shard_map/all_gather | solution.py:66
  297.3 6.7 %all_gather.74 = bf16[64,4096]{1,0:T(8,128)(2,1)S(1)} all-gather(bf16[64,1024]{1,0:T(8,128)(2,1)S(1)} %fusion.34), channel_id=1, replica_groups=mesh['section'=16,'dp'=8,'mp'=4] {'mp'}, dimensions={1}, use_global_device_ids=true | all-gather | bytes 655360 | tf_op jit(solution)/shard_map/all_gather | solution.py:66
  306.6 7.5 %all_gather.75 = bf16[64,4096]{1,0:T(8,128)(2,1)S(1)} all-gather(bf16[64,1024]{1,0:T(8,128)(2,1)S(1)} %fusion.35), channel_id=1, replica_groups=mesh['section'=16,'dp'=8,'mp'=4] {'mp'}, dimensions={1}, use_global_device_ids=true | all-gather | bytes 655360 | tf_op jit(solution)/shard_map/all_gather | solution.py:66
  316.6 7.3 %all_gather.76 = bf16[64,4096]{1,0:T(8,128)(2,1)S(1)} all-gather(bf16[64,1024]{1,0:T(8,128)(2,1)S(1)} %fusion.36), channel_id=1, replica_groups=mesh['section'=16,'dp'=8,'mp'=4] {'mp'}, dimensions={1}, use_global_device_ids=true | all-gather | bytes 655360 | tf_op jit(solution)/shard_map/all_gather | solution.py:66
  326.4 7.3 %all_gather.77 = bf16[64,4096]{1,0:T(8,128)(2,1)S(1)} all-gather(bf16[64,1024]{1,0:T(8,128)(2,1)S(1)} %fusion.37), channel_id=1, replica_groups=mesh['section'=16,'dp'=8,'mp'=4] {'mp'}, dimensions={1}, use_global_device_ids=true | all-gather | bytes 655360 | tf_op jit(solution)/shard_map/all_gather | solution.py:66
  336.3 7.3 %all_gather.78 = bf16[64,4096]{1,0:T(8,128)(2,1)S(1)} all-gather(bf16[64,1024]{1,0:T(8,128)(2,1)S(1)} %fusion.38), channel_id=1, replica_groups=mesh['section'=16,'dp'=8,'mp'=4] {'mp'}, dimensions={1}, use_global_device_ids=true | all-gather | bytes 655360 | tf_op jit(solution)/shard_map/all_gather | solution.py:66
  346.1 7.3 %all_gather.79 = bf16[64,4096]{1,0:T(8,128)(2,1)S(1)} all-gather(bf16[64,1024]{1,0:T(8,128)(2,1)S(1)} %fusion.39), channel_id=1, replica_groups=mesh['section'=16,'dp'=8,'mp'=4] {'mp'}, dimensions={1}, use_global_device_ids=true | all-gather | bytes 655360 | tf_op jit(solution)/shard_map/all_gather | solution.py:66
  355.9 7.3 %all_gather.80 = bf16[64,4096]{1,0:T(8,128)(2,1)S(1)} all-gather(bf16[64,1024]{1,0:T(8,128)(2,1)S(1)} %multiply_convert_fusion), channel_id=1, replica_groups=mesh['section'=16,'dp'=8,'mp'=4] {'mp'}, dimensions={1}, use_global_device_ids=true | all-gather | bytes 655360 | tf_op jit(solution)/shard_map/all_gather | solution.py:66
  364.8 7.8 %collective-permute-start.16 = (f32[16,8,4]{0,2,1:T(4,128)S(1)}, f32[16,8,4]{0,2,1:T(4,128)S(1)}, u32[]{:S(2)}, u32[]{:S(2)}) collective-permute-start(f32[16,8,4]{0,2,1:T(4,128)S(1)} %broadcast_select_fusion), channel_id=1, source_target_pairs={{0,32},{4,36},{8,40},{12,44},{16,48},{20,52},{24,56},{28,60},{32,0... | collective-permute-start | bytes 6152 | tf_op jit(solution)/shard_map/ppermute | solution.py:99
  374.3 13.1 %collective-permute-start.17 = (f32[16,8,4]{0,2,1:T(4,128)S(1)}, f32[16,8,4]{0,2,1:T(4,128)S(1)}, u32[]{:S(2)}, u32[]{:S(2)}) collective-permute-start(f32[16,8,4]{0,2,1:T(4,128)S(1)} %fusion.45), channel_id=1, source_target_pairs={{0,64},{4,68},{8,72},{12,76},{16,80},{20,84},{24,88},{28,92},{32,9... | collective-permute-start | bytes 6152 | tf_op jit(solution)/shard_map/ppermute | solution.py:99
  389.2 22.1 %collective-permute-start.18 = (f32[16,8,4]{0,2,1:T(4,128)S(1)}, f32[16,8,4]{0,2,1:T(4,128)S(1)}, u32[]{:S(2)}, u32[]{:S(2)}) collective-permute-start(f32[16,8,4]{0,2,1:T(4,128)S(1)} %fusion.83), channel_id=1, source_target_pairs={{0,128},{4,132},{8,136},{12,140},{16,144},{20,148},{24,152},{28,15... | collective-permute-start | bytes 6152 | tf_op jit(solution)/shard_map/ppermute | solution.py:99
  (152 shorter events, 115.7 us)
Async XLA Ops:
  7.2 104.5 %all-gather.5.cloned.1.call-start = ((), (), s32[]{:S(2)}) async-start(), calls=%async_computation | async-start | bytes 9437184 | tf_op jit(solution)/shard_map/all_gather | solution.py:35
  117.3 30.8 %collective-permute-start = (bf16[64,1024]{1,0:T(8,128)(2,1)}, bf16[64,1024]{1,0:T(8,128)(2,1)S(1)}, u32[]{:S(2)}, u32[]{:S(2)}) collective-permute-start(bf16[64,1024]{1,0:T(8,128)(2,1)} %fusion), channel_id=1, source_target_pairs={{480,448},{481,449},{482,450},{483,451},{484,452},{485,453},{486,4... | collective-permute-start | bytes 393224 | tf_op jit(solution)/shard_map/ppermute | solution.py:60
  160.6 0.9 collective-permute-start.1
  170.5 0.9 collective-permute-start.2
  180.3 0.9 collective-permute-start.3
  190.1 0.9 collective-permute-start.4
  200.1 0.9 collective-permute-start.5
  210.0 0.9 collective-permute-start.6
  219.8 44.6 %collective-permute-start.7 = (bf16[64,1024]{1,0:T(8,128)(2,1)S(1)}, bf16[64,1024]{1,0:T(8,128)(2,1)S(1)}, u32[]{:S(2)}, u32[]{:S(2)}) collective-permute-start(bf16[64,1024]{1,0:T(8,128)(2,1)S(1)} %fusion.7), channel_id=1, source_target_pairs={{256,224},{288,256},{257,225},{289,257},{258,226},{290,258},{259,2... | collective-permute-start | bytes 393224 | tf_op jit(solution)/shard_map/ppermute | solution.py:60
  272.7 11.3 %collective-permute-start.8 = (bf16[64,1024]{1,0:T(8,128)(2,1)S(1)}, bf16[64,1024]{1,0:T(8,128)(2,1)S(1)}, u32[]{:S(2)}, u32[]{:S(2)}) collective-permute-start(bf16[64,1024]{1,0:T(8,128)(2,1)S(1)} %fusion.8), channel_id=1, source_target_pairs={{224,192},{256,224},{225,193},{257,225},{226,194},{258,226},{227,1... | collective-permute-start | bytes 393224 | tf_op jit(solution)/shard_map/ppermute | solution.py:60
  292.4 4.8 %collective-permute-start.9 = (bf16[64,1024]{1,0:T(8,128)(2,1)S(1)}, bf16[64,1024]{1,0:T(8,128)(2,1)S(1)}, u32[]{:S(2)}, u32[]{:S(2)}) collective-permute-start(bf16[64,1024]{1,0:T(8,128)(2,1)S(1)} %fusion.9), channel_id=1, source_target_pairs={{192,160},{224,192},{193,161},{225,193},{194,162},{226,194},{195,1... | collective-permute-start | bytes 393224 | tf_op jit(solution)/shard_map/ppermute | solution.py:60
  305.6 0.9 collective-permute-start.10
  315.7 0.9 collective-permute-start.11
  325.5 0.9 collective-permute-start.12
  335.3 0.9 collective-permute-start.13
  345.1 0.9 collective-permute-start.14
  355.0 0.9 collective-permute-start.15
  364.8 9.5 %collective-permute-start.16 = (f32[16,8,4]{0,2,1:T(4,128)S(1)}, f32[16,8,4]{0,2,1:T(4,128)S(1)}, u32[]{:S(2)}, u32[]{:S(2)}) collective-permute-start(f32[16,8,4]{0,2,1:T(4,128)S(1)} %broadcast_select_fusion), channel_id=1, source_target_pairs={{0,32},{4,36},{8,40},{12,44},{16,48},{20,52},{24,56},{28,60},{32,0... | collective-permute-start | bytes 6152 | tf_op jit(solution)/shard_map/ppermute | solution.py:99
  374.3 14.9 %collective-permute-start.17 = (f32[16,8,4]{0,2,1:T(4,128)S(1)}, f32[16,8,4]{0,2,1:T(4,128)S(1)}, u32[]{:S(2)}, u32[]{:S(2)}) collective-permute-start(f32[16,8,4]{0,2,1:T(4,128)S(1)} %fusion.45), channel_id=1, source_target_pairs={{0,64},{4,68},{8,72},{12,76},{16,80},{20,84},{24,88},{28,92},{32,9... | collective-permute-start | bytes 6152 | tf_op jit(solution)/shard_map/ppermute | solution.py:99
  389.2 23.8 %collective-permute-start.18 = (f32[16,8,4]{0,2,1:T(4,128)S(1)}, f32[16,8,4]{0,2,1:T(4,128)S(1)}, u32[]{:S(2)}, u32[]{:S(2)}) collective-permute-start(f32[16,8,4]{0,2,1:T(4,128)S(1)} %fusion.83), channel_id=1, source_target_pairs={{0,128},{4,132},{8,136},{12,140},{16,144},{20,148},{24,152},{28,15... | collective-permute-start | bytes 6152 | tf_op jit(solution)/shard_map/ppermute | solution.py:99
  413.1 7.1 %collective-permute-start.19 = (f32[16,8,4]{0,2,1:T(4,128)S(1)}, f32[16,8,4]{0,2,1:T(4,128)S(1)}, u32[]{:S(2)}, u32[]{:S(2)}) collective-permute-start(f32[16,8,4]{0,2,1:T(4,128)S(1)} %add.241), channel_id=1, source_target_pairs={{0,256},{4,260},{8,264},{12,268},{16,272},{20,276},{24,280},{28,28... | collective-permute-start | bytes 6152 | tf_op jit(solution)/shard_map/ppermute | solution.py:99
  420.2 5.6 %collective-permute-start.20 = (f32[16,8,4]{0,2,1:T(4,128)S(1)}, f32[16,8,4]{0,2,1:T(4,128)S(1)}, u32[]{:S(2)}, u32[]{:S(2)}) collective-permute-start(f32[16,8,4]{0,2,1:T(4,128)S(1)} %add.242), channel_id=1, source_target_pairs={{0,4},{4,0},{8,12},{12,8},{16,20},{20,16},{24,28},{28,24},{32,36},... | collective-permute-start | bytes 6152 | tf_op jit(solution)/shard_map/ppermute | solution.py:99
  425.8 6.5 %collective-permute-start.21 = (f32[16,8,4]{0,2,1:T(4,128)S(1)}, f32[16,8,4]{0,2,1:T(4,128)S(1)}, u32[]{:S(2)}, u32[]{:S(2)}) collective-permute-start(f32[16,8,4]{0,2,1:T(4,128)S(1)} %add.243), channel_id=1, source_target_pairs={{0,8},{4,12},{8,0},{12,4},{16,24},{20,28},{24,16},{28,20},{32,40},... | collective-permute-start | bytes 6152 | tf_op jit(solution)/shard_map/ppermute | solution.py:99
  432.4 9.5 %collective-permute-start.22 = (f32[16,8,4]{0,2,1:T(4,128)S(1)}, f32[16,8,4]{0,2,1:T(4,128)S(1)}, u32[]{:S(2)}, u32[]{:S(2)}) collective-permute-start(f32[16,8,4]{0,2,1:T(4,128)S(1)} %add.244), channel_id=1, source_target_pairs={{0,16},{4,20},{8,24},{12,28},{16,0},{20,4},{24,8},{28,12},{32,48},... | collective-permute-start | bytes 6152 | tf_op jit(solution)/shard_map/ppermute | solution.py:99
  (7 other events, 235.0 us)
Sparse Core Ops, SparseCore 0:
  10.1 101.5 all-gather.4

commit v10 on v9

--- a/solution.py
+++ b/solution.py
@@ -42,7 +42,7 @@
     asked = queries.shape[0] * data_count
     queries = lax.all_gather(queries, "dp", axis=0, tiled=True)
 
-    grad_store = jnp.zeros((CHUNKS, chunk, piece * model_count), jnp.bfloat16)
+    grad_store = jnp.zeros((CHUNKS + 1, chunk, piece * model_count), jnp.bfloat16)
     outgoing = jnp.zeros((chunk, piece), jnp.bfloat16)
     is_top = section_index == top_section
     step_count = CHUNKS + section_count - 1
@@ -68,12 +68,10 @@
             back_term = jnp.dot(grad_full, w_cols, preferred_element_type=jnp.float32)
             outgoing = (delta_piece.astype(jnp.float32) + back_term).astype(jnp.bfloat16)
 
-        previous = lax.dynamic_index_in_dim(grad_store, clipped, 0, keepdims=False)
-        grad_store = lax.dynamic_update_index_in_dim(
-            grad_store, jnp.where(active, grad_full, previous), clipped, 0
-        )
+        slot = jnp.where(active, clipped, CHUNKS)
+        grad_store = lax.dynamic_update_index_in_dim(grad_store, grad_full, slot, 0)
 
-    grads = grad_store.reshape(tokens, piece * model_count)
+    grads = grad_store[:CHUNKS].reshape(tokens, piece * model_count)
     out_side = jnp.dot(grads, out_proj, preferred_element_type=jnp.float32)
     whole = jnp.einsum(
         "etr,etc->erc",

time: 457 us -> 457 us (level)
  waiting for transfers between devices: 146 us -> 152 us
  transfers between devices with their start and end apart: 24 -> 24, of which waited for: 11 -> 11; matrix products, arithmetic and copies ran while one was open for 2% -> 1% of each run, Pallas kernels for 0% -> 0%
where the time goes in v10:
time: 457 us; the launch traced here: 450 us
  blocking collectives  171 us (37%)
  waiting for transfers between devices  152 us (33%)
  starting transfers between devices  70.2 us (15%)
  matrix products  33.9 us (7%)
  between operations  15.1 us (3%)
  local copies, waits for them, and re-layouts  5.79 us (1%)
    all_gather x17, blocking collectives, body(): grad_full = lax.all_gather(grad_piece, 'mp', axis=1, tiled=True)  122 us
    all_gather x1, waiting for transfers between devices, body(): w_cols = lax.all_gather(weights[0].T, 'dp', axis=0, tiled=True)  74.3 us
    ppermute x16, waiting for transfers between devices, body(): received = lax.ppermute(outgoing, 'section', [(k, k - 1) for k in senders])  57.1 us
    ppermute x7, starting transfers between devices, body(): scores = scores + lax.ppermute(scores, ('section', 'dp'), route)  56.9 us
    dot_general x16, matrix products, body(): back_term = jnp.dot(grad_full, w_cols, preferred_element_type=jnp.float32)  32.4 us
    all_gather x1, blocking collectives, body(): queries = lax.all_gather(queries, 'dp', axis=0, tiled=True)  24.8 us
    ppermute x7, waiting for transfers between devices, body(): scores = scores + lax.ppermute(scores, ('section', 'dp'), route)  20.3 us
    ppermute x16, starting transfers between devices, body(): received = lax.ppermute(outgoing, 'section', [(k, k - 1) for k in senders])  13.2 us
  transfers between devices with their start and end apart: 24, of which 11 were waited for; matrix products, arithmetic and copies ran while one was open for 1% of the time, Pallas kernels for 0%

profile of v10, /device:TPU:56, one launch (start us, length us, event | category | flops | bytes accessed | tf_op | source)
XLA Modules:
  0.0 449.9 jit_solution(9595020677702445456)
XLA Ops:
  10.7 12.0 %psum.7 = f32[4,32,64]{2,1,0:T(8,128)S(1)} all-reduce(f32[4,32,64]{2,1,0:T(8,128)S(1)} %bitcast.99), channel_id=1, replica_groups=mesh['section'=16,'dp'=8,'mp'=4] {'mp'}, use_global_device_ids=true, to_apply=%region_0.0 | all-reduce | flops 8192 | bytes 65536 | tf_op jit(solution)/shard_map/psum | solution.py:40
  29.5 7.7 %all-gather = bf16[1,4096,64]{1,2,0:T(8,128)(2,1)} all-gather(bf16[1,1024,64]{1,2,0:T(8,128)(2,1)S(1)} %copy-done.5), channel_id=2, replica_groups=mesh['section'=16,'dp'=8,'mp'=4] {'mp'}, dimensions={1}, use_global_device_ids=true | all-gather | bytes 655360 | tf_op jit(solution)/shard_map/all_gather | solution.py:38
  37.4 74.3 %all-gather.5.cloned.1.call-done = bf16[4096,1024]{1,0:T(8,128)(2,1)} async-done(((bf16[512,1024]{1,0:T(8,128)(2,1)}), bf16[4096,1024]{1,0:T(8,128)(2,1)}) %all-gather.5.cloned.1.call-update) | async-done | bytes 8388624 | tf_op jit(solution)/shard_map/all_gather | solution.py:35
  122.8 24.8 %all-gather.2 = f32[1,16,4096]{2,0,1:T(1,128)S(1)} all-gather(f32[1,2,4096]{2,0,1:T(1,128)S(1)} %all-gather.1), channel_id=4, replica_groups=mesh['section'=16,'dp'=8,'mp'=4] {'dp'}, dimensions={1}, use_global_device_ids=true | all-gather | bytes 294912 | tf_op jit(solution)/shard_map/all_gather | solution.py:43
  147.6 7.3 %all_gather.65 = bf16[64,4096]{1,0:T(8,128)(2,1)S(1)} all-gather(bf16[64,1024]{1,0:T(8,128)(2,1)S(1)} %fusion.25), channel_id=1, replica_groups=mesh['section'=16,'dp'=8,'mp'=4] {'mp'}, dimensions={1}, use_global_device_ids=true | all-gather | bytes 655360 | tf_op jit(solution)/shard_map/all_gather | solution.py:66
  160.8 7.3 %all_gather.66 = bf16[64,4096]{1,0:T(8,128)(2,1)S(1)} all-gather(bf16[64,1024]{1,0:T(8,128)(2,1)S(1)} %fusion.26), channel_id=1, replica_groups=mesh['section'=16,'dp'=8,'mp'=4] {'mp'}, dimensions={1}, use_global_device_ids=true | all-gather | bytes 655360 | tf_op jit(solution)/shard_map/all_gather | solution.py:66
  170.5 7.3 %all_gather.67 = bf16[64,4096]{1,0:T(8,128)(2,1)S(1)} all-gather(bf16[64,1024]{1,0:T(8,128)(2,1)S(1)} %fusion.27), channel_id=1, replica_groups=mesh['section'=16,'dp'=8,'mp'=4] {'mp'}, dimensions={1}, use_global_device_ids=true | all-gather | bytes 655360 | tf_op jit(solution)/shard_map/all_gather | solution.py:66
  180.2 7.3 %all_gather.68 = bf16[64,4096]{1,0:T(8,128)(2,1)S(1)} all-gather(bf16[64,1024]{1,0:T(8,128)(2,1)S(1)} %fusion.28), channel_id=1, replica_groups=mesh['section'=16,'dp'=8,'mp'=4] {'mp'}, dimensions={1}, use_global_device_ids=true | all-gather | bytes 655360 | tf_op jit(solution)/shard_map/all_gather | solution.py:66
  189.9 7.5 %all_gather.69 = bf16[64,4096]{1,0:T(8,128)(2,1)S(1)} all-gather(bf16[64,1024]{1,0:T(8,128)(2,1)S(1)} %fusion.29), channel_id=1, replica_groups=mesh['section'=16,'dp'=8,'mp'=4] {'mp'}, dimensions={1}, use_global_device_ids=true | all-gather | bytes 655360 | tf_op jit(solution)/shard_map/all_gather | solution.py:66
  199.8 7.3 %all_gather.70 = bf16[64,4096]{1,0:T(8,128)(2,1)S(1)} all-gather(bf16[64,1024]{1,0:T(8,128)(2,1)S(1)} %fusion.30), channel_id=1, replica_groups=mesh['section'=16,'dp'=8,'mp'=4] {'mp'}, dimensions={1}, use_global_device_ids=true | all-gather | bytes 655360 | tf_op jit(solution)/shard_map/all_gather | solution.py:66
  209.4 7.3 %all_gather.71 = bf16[64,4096]{1,0:T(8,128)(2,1)S(1)} all-gather(bf16[64,1024]{1,0:T(8,128)(2,1)S(1)} %fusion.31), channel_id=1, replica_groups=mesh['section'=16,'dp'=8,'mp'=4] {'mp'}, dimensions={1}, use_global_device_ids=true | all-gather | bytes 655360 | tf_op jit(solution)/shard_map/all_gather | solution.py:66
  219.7 44.2 %collective-permute-done.7 = bf16[64,1024]{1,0:T(8,128)(2,1)S(1)} collective-permute-done((bf16[64,1024]{1,0:T(8,128)(2,1)S(1)}, bf16[64,1024]{1,0:T(8,128)(2,1)S(1)}, u32[]{:S(2)}, u32[]{:S(2)}) %collective-permute-start.7) | collective-permute-done | bytes 131104 | tf_op jit(solution)/shard_map/ppermute | solution.py:60
  274.1 9.4 %collective-permute-done.8 = bf16[64,1024]{1,0:T(8,128)(2,1)S(1)} collective-permute-done((bf16[64,1024]{1,0:T(8,128)(2,1)S(1)}, bf16[64,1024]{1,0:T(8,128)(2,1)S(1)}, u32[]{:S(2)}, u32[]{:S(2)}) %collective-permute-start.8) | collective-permute-done | bytes 131104 | tf_op jit(solution)/shard_map/ppermute | solution.py:60
  283.6 6.7 %all_gather.73 = bf16[64,4096]{1,0:T(8,128)(2,1)S(1)} all-gather(bf16[64,1024]{1,0:T(8,128)(2,1)S(1)} %fusion.33), channel_id=1, replica_groups=mesh['section'=16,'dp'=8,'mp'=4] {'mp'}, dimensions={1}, use_global_device_ids=true | all-gather | bytes 655360 | tf_op jit(solution)/shard_map/all_gather | solution.py:66
  296.8 6.7 %all_gather.74 = bf16[64,4096]{1,0:T(8,128)(2,1)S(1)} all-gather(bf16[64,1024]{1,0:T(8,128)(2,1)S(1)} %fusion.34), channel_id=1, replica_groups=mesh['section'=16,'dp'=8,'mp'=4] {'mp'}, dimensions={1}, use_global_device_ids=true | all-gather | bytes 655360 | tf_op jit(solution)/shard_map/all_gather | solution.py:66
  305.9 7.3 %all_gather.75 = bf16[64,4096]{1,0:T(8,128)(2,1)S(1)} all-gather(bf16[64,1024]{1,0:T(8,128)(2,1)S(1)} %fusion.35), channel_id=1, replica_groups=mesh['section'=16,'dp'=8,'mp'=4] {'mp'}, dimensions={1}, use_global_device_ids=true | all-gather | bytes 655360 | tf_op jit(solution)/shard_map/all_gather | solution.py:66
  315.6 7.5 %all_gather.76 = bf16[64,4096]{1,0:T(8,128)(2,1)S(1)} all-gather(bf16[64,1024]{1,0:T(8,128)(2,1)S(1)} %fusion.36), channel_id=1, replica_groups=mesh['section'=16,'dp'=8,'mp'=4] {'mp'}, dimensions={1}, use_global_device_ids=true | all-gather | bytes 655360 | tf_op jit(solution)/shard_map/all_gather | solution.py:66
  325.5 7.3 %all_gather.77 = bf16[64,4096]{1,0:T(8,128)(2,1)S(1)} all-gather(bf16[64,1024]{1,0:T(8,128)(2,1)S(1)} %fusion.37), channel_id=1, replica_groups=mesh['section'=16,'dp'=8,'mp'=4] {'mp'}, dimensions={1}, use_global_device_ids=true | all-gather | bytes 655360 | tf_op jit(solution)/shard_map/all_gather | solution.py:66
  335.2 7.3 %all_gather.78 = bf16[64,4096]{1,0:T(8,128)(2,1)S(1)} all-gather(bf16[64,1024]{1,0:T(8,128)(2,1)S(1)} %fusion.38), channel_id=1, replica_groups=mesh['section'=16,'dp'=8,'mp'=4] {'mp'}, dimensions={1}, use_global_device_ids=true | all-gather | bytes 655360 | tf_op jit(solution)/shard_map/all_gather | solution.py:66
  344.9 7.3 %all_gather.79 = bf16[64,4096]{1,0:T(8,128)(2,1)S(1)} all-gather(bf16[64,1024]{1,0:T(8,128)(2,1)S(1)} %fusion.39), channel_id=1, replica_groups=mesh['section'=16,'dp'=8,'mp'=4] {'mp'}, dimensions={1}, use_global_device_ids=true | all-gather | bytes 655360 | tf_op jit(solution)/shard_map/all_gather | solution.py:66
  354.6 7.3 %all_gather.80 = bf16[64,4096]{1,0:T(8,128)(2,1)S(1)} all-gather(bf16[64,1024]{1,0:T(8,128)(2,1)S(1)} %multiply_convert_fusion), channel_id=1, replica_groups=mesh['section'=16,'dp'=8,'mp'=4] {'mp'}, dimensions={1}, use_global_device_ids=true | all-gather | bytes 655360 | tf_op jit(solution)/shard_map/all_gather | solution.py:66
  364.3 7.9 %collective-permute-start.16 = (f32[16,8,4]{0,2,1:T(4,128)S(1)}, f32[16,8,4]{0,2,1:T(4,128)S(1)}, u32[]{:S(2)}, u32[]{:S(2)}) collective-permute-start(f32[16,8,4]{0,2,1:T(4,128)S(1)} %broadcast_select_fusion), channel_id=1, source_target_pairs={{0,32},{4,36},{8,40},{12,44},{16,48},{20,52},{24,56},{28,60},{32,0... | collective-permute-start | bytes 6152 | tf_op jit(solution)/shard_map/ppermute | solution.py:97
  374.0 13.4 %collective-permute-start.17 = (f32[16,8,4]{0,2,1:T(4,128)S(1)}, f32[16,8,4]{0,2,1:T(4,128)S(1)}, u32[]{:S(2)}, u32[]{:S(2)}) collective-permute-start(f32[16,8,4]{0,2,1:T(4,128)S(1)} %fusion.45), channel_id=1, source_target_pairs={{0,64},{4,68},{8,72},{12,76},{16,80},{20,84},{24,88},{28,92},{32,9... | collective-permute-start | bytes 6152 | tf_op jit(solution)/shard_map/ppermute | solution.py:97
  389.3 22.6 %collective-permute-start.18 = (f32[16,8,4]{0,2,1:T(4,128)S(1)}, f32[16,8,4]{0,2,1:T(4,128)S(1)}, u32[]{:S(2)}, u32[]{:S(2)}) collective-permute-start(f32[16,8,4]{0,2,1:T(4,128)S(1)} %fusion.83), channel_id=1, source_target_pairs={{0,128},{4,132},{8,136},{12,140},{16,144},{20,148},{24,152},{28,15... | collective-permute-start | bytes 6152 | tf_op jit(solution)/shard_map/ppermute | solution.py:97
  (143 shorter events, 109.8 us)
Async XLA Ops:
  7.2 104.5 %all-gather.5.cloned.1.call-start = ((), (), s32[]{:S(2)}) async-start(), calls=%async_computation | async-start | bytes 9437184 | tf_op jit(solution)/shard_map/all_gather | solution.py:35
  116.7 30.8 %collective-permute-start = (bf16[64,1024]{1,0:T(8,128)(2,1)S(1)}, bf16[64,1024]{1,0:T(8,128)(2,1)S(1)}, u32[]{:S(2)}, u32[]{:S(2)}) collective-permute-start(bf16[64,1024]{1,0:T(8,128)(2,1)S(1)} %fusion), channel_id=1, source_target_pairs={{480,448},{481,449},{482,450},{483,451},{484,452},{485,453},{486,4... | collective-permute-start | bytes 393224 | tf_op jit(solution)/shard_map/ppermute | solution.py:60
  160.0 0.7 collective-permute-start.1
  169.7 0.7 collective-permute-start.2
  179.4 0.7 collective-permute-start.3
  189.1 0.7 collective-permute-start.4
  199.0 0.7 collective-permute-start.5
  208.7 0.7 collective-permute-start.6
  218.3 45.5 %collective-permute-start.7 = (bf16[64,1024]{1,0:T(8,128)(2,1)S(1)}, bf16[64,1024]{1,0:T(8,128)(2,1)S(1)}, u32[]{:S(2)}, u32[]{:S(2)}) collective-permute-start(bf16[64,1024]{1,0:T(8,128)(2,1)S(1)} %fusion.7), channel_id=1, source_target_pairs={{256,224},{288,256},{257,225},{289,257},{258,226},{290,258},{259,2... | collective-permute-start | bytes 393224 | tf_op jit(solution)/shard_map/ppermute | solution.py:60
  272.2 11.4 %collective-permute-start.8 = (bf16[64,1024]{1,0:T(8,128)(2,1)S(1)}, bf16[64,1024]{1,0:T(8,128)(2,1)S(1)}, u32[]{:S(2)}, u32[]{:S(2)}) collective-permute-start(bf16[64,1024]{1,0:T(8,128)(2,1)S(1)} %fusion.8), channel_id=1, source_target_pairs={{224,192},{256,224},{225,193},{257,225},{226,194},{258,226},{227,1... | collective-permute-start | bytes 393224 | tf_op jit(solution)/shard_map/ppermute | solution.py:60
  291.9 4.8 %collective-permute-start.9 = (bf16[64,1024]{1,0:T(8,128)(2,1)S(1)}, bf16[64,1024]{1,0:T(8,128)(2,1)S(1)}, u32[]{:S(2)}, u32[]{:S(2)}) collective-permute-start(bf16[64,1024]{1,0:T(8,128)(2,1)S(1)} %fusion.9), channel_id=1, source_target_pairs={{192,160},{224,192},{193,161},{225,193},{194,162},{226,194},{195,1... | collective-permute-start | bytes 393224 | tf_op jit(solution)/shard_map/ppermute | solution.py:60
  305.1 0.7 collective-permute-start.10
  314.8 0.7 collective-permute-start.11
  324.7 0.7 collective-permute-start.12
  334.4 0.7 collective-permute-start.13
  344.1 0.7 collective-permute-start.14
  353.8 0.7 collective-permute-start.15
  364.3 9.6 %collective-permute-start.16 = (f32[16,8,4]{0,2,1:T(4,128)S(1)}, f32[16,8,4]{0,2,1:T(4,128)S(1)}, u32[]{:S(2)}, u32[]{:S(2)}) collective-permute-start(f32[16,8,4]{0,2,1:T(4,128)S(1)} %broadcast_select_fusion), channel_id=1, source_target_pairs={{0,32},{4,36},{8,40},{12,44},{16,48},{20,52},{24,56},{28,60},{32,0... | collective-permute-start | bytes 6152 | tf_op jit(solution)/shard_map/ppermute | solution.py:97
  374.0 15.3 %collective-permute-start.17 = (f32[16,8,4]{0,2,1:T(4,128)S(1)}, f32[16,8,4]{0,2,1:T(4,128)S(1)}, u32[]{:S(2)}, u32[]{:S(2)}) collective-permute-start(f32[16,8,4]{0,2,1:T(4,128)S(1)} %fusion.45), channel_id=1, source_target_pairs={{0,64},{4,68},{8,72},{12,76},{16,80},{20,84},{24,88},{28,92},{32,9... | collective-permute-start | bytes 6152 | tf_op jit(solution)/shard_map/ppermute | solution.py:97
  389.3 24.3 %collective-permute-start.18 = (f32[16,8,4]{0,2,1:T(4,128)S(1)}, f32[16,8,4]{0,2,1:T(4,128)S(1)}, u32[]{:S(2)}, u32[]{:S(2)}) collective-permute-start(f32[16,8,4]{0,2,1:T(4,128)S(1)} %fusion.83), channel_id=1, source_target_pairs={{0,128},{4,132},{8,136},{12,140},{16,144},{20,148},{24,152},{28,15... | collective-permute-start | bytes 6152 | tf_op jit(solution)/shard_map/ppermute | solution.py:97
  413.6 7.1 %collective-permute-start.19 = (f32[16,8,4]{0,2,1:T(4,128)S(1)}, f32[16,8,4]{0,2,1:T(4,128)S(1)}, u32[]{:S(2)}, u32[]{:S(2)}) collective-permute-start(f32[16,8,4]{0,2,1:T(4,128)S(1)} %add.223), channel_id=1, source_target_pairs={{0,256},{4,260},{8,264},{12,268},{16,272},{20,276},{24,280},{28,28... | collective-permute-start | bytes 6152 | tf_op jit(solution)/shard_map/ppermute | solution.py:97
  420.7 5.6 %collective-permute-start.20 = (f32[16,8,4]{0,2,1:T(4,128)S(1)}, f32[16,8,4]{0,2,1:T(4,128)S(1)}, u32[]{:S(2)}, u32[]{:S(2)}) collective-permute-start(f32[16,8,4]{0,2,1:T(4,128)S(1)} %add.224), channel_id=1, source_target_pairs={{0,4},{4,0},{8,12},{12,8},{16,20},{20,16},{24,28},{28,24},{32,36},... | collective-permute-start | bytes 6152 | tf_op jit(solution)/shard_map/ppermute | solution.py:97
  426.4 6.5 %collective-permute-start.21 = (f32[16,8,4]{0,2,1:T(4,128)S(1)}, f32[16,8,4]{0,2,1:T(4,128)S(1)}, u32[]{:S(2)}, u32[]{:S(2)}) collective-permute-start(f32[16,8,4]{0,2,1:T(4,128)S(1)} %add.225), channel_id=1, source_target_pairs={{0,8},{4,12},{8,0},{12,4},{16,24},{20,28},{24,16},{28,20},{32,40},... | collective-permute-start | bytes 6152 | tf_op jit(solution)/shard_map/ppermute | solution.py:97
  432.9 9.5 %collective-permute-start.22 = (f32[16,8,4]{0,2,1:T(4,128)S(1)}, f32[16,8,4]{0,2,1:T(4,128)S(1)}, u32[]{:S(2)}, u32[]{:S(2)}) collective-permute-start(f32[16,8,4]{0,2,1:T(4,128)S(1)} %add.226), channel_id=1, source_target_pairs={{0,16},{4,20},{8,24},{12,28},{16,0},{20,4},{24,8},{28,12},{32,48},... | collective-permute-start | bytes 6152 | tf_op jit(solution)/shard_map/ppermute | solution.py:97
  (10 other events, 172.8 us)
Sparse Core Ops, SparseCore 0:
  10.1 101.5 all-gather.4

commit v11 on v9

--- a/solution.py
+++ b/solution.py
@@ -7,7 +7,7 @@
 from jax.sharding import PartitionSpec as P
 
 LEN = 32
-CHUNKS = 2
+CHUNKS = 4
 
 
 def silu_slope(pre_state):

time: 457 us -> 459 us (level)
  waiting for transfers between devices: 146 us -> 162 us
  blocking collectives: 172 us -> 160 us
    all_gather x17 -> x19, blocking collectives: 122 us -> 112 us  [body(): grad_full = lax.all_gather(grad_piece, 'mp', axis=1, tiled=True)]
    all_gather x1, waiting for transfers between devices: 69.9 us -> 78.2 us  [body(): w_cols = lax.all_gather(weights[0].T, 'dp', axis=0, tiled=True)]
    ppermute x16 -> x18, waiting for transfers between devices: 55.6 us -> 62.6 us  [body(): received = lax.ppermute(outgoing, 'section', [(k, k - 1) for k in senders])]
    ppermute x7, starting transfers between devices: 55.6 us -> 49.6 us  [body(): scores = scores + lax.ppermute(scores, ('section', 'dp'), route)]
    ppermute x16 -> x18, starting transfers between devices: 13.2 us -> 17 us  [body(): received = lax.ppermute(outgoing, 'section', [(k, k - 1) for k in senders])]
    dot_general x16 -> x18, matrix products: 33 us -> 34.9 us  [body(): back_term = jnp.dot(grad_full, w_cols, preferred_element_type=jnp.float32)]
  transfers between devices with their start and end apart: 24 -> 26, of which waited for: 11 -> 13; matrix products, arithmetic and copies ran while one was open for 2% -> 2% of each run, Pallas kernels for 0% -> 0%
where the time goes in v11:
time: 459 us; the launch traced here: 452 us
  waiting for transfers between devices  162 us (35%)
  blocking collectives  160 us (35%)
  starting transfers between devices  66.6 us (15%)
  matrix products  37.3 us (8%)
  between operations  14.9 us (3%)
  local copies, waits for them, and re-layouts  5.82 us (1%)
    all_gather x19, blocking collectives, body(): grad_full = lax.all_gather(grad_piece, 'mp', axis=1, tiled=True)  112 us
    all_gather x1, waiting for transfers between devices, body(): w_cols = lax.all_gather(weights[0].T, 'dp', axis=0, tiled=True)  78.2 us
    ppermute x18, waiting for transfers between devices, body(): received = lax.ppermute(outgoing, 'section', [(k, k - 1) for k in senders])  62.6 us
    ppermute x7, starting transfers between devices, body(): scores = scores + lax.ppermute(scores, ('section', 'dp'), route)  49.6 us
    dot_general x18, matrix products, body(): back_term = jnp.dot(grad_full, w_cols, preferred_element_type=jnp.float32)  34.9 us
    all_gather x1, blocking collectives, body(): queries = lax.all_gather(queries, 'dp', axis=0, tiled=True)  25 us
    ppermute x7, waiting for transfers between devices, body(): scores = scores + lax.ppermute(scores, ('section', 'dp'), route)  21.7 us
    ppermute x18, starting transfers between devices, body(): received = lax.ppermute(outgoing, 'section', [(k, k - 1) for k in senders])  17 us
  transfers between devices with their start and end apart: 26, of which 13 were waited for; matrix products, arithmetic and copies ran while one was open for 2% of the time, Pallas kernels for 0%

profile of v11, /device:TPU:56, one launch (start us, length us, event | category | flops | bytes accessed | tf_op | source)
XLA Modules:
  0.0 451.6 jit_solution(2223510797415138819)
XLA Ops:
  24.7 7.5 %all-gather = bf16[1,4096,64]{1,2,0:T(8,128)(2,1)S(1)} all-gather(bf16[1,1024,64]{1,2,0:T(8,128)(2,1)} %param.13), channel_id=2, replica_groups=mesh['section'=16,'dp'=8,'mp'=4] {'mp'}, dimensions={1}, use_global_device_ids=true | all-gather | bytes 655360 | tf_op jit(solution)/shard_map/all_gather | solution.py:38
  33.6 78.2 %all-gather.5.cloned.1.call-done = bf16[4096,1024]{1,0:T(8,128)(2,1)} async-done(((bf16[512,1024]{1,0:T(8,128)(2,1)}), bf16[4096,1024]{1,0:T(8,128)(2,1)}) %all-gather.5.cloned.1.call-update) | async-done | bytes 8388624 | tf_op jit(solution)/shard_map/all_gather | solution.py:35
  117.3 25.0 %all-gather.2 = f32[1,16,4096]{2,0,1:T(1,128)S(1)} all-gather(f32[1,2,4096]{2,0,1:T(1,128)S(1)} %all-gather.1), channel_id=4, replica_groups=mesh['section'=16,'dp'=8,'mp'=4] {'dp'}, dimensions={1}, use_global_device_ids=true | all-gather | bytes 294912 | tf_op jit(solution)/shard_map/all_gather | solution.py:43
  142.3 10.7 %psum.7 = f32[4,32,64]{2,1,0:T(8,128)S(1)} all-reduce(f32[4,32,64]{2,1,0:T(8,128)S(1)} %bitcast.177), channel_id=1, replica_groups=mesh['section'=16,'dp'=8,'mp'=4] {'mp'}, use_global_device_ids=true, to_apply=%region_0.0 | all-reduce | flops 8192 | bytes 65536 | tf_op jit(solution)/shard_map/psum | solution.py:40
  153.1 6.2 %all_gather.71 = bf16[32,4096]{1,0:T(8,128)(2,1)S(1)} all-gather(bf16[32,1024]{1,0:T(8,128)(2,1)S(1)} %fusion.31), channel_id=1, replica_groups=mesh['section'=16,'dp'=8,'mp'=4] {'mp'}, dimensions={1}, use_global_device_ids=true | all-gather | bytes 327680 | tf_op jit(solution)/shard_map/all_gather | solution.py:66
  165.2 5.9 %all_gather.72 = bf16[32,4096]{1,0:T(8,128)(2,1)S(1)} all-gather(bf16[32,1024]{1,0:T(8,128)(2,1)S(1)} %fusion.32), channel_id=1, replica_groups=mesh['section'=16,'dp'=8,'mp'=4] {'mp'}, dimensions={1}, use_global_device_ids=true | all-gather | bytes 327680 | tf_op jit(solution)/shard_map/all_gather | solution.py:66
  173.4 5.9 %all_gather.73 = bf16[32,4096]{1,0:T(8,128)(2,1)S(1)} all-gather(bf16[32,1024]{1,0:T(8,128)(2,1)S(1)} %fusion.33), channel_id=1, replica_groups=mesh['section'=16,'dp'=8,'mp'=4] {'mp'}, dimensions={1}, use_global_device_ids=true | all-gather | bytes 327680 | tf_op jit(solution)/shard_map/all_gather | solution.py:66
  181.7 5.9 %all_gather.74 = bf16[32,4096]{1,0:T(8,128)(2,1)S(1)} all-gather(bf16[32,1024]{1,0:T(8,128)(2,1)S(1)} %fusion.34), channel_id=1, replica_groups=mesh['section'=16,'dp'=8,'mp'=4] {'mp'}, dimensions={1}, use_global_device_ids=true | all-gather | bytes 327680 | tf_op jit(solution)/shard_map/all_gather | solution.py:66
  189.9 6.0 %all_gather.75 = bf16[32,4096]{1,0:T(8,128)(2,1)S(1)} all-gather(bf16[32,1024]{1,0:T(8,128)(2,1)S(1)} %fusion.35), channel_id=1, replica_groups=mesh['section'=16,'dp'=8,'mp'=4] {'mp'}, dimensions={1}, use_global_device_ids=true | all-gather | bytes 327680 | tf_op jit(solution)/shard_map/all_gather | solution.py:66
  198.4 5.9 %all_gather.76 = bf16[32,4096]{1,0:T(8,128)(2,1)S(1)} all-gather(bf16[32,1024]{1,0:T(8,128)(2,1)S(1)} %fusion.36), channel_id=1, replica_groups=mesh['section'=16,'dp'=8,'mp'=4] {'mp'}, dimensions={1}, use_global_device_ids=true | all-gather | bytes 327680 | tf_op jit(solution)/shard_map/all_gather | solution.py:66
  206.6 5.9 %all_gather.77 = bf16[32,4096]{1,0:T(8,128)(2,1)S(1)} all-gather(bf16[32,1024]{1,0:T(8,128)(2,1)S(1)} %fusion.37), channel_id=1, replica_groups=mesh['section'=16,'dp'=8,'mp'=4] {'mp'}, dimensions={1}, use_global_device_ids=true | all-gather | bytes 327680 | tf_op jit(solution)/shard_map/all_gather | solution.py:66
  215.4 36.9 %collective-permute-done.7 = bf16[32,1024]{1,0:T(8,128)(2,1)S(1)} collective-permute-done((bf16[32,1024]{1,0:T(8,128)(2,1)S(1)}, bf16[32,1024]{1,0:T(8,128)(2,1)S(1)}, u32[]{:S(2)}, u32[]{:S(2)}) %collective-permute-start.7) | collective-permute-done | bytes 65568 | tf_op jit(solution)/shard_map/ppermute | solution.py:60
  261.7 7.8 %collective-permute-done.8 = bf16[32,1024]{1,0:T(8,128)(2,1)S(1)} collective-permute-done((bf16[32,1024]{1,0:T(8,128)(2,1)S(1)}, bf16[32,1024]{1,0:T(8,128)(2,1)S(1)}, u32[]{:S(2)}, u32[]{:S(2)}) %collective-permute-start.8) | collective-permute-done | bytes 65568 | tf_op jit(solution)/shard_map/ppermute | solution.py:60
  279.0 7.9 %collective-permute-done.9 = bf16[32,1024]{1,0:T(8,128)(2,1)S(1)} collective-permute-done((bf16[32,1024]{1,0:T(8,128)(2,1)S(1)}, bf16[32,1024]{1,0:T(8,128)(2,1)S(1)}, u32[]{:S(2)}, u32[]{:S(2)}) %collective-permute-start.9) | collective-permute-done | bytes 65568 | tf_op jit(solution)/shard_map/ppermute | solution.py:60
  296.3 7.9 %collective-permute-done.10 = bf16[32,1024]{1,0:T(8,128)(2,1)S(1)} collective-permute-done((bf16[32,1024]{1,0:T(8,128)(2,1)S(1)}, bf16[32,1024]{1,0:T(8,128)(2,1)S(1)}, u32[]{:S(2)}, u32[]{:S(2)}) %collective-permute-start.10) | collective-permute-done | bytes 65568 | tf_op jit(solution)/shard_map/ppermute | solution.py:60
  315.0 6.0 %all_gather.82 = bf16[32,4096]{1,0:T(8,128)(2,1)S(1)} all-gather(bf16[32,1024]{1,0:T(8,128)(2,1)S(1)} %fusion.42), channel_id=1, replica_groups=mesh['section'=16,'dp'=8,'mp'=4] {'mp'}, dimensions={1}, use_global_device_ids=true | all-gather | bytes 327680 | tf_op jit(solution)/shard_map/all_gather | solution.py:66
  323.4 5.9 %all_gather.83 = bf16[32,4096]{1,0:T(8,128)(2,1)S(1)} all-gather(bf16[32,1024]{1,0:T(8,128)(2,1)S(1)} %fusion.43), channel_id=1, replica_groups=mesh['section'=16,'dp'=8,'mp'=4] {'mp'}, dimensions={1}, use_global_device_ids=true | all-gather | bytes 327680 | tf_op jit(solution)/shard_map/all_gather | solution.py:66
  331.6 5.9 %all_gather.84 = bf16[32,4096]{1,0:T(8,128)(2,1)S(1)} all-gather(bf16[32,1024]{1,0:T(8,128)(2,1)S(1)} %fusion.44), channel_id=1, replica_groups=mesh['section'=16,'dp'=8,'mp'=4] {'mp'}, dimensions={1}, use_global_device_ids=true | all-gather | bytes 327680 | tf_op jit(solution)/shard_map/all_gather | solution.py:66
  348.1 5.9 %all_gather.86 = bf16[32,4096]{1,0:T(8,128)(2,1)S(1)} all-gather(bf16[32,1024]{1,0:T(8,128)(2,1)S(1)} %fusion.46), channel_id=1, replica_groups=mesh['section'=16,'dp'=8,'mp'=4] {'mp'}, dimensions={1}, use_global_device_ids=true | all-gather | bytes 327680 | tf_op jit(solution)/shard_map/all_gather | solution.py:66
  356.4 5.9 %all_gather.87 = bf16[32,4096]{1,0:T(8,128)(2,1)S(1)} all-gather(bf16[32,1024]{1,0:T(8,128)(2,1)S(1)} %fusion.47), channel_id=1, replica_groups=mesh['section'=16,'dp'=8,'mp'=4] {'mp'}, dimensions={1}, use_global_device_ids=true | all-gather | bytes 327680 | tf_op jit(solution)/shard_map/all_gather | solution.py:66
  364.6 5.9 %all_gather.88 = bf16[32,4096]{1,0:T(8,128)(2,1)S(1)} all-gather(bf16[32,1024]{1,0:T(8,128)(2,1)S(1)} %multiply_convert_fusion), channel_id=1, replica_groups=mesh['section'=16,'dp'=8,'mp'=4] {'mp'}, dimensions={1}, use_global_device_ids=true | all-gather | bytes 327680 | tf_op jit(solution)/shard_map/all_gather | solution.py:66
  372.0 6.9 %collective-permute-start.18 = (f32[16,8,4]{0,2,1:T(4,128)S(1)}, f32[16,8,4]{0,2,1:T(4,128)S(1)}, u32[]{:S(2)}, u32[]{:S(2)}) collective-permute-start(f32[16,8,4]{0,2,1:T(4,128)S(1)} %broadcast_select_fusion), channel_id=1, source_target_pairs={{0,32},{4,36},{8,40},{12,44},{16,48},{20,52},{24,56},{28,60},{32,0... | collective-permute-start | bytes 6152 | tf_op jit(solution)/shard_map/ppermute | solution.py:99
  380.7 11.5 %collective-permute-start.19 = (f32[16,8,4]{0,2,1:T(4,128)S(1)}, f32[16,8,4]{0,2,1:T(4,128)S(1)}, u32[]{:S(2)}, u32[]{:S(2)}) collective-permute-start(f32[16,8,4]{0,2,1:T(4,128)S(1)} %fusion.49), channel_id=1, source_target_pairs={{0,64},{4,68},{8,72},{12,76},{16,80},{20,84},{24,88},{28,92},{32,9... | collective-permute-start | bytes 6152 | tf_op jit(solution)/shard_map/ppermute | solution.py:99
  394.0 19.6 %collective-permute-start.20 = (f32[16,8,4]{0,2,1:T(4,128)S(1)}, f32[16,8,4]{0,2,1:T(4,128)S(1)}, u32[]{:S(2)}, u32[]{:S(2)}) collective-permute-start(f32[16,8,4]{0,2,1:T(4,128)S(1)} %fusion.91), channel_id=1, source_target_pairs={{0,128},{4,132},{8,136},{12,140},{16,144},{20,148},{24,152},{28,15... | collective-permute-start | bytes 6152 | tf_op jit(solution)/shard_map/ppermute | solution.py:99
  (160 shorter events, 140.0 us)
Async XLA Ops:
  7.2 104.5 %all-gather.5.cloned.1.call-start = ((), (), s32[]{:S(2)}) async-start(), calls=%async_computation | async-start | bytes 9437184 | tf_op jit(solution)/shard_map/all_gather | solution.py:35
  116.7 36.4 %collective-permute-start = (bf16[32,1024]{1,0:T(8,128)(2,1)S(1)}, bf16[32,1024]{1,0:T(8,128)(2,1)S(1)}, u32[]{:S(2)}, u32[]{:S(2)}) collective-permute-start(bf16[32,1024]{1,0:T(8,128)(2,1)S(1)} %fusion), channel_id=1, source_target_pairs={{480,448},{481,449},{482,450},{483,451},{484,452},{485,453},{486,4... | collective-permute-start | bytes 196616 | tf_op jit(solution)/shard_map/ppermute | solution.py:60
  164.3 0.8 collective-permute-start.1
  172.6 0.8 collective-permute-start.2
  180.8 0.8 collective-permute-start.3
  189.1 0.8 collective-permute-start.4
  197.5 0.8 collective-permute-start.5
  205.8 0.8 collective-permute-start.6
  214.0 38.3 %collective-permute-start.7 = (bf16[32,1024]{1,0:T(8,128)(2,1)S(1)}, bf16[32,1024]{1,0:T(8,128)(2,1)S(1)}, u32[]{:S(2)}, u32[]{:S(2)}) collective-permute-start(bf16[32,1024]{1,0:T(8,128)(2,1)S(1)} %fusion.7), channel_id=1, source_target_pairs={{256,224},{288,256},{320,288},{352,320},{257,225},{289,257},{321,2... | collective-permute-start | bytes 196616 | tf_op jit(solution)/shard_map/ppermute | solution.py:60
  259.7 9.9 %collective-permute-start.8 = (bf16[32,1024]{1,0:T(8,128)(2,1)S(1)}, bf16[32,1024]{1,0:T(8,128)(2,1)S(1)}, u32[]{:S(2)}, u32[]{:S(2)}) collective-permute-start(bf16[32,1024]{1,0:T(8,128)(2,1)S(1)} %fusion.8), channel_id=1, source_target_pairs={{224,192},{256,224},{288,256},{320,288},{225,193},{257,225},{289,2... | collective-permute-start | bytes 196616 | tf_op jit(solution)/shard_map/ppermute | solution.py:60
  276.9 9.9 %collective-permute-start.9 = (bf16[32,1024]{1,0:T(8,128)(2,1)S(1)}, bf16[32,1024]{1,0:T(8,128)(2,1)S(1)}, u32[]{:S(2)}, u32[]{:S(2)}) collective-permute-start(bf16[32,1024]{1,0:T(8,128)(2,1)S(1)} %fusion.9), channel_id=1, source_target_pairs={{192,160},{224,192},{256,224},{288,256},{193,161},{225,193},{257,2... | collective-permute-start | bytes 196616 | tf_op jit(solution)/shard_map/ppermute | solution.py:60
  294.2 9.9 %collective-permute-start.10 = (bf16[32,1024]{1,0:T(8,128)(2,1)S(1)}, bf16[32,1024]{1,0:T(8,128)(2,1)S(1)}, u32[]{:S(2)}, u32[]{:S(2)}) collective-permute-start(bf16[32,1024]{1,0:T(8,128)(2,1)S(1)} %fusion.10), channel_id=1, source_target_pairs={{160,128},{192,160},{224,192},{256,224},{161,129},{193,161},{225,1... | collective-permute-start | bytes 196616 | tf_op jit(solution)/shard_map/ppermute | solution.py:60
  311.5 3.4 collective-permute-start.11
  322.6 0.8 collective-permute-start.12
  330.8 0.8 collective-permute-start.13
  339.1 0.8 collective-permute-start.14
  347.3 0.8 collective-permute-start.15
  372.0 8.6 %collective-permute-start.18 = (f32[16,8,4]{0,2,1:T(4,128)S(1)}, f32[16,8,4]{0,2,1:T(4,128)S(1)}, u32[]{:S(2)}, u32[]{:S(2)}) collective-permute-start(f32[16,8,4]{0,2,1:T(4,128)S(1)} %broadcast_select_fusion), channel_id=1, source_target_pairs={{0,32},{4,36},{8,40},{12,44},{16,48},{20,52},{24,56},{28,60},{32,0... | collective-permute-start | bytes 6152 | tf_op jit(solution)/shard_map/ppermute | solution.py:99
  380.7 13.3 %collective-permute-start.19 = (f32[16,8,4]{0,2,1:T(4,128)S(1)}, f32[16,8,4]{0,2,1:T(4,128)S(1)}, u32[]{:S(2)}, u32[]{:S(2)}) collective-permute-start(f32[16,8,4]{0,2,1:T(4,128)S(1)} %fusion.49), channel_id=1, source_target_pairs={{0,64},{4,68},{8,72},{12,76},{16,80},{20,84},{24,88},{28,92},{32,9... | collective-permute-start | bytes 6152 | tf_op jit(solution)/shard_map/ppermute | solution.py:99
  394.0 21.3 %collective-permute-start.20 = (f32[16,8,4]{0,2,1:T(4,128)S(1)}, f32[16,8,4]{0,2,1:T(4,128)S(1)}, u32[]{:S(2)}, u32[]{:S(2)}) collective-permute-start(f32[16,8,4]{0,2,1:T(4,128)S(1)} %fusion.91), channel_id=1, source_target_pairs={{0,128},{4,132},{8,136},{12,140},{16,144},{20,148},{24,152},{28,15... | collective-permute-start | bytes 6152 | tf_op jit(solution)/shard_map/ppermute | solution.py:99
  415.3 7.1 %collective-permute-start.21 = (f32[16,8,4]{0,2,1:T(4,128)S(1)}, f32[16,8,4]{0,2,1:T(4,128)S(1)}, u32[]{:S(2)}, u32[]{:S(2)}) collective-permute-start(f32[16,8,4]{0,2,1:T(4,128)S(1)} %add.263), channel_id=1, source_target_pairs={{0,256},{4,260},{8,264},{12,268},{16,272},{20,276},{24,280},{28,28... | collective-permute-start | bytes 6152 | tf_op jit(solution)/shard_map/ppermute | solution.py:99
  422.5 5.6 %collective-permute-start.22 = (f32[16,8,4]{0,2,1:T(4,128)S(1)}, f32[16,8,4]{0,2,1:T(4,128)S(1)}, u32[]{:S(2)}, u32[]{:S(2)}) collective-permute-start(f32[16,8,4]{0,2,1:T(4,128)S(1)} %add.264), channel_id=1, source_target_pairs={{0,4},{4,0},{8,12},{12,8},{16,20},{20,16},{24,28},{28,24},{32,36},... | collective-permute-start | bytes 6152 | tf_op jit(solution)/shard_map/ppermute | solution.py:99
  428.1 6.5 %collective-permute-start.23 = (f32[16,8,4]{0,2,1:T(4,128)S(1)}, f32[16,8,4]{0,2,1:T(4,128)S(1)}, u32[]{:S(2)}, u32[]{:S(2)}) collective-permute-start(f32[16,8,4]{0,2,1:T(4,128)S(1)} %add.265), channel_id=1, source_target_pairs={{0,8},{4,12},{8,0},{12,4},{16,24},{20,28},{24,16},{28,20},{32,40},... | collective-permute-start | bytes 6152 | tf_op jit(solution)/shard_map/ppermute | solution.py:99
  434.6 9.5 %collective-permute-start.24 = (f32[16,8,4]{0,2,1:T(4,128)S(1)}, f32[16,8,4]{0,2,1:T(4,128)S(1)}, u32[]{:S(2)}, u32[]{:S(2)}) collective-permute-start(f32[16,8,4]{0,2,1:T(4,128)S(1)} %add.266), channel_id=1, source_target_pairs={{0,16},{4,20},{8,24},{12,28},{16,0},{20,4},{24,8},{28,12},{32,48},... | collective-permute-start | bytes 6152 | tf_op jit(solution)/shard_map/ppermute | solution.py:99
  (6 other events, 175.9 us)
Sparse Core Ops, SparseCore 0:
  10.1 101.5 all-gather.4

commit v12 on v11

--- a/solution.py
+++ b/solution.py
@@ -7,7 +7,7 @@
 from jax.sharding import PartitionSpec as P
 
 LEN = 32
-CHUNKS = 4
+CHUNKS = 1
 
 
 def silu_slope(pre_state):

time: 459 us -> 840 us (1.83)
  waiting for transfers between devices: 162 us -> 620 us
  blocking collectives: 160 us -> 50.2 us
  matrix products: 37.3 us -> 76.3 us
  starting transfers between devices: 66.6 us -> 48.5 us
  other arithmetic: 4.45 us -> 19 us
    all_gather x0 -> x16, waiting for transfers between devices: none -> 481 us  [body(): grad_full = lax.all_gather(grad_piece, 'mp', axis=1, tiled=True)]
    all_gather x19 -> x0, blocking collectives: 112 us -> none  [body(): grad_full = lax.all_gather(grad_piece, 'mp', axis=1, tiled=True)]
    ppermute x18 -> x15, waiting for transfers between devices: 62.6 us -> 18.7 us  [body(): received = lax.ppermute(outgoing, 'section', [(k, k - 1) for k in senders])]
    dot_general x18 -> x15, matrix products: 34.9 us -> 74.8 us  [body(): back_term = jnp.dot(grad_full, w_cols, preferred_element_type=jnp.float32)]
    all_gather x1, waiting for transfers between devices: 78.2 us -> 101 us  [body(): w_cols = lax.all_gather(weights[0].T, 'dp', axis=0, tiled=True)]
    ppermute x7, starting transfers between devices: 49.6 us -> 34 us  [body(): scores = scores + lax.ppermute(scores, ('section', 'dp'), route)]
    convert_element_type x19 -> x16, other arithmetic: 1.37 us -> 16.2 us  [body(): (delta_piece.astype(jnp.float32) * slope_rows).astype(jnp.bfloat16)]
    ppermute x18 -> x15, starting transfers between devices: 17 us -> 13.6 us  [body(): received = lax.ppermute(outgoing, 'section', [(k, k - 1) for k in senders])]
  transfers between devices with their start and end apart: 26 -> 39, of which waited for: 13 -> 25; matrix products, arithmetic and copies ran while one was open for 2% -> 0% of each run, Pallas kernels for 0% -> 0%
where the time goes in v12:
time: 840 us; the launch traced here: 833 us
  waiting for transfers between devices  620 us (74%)
  matrix products  76.3 us (9%)
  blocking collectives  50.2 us (6%)
  starting transfers between devices  48.5 us (6%)
  other arithmetic  19 us (2%)
  between operations  14.7 us (2%)
    all_gather x16, waiting for transfers between devices, body(): grad_full = lax.all_gather(grad_piece, 'mp', axis=1, tiled=True)  481 us
    all_gather x1, waiting for transfers between devices, body(): w_cols = lax.all_gather(weights[0].T, 'dp', axis=0, tiled=True)  101 us
    dot_general x15, matrix products, body(): back_term = jnp.dot(grad_full, w_cols, preferred_element_type=jnp.float32)  74.8 us
    ppermute x7, starting transfers between devices, body(): scores = scores + lax.ppermute(scores, ('section', 'dp'), route)  34 us
    all_gather x1, blocking collectives, body(): queries = lax.all_gather(queries, 'dp', axis=0, tiled=True)  26.9 us
    ppermute x7, waiting for transfers between devices, body(): scores = scores + lax.ppermute(scores, ('section', 'dp'), route)  19.9 us
    ppermute x15, waiting for transfers between devices, body(): received = lax.ppermute(outgoing, 'section', [(k, k - 1) for k in senders])  18.7 us
  transfers between devices with their start and end apart: 39, of which 25 were waited for; matrix products, arithmetic and copies ran while one was open for 0% of the time, Pallas kernels for 0%

profile of v12, /device:TPU:56, one launch (start us, length us, event | category | flops | bytes accessed | tf_op | source)
XLA Modules:
  0.0 832.8 jit_solution(13613971058043122967)
XLA Ops:
  11.6 28.5 %all-gather.21.cloned.1.call-done = bf16[128,4096]{1,0:T(8,128)(2,1)} async-done(((bf16[128,1024]{1,0:T(8,128)(2,1)}), bf16[128,4096]{1,0:T(8,128)(2,1)}) %all-gather.21.cloned.1.call-update) | async-done | bytes 1048592 | tf_op jit(solution)/shard_map/all_gather | solution.py:66
  40.2 100.7 %all-gather.23.cloned.1.call-done = bf16[4096,1024]{1,0:T(8,128)(2,1)} async-done(((bf16[512,1024]{1,0:T(8,128)(2,1)}), bf16[4096,1024]{1,0:T(8,128)(2,1)}) %all-gather.23.cloned.1.call-update) | async-done | bytes 8388624 | tf_op jit(solution)/shard_map/all_gather | solution.py:35
  147.6 31.7 %all-gather.25.cloned.1.call-done = bf16[128,4096]{1,0:T(8,128)(2,1)} async-done(((bf16[128,1024]{1,0:T(8,128)(2,1)}), bf16[128,4096]{1,0:T(8,128)(2,1)}) %all-gather.25.cloned.1.call-update) | async-done | bytes 1048592 | tf_op jit(solution)/shard_map/all_gather | solution.py:66
  185.9 35.9 %all-gather.27.cloned.1.call-done = bf16[128,4096]{1,0:T(8,128)(2,1)} async-done(((bf16[128,1024]{1,0:T(8,128)(2,1)}), bf16[128,4096]{1,0:T(8,128)(2,1)}) %all-gather.27.cloned.1.call-update) | async-done | bytes 1048592 | tf_op jit(solution)/shard_map/all_gather | solution.py:66
  228.6 36.8 %all-gather.29.cloned.1.call-done = bf16[128,4096]{1,0:T(8,128)(2,1)} async-done(((bf16[128,1024]{1,0:T(8,128)(2,1)}), bf16[128,4096]{1,0:T(8,128)(2,1)}) %all-gather.29.cloned.1.call-update) | async-done | bytes 1048592 | tf_op jit(solution)/shard_map/all_gather | solution.py:66
  272.1 35.9 %all-gather.31.cloned.1.call-done = bf16[128,4096]{1,0:T(8,128)(2,1)} async-done(((bf16[128,1024]{1,0:T(8,128)(2,1)}), bf16[128,4096]{1,0:T(8,128)(2,1)}) %all-gather.31.cloned.1.call-update) | async-done | bytes 1048592 | tf_op jit(solution)/shard_map/all_gather | solution.py:66
  314.7 33.7 %all-gather.33.cloned.1.call-done = bf16[128,4096]{1,0:T(8,128)(2,1)} async-done(((bf16[128,1024]{1,0:T(8,128)(2,1)}), bf16[128,4096]{1,0:T(8,128)(2,1)}) %all-gather.33.cloned.1.call-update) | async-done | bytes 1048592 | tf_op jit(solution)/shard_map/all_gather | solution.py:66
  355.1 32.8 %all-gather.35.cloned.1.call-done = bf16[128,4096]{1,0:T(8,128)(2,1)} async-done(((bf16[128,1024]{1,0:T(8,128)(2,1)}), bf16[128,4096]{1,0:T(8,128)(2,1)}) %all-gather.35.cloned.1.call-update) | async-done | bytes 1048592 | tf_op jit(solution)/shard_map/all_gather | solution.py:66
  394.9 31.9 %all-gather.37.cloned.1.call-done = bf16[128,4096]{1,0:T(8,128)(2,1)} async-done(((bf16[128,1024]{1,0:T(8,128)(2,1)}), bf16[128,4096]{1,0:T(8,128)(2,1)}) %all-gather.37.cloned.1.call-update) | async-done | bytes 1048592 | tf_op jit(solution)/shard_map/all_gather | solution.py:66
  433.1 12.7 %collective-permute-done.7 = bf16[128,1024]{1,0:T(8,128)(2,1)S(1)} collective-permute-done((bf16[128,1024]{1,0:T(8,128)(2,1)S(1)}, bf16[128,1024]{1,0:T(8,128)(2,1)S(1)}, u32[]{:S(2)}, u32[]{:S(2)}) %collective-permute-start.7) | collective-permute-done | bytes 262176 | tf_op jit(solution)/shard_map/ppermute | solution.py:60
  446.8 22.7 %all-gather.39.cloned.1.call-done = bf16[128,4096]{1,0:T(8,128)(2,1)} async-done(((bf16[128,1024]{1,0:T(8,128)(2,1)}), bf16[128,4096]{1,0:T(8,128)(2,1)}) %all-gather.39.cloned.1.call-update) | async-done | bytes 1048592 | tf_op jit(solution)/shard_map/all_gather | solution.py:66
  477.9 6.0 collective-permute-done.8
  484.8 24.6 %all-gather.41.cloned.1.call-done = bf16[128,4096]{1,0:T(8,128)(2,1)} async-done(((bf16[128,1024]{1,0:T(8,128)(2,1)}), bf16[128,4096]{1,0:T(8,128)(2,1)}) %all-gather.41.cloned.1.call-update) | async-done | bytes 1048592 | tf_op jit(solution)/shard_map/all_gather | solution.py:66
  516.2 34.1 %all-gather.43.cloned.1.call-done = bf16[128,4096]{1,0:T(8,128)(2,1)} async-done(((bf16[128,1024]{1,0:T(8,128)(2,1)}), bf16[128,4096]{1,0:T(8,128)(2,1)}) %all-gather.43.cloned.1.call-update) | async-done | bytes 1048592 | tf_op jit(solution)/shard_map/all_gather | solution.py:66
  557.1 35.0 %all-gather.45.cloned.1.call-done = bf16[128,4096]{1,0:T(8,128)(2,1)} async-done(((bf16[128,1024]{1,0:T(8,128)(2,1)}), bf16[128,4096]{1,0:T(8,128)(2,1)}) %all-gather.45.cloned.1.call-update) | async-done | bytes 1048592 | tf_op jit(solution)/shard_map/all_gather | solution.py:66
  598.9 34.1 %all-gather.47.cloned.1.call-done = bf16[128,4096]{1,0:T(8,128)(2,1)} async-done(((bf16[128,1024]{1,0:T(8,128)(2,1)}), bf16[128,4096]{1,0:T(8,128)(2,1)}) %all-gather.47.cloned.1.call-update) | async-done | bytes 1048592 | tf_op jit(solution)/shard_map/all_gather | solution.py:66
  639.7 32.0 %all-gather.49.cloned.1.call-done = bf16[128,4096]{1,0:T(8,128)(2,1)} async-done(((bf16[128,1024]{1,0:T(8,128)(2,1)}), bf16[128,4096]{1,0:T(8,128)(2,1)}) %all-gather.49.cloned.1.call-update) | async-done | bytes 1048592 | tf_op jit(solution)/shard_map/all_gather | solution.py:66
  678.6 30.8 %all-gather.51.cloned.1.call-done = bf16[128,4096]{1,0:T(8,128)(2,1)} async-done(((bf16[128,1024]{1,0:T(8,128)(2,1)}), bf16[128,4096]{1,0:T(8,128)(2,1)}) %all-gather.51.cloned.1.call-update) | async-done | bytes 1048592 | tf_op jit(solution)/shard_map/all_gather | solution.py:66
  722.4 11.6 %psum.7 = f32[4,32,64]{2,1,0:T(8,128)S(1)} all-reduce(f32[4,32,64]{2,1,0:T(8,128)S(1)} %bitcast.93), channel_id=1, replica_groups=mesh['section'=16,'dp'=8,'mp'=4] {'mp'}, use_global_device_ids=true, to_apply=%region_0.0 | all-reduce | flops 8192 | bytes 65536 | tf_op jit(solution)/shard_map/psum | solution.py:40
  734.0 26.9 %all-gather.2 = f32[1,16,4096]{2,0,1:T(1,128)S(1)} all-gather(f32[1,2,4096]{2,0,1:T(1,128)S(1)} %all-gather.1), channel_id=4, replica_groups=mesh['section'=16,'dp'=8,'mp'=4] {'dp'}, dimensions={1}, use_global_device_ids=true | all-gather | bytes 294912 | tf_op jit(solution)/shard_map/all_gather | solution.py:43
  760.8 6.6 all-gather
  783.2 11.9 %collective-permute-start.17 = (f32[16,8,4]{0,2,1:T(4,128)S(1)}, f32[16,8,4]{0,2,1:T(4,128)S(1)}, u32[]{:S(2)}, u32[]{:S(2)}) collective-permute-start(f32[16,8,4]{0,2,1:T(4,128)S(1)} %fusion.79), channel_id=1, source_target_pairs={{0,128},{4,132},{8,136},{12,140},{16,144},{20,148},{24,152},{28,15... | collective-permute-start | bytes 6152 | tf_op jit(solution)/shard_map/ppermute | solution.py:99
  798.7 5.2 collective-permute-done.18
  816.1 6.0 collective-permute-start.21
  (148 shorter events, 149.9 us)
Async XLA Ops:
  7.2 33.0 %all-gather.21.cloned.1.call-start = ((), (), s32[]{:S(2)}) async-start(), calls=%async_computation | async-start | bytes 1310720 | tf_op jit(solution)/shard_map/all_gather | solution.py:66
  9.2 131.7 %all-gather.23.cloned.1.call-start = ((), (), s32[]{:S(2)}) async-start(), calls=%async_computation.1 | async-start | bytes 9437184 | tf_op jit(solution)/shard_map/all_gather | solution.py:35
  11.6 167.6 %all-gather.25.cloned.1.call-start = ((), (), s32[]{:S(2)}) async-start(), calls=%async_computation.2 | async-start | bytes 1310720 | tf_op jit(solution)/shard_map/all_gather | solution.py:66
  147.5 74.4 %all-gather.27.cloned.1.call-start = ((), (), s32[]{:S(2)}) async-start(), calls=%async_computation.3 | async-start | bytes 1310720 | tf_op jit(solution)/shard_map/all_gather | solution.py:66
  185.9 79.5 %all-gather.29.cloned.1.call-start = ((), (), s32[]{:S(2)}) async-start(), calls=%async_computation.4 | async-start | bytes 1310720 | tf_op jit(solution)/shard_map/all_gather | solution.py:66
  228.5 79.5 %all-gather.31.cloned.1.call-start = ((), (), s32[]{:S(2)}) async-start(), calls=%async_computation.5 | async-start | bytes 1310720 | tf_op jit(solution)/shard_map/all_gather | solution.py:66
  272.0 76.4 %all-gather.33.cloned.1.call-start = ((), (), s32[]{:S(2)}) async-start(), calls=%async_computation.6 | async-start | bytes 1310720 | tf_op jit(solution)/shard_map/all_gather | solution.py:66
  314.6 73.3 %all-gather.35.cloned.1.call-start = ((), (), s32[]{:S(2)}) async-start(), calls=%async_computation.7 | async-start | bytes 1310720 | tf_op jit(solution)/shard_map/all_gather | solution.py:66
  355.1 71.7 %all-gather.37.cloned.1.call-start = ((), (), s32[]{:S(2)}) async-start(), calls=%async_computation.8 | async-start | bytes 1310720 | tf_op jit(solution)/shard_map/all_gather | solution.py:66
  394.8 74.7 %all-gather.39.cloned.1.call-start = ((), (), s32[]{:S(2)}) async-start(), calls=%async_computation.9 | async-start | bytes 1310720 | tf_op jit(solution)/shard_map/all_gather | solution.py:66
  431.8 14.0 %collective-permute-start.7 = (bf16[128,1024]{1,0:T(8,128)(2,1)S(1)}, bf16[128,1024]{1,0:T(8,128)(2,1)S(1)}, u32[]{:S(2)}, u32[]{:S(2)}) collective-permute-start(bf16[128,1024]{1,0:T(8,128)(2,1)S(1)} %fusion.7), channel_id=1, source_target_pairs={{256,224},{257,225},{258,226},{259,227},{260,228},{261,229},{262,2... | collective-permute-start | bytes 786440 | tf_op jit(solution)/shard_map/ppermute | solution.py:60
  446.7 62.8 %all-gather.41.cloned.1.call-start = ((), (), s32[]{:S(2)}) async-start(), calls=%async_computation.10 | async-start | bytes 1310720 | tf_op jit(solution)/shard_map/all_gather | solution.py:66
  474.5 9.3 %collective-permute-start.8 = (bf16[128,1024]{1,0:T(8,128)(2,1)S(1)}, bf16[128,1024]{1,0:T(8,128)(2,1)S(1)}, u32[]{:S(2)}, u32[]{:S(2)}) collective-permute-start(bf16[128,1024]{1,0:T(8,128)(2,1)S(1)} %fusion.8), channel_id=1, source_target_pairs={{224,192},{225,193},{226,194},{227,195},{228,196},{229,197},{230,1... | collective-permute-start | bytes 786440 | tf_op jit(solution)/shard_map/ppermute | solution.py:60
  484.8 65.5 %all-gather.43.cloned.1.call-start = ((), (), s32[]{:S(2)}) async-start(), calls=%async_computation.11 | async-start | bytes 1310720 | tf_op jit(solution)/shard_map/all_gather | solution.py:66
  516.1 76.0 %all-gather.45.cloned.1.call-start = ((), (), s32[]{:S(2)}) async-start(), calls=%async_computation.12 | async-start | bytes 1310720 | tf_op jit(solution)/shard_map/all_gather | solution.py:66
  557.1 75.9 %all-gather.47.cloned.1.call-start = ((), (), s32[]{:S(2)}) async-start(), calls=%async_computation.13 | async-start | bytes 1310720 | tf_op jit(solution)/shard_map/all_gather | solution.py:66
  598.8 72.8 %all-gather.49.cloned.1.call-start = ((), (), s32[]{:S(2)}) async-start(), calls=%async_computation.14 | async-start | bytes 1310720 | tf_op jit(solution)/shard_map/all_gather | solution.py:66
  639.6 69.8 %all-gather.51.cloned.1.call-start = ((), (), s32[]{:S(2)}) async-start(), calls=%async_computation.15 | async-start | bytes 1310720 | tf_op jit(solution)/shard_map/all_gather | solution.py:66
  678.3 89.1 %all-gather.53.cloned.1.call-start = ((), (), s32[]{:S(2)}) async-start(), calls=%async_computation.16 | async-start | bytes 1310720 | tf_op jit(solution)/shard_map/all_gather | solution.py:66
  776.6 6.5 collective-permute-start.16
  783.2 13.7 %collective-permute-start.17 = (f32[16,8,4]{0,2,1:T(4,128)S(1)}, f32[16,8,4]{0,2,1:T(4,128)S(1)}, u32[]{:S(2)}, u32[]{:S(2)}) collective-permute-start(f32[16,8,4]{0,2,1:T(4,128)S(1)} %fusion.79), channel_id=1, source_target_pairs={{0,128},{4,132},{8,136},{12,140},{16,144},{20,148},{24,152},{28,15... | collective-permute-start | bytes 6152 | tf_op jit(solution)/shard_map/ppermute | solution.py:99
  796.8 7.1 collective-permute-start.18
  809.6 6.5 collective-permute-start.20
  816.1 9.5 %collective-permute-start.21 = (f32[16,8,4]{0,2,1:T(4,128)S(1)}, f32[16,8,4]{0,2,1:T(4,128)S(1)}, u32[]{:S(2)}, u32[]{:S(2)}) collective-permute-start(f32[16,8,4]{0,2,1:T(4,128)S(1)} %add.185), channel_id=1, source_target_pairs={{0,16},{4,20},{8,24},{12,28},{16,0},{20,4},{24,8},{28,12},{32,48},... | collective-permute-start | bytes 6152 | tf_op jit(solution)/shard_map/ppermute | solution.py:99
  (24 other events, 1385.5 us)
Sparse Core Ops, SparseCore 0:
  10.1 30.0 all-gather.20
  42.3 98.5 all-gather.22
  147.6 31.5 all-gather.24
  186.0 35.8 all-gather.26
  228.6 36.6 all-gather.28
  272.2 35.7 all-gather.30
  314.8 33.6 all-gather.32
  355.2 32.7 all-gather.34
  395.0 31.7 all-gather.36
  446.9 22.6 all-gather.38
  484.9 24.5 all-gather.40
  516.3 34.0 all-gather.42
  557.2 34.9 all-gather.44
  598.9 33.9 all-gather.46
  639.7 31.8 all-gather.48
  678.4 30.9 all-gather.50
  716.2 30.0 all-gather.52

commit v13 on v9

--- a/solution.py
+++ b/solution.py
@@ -94,7 +94,7 @@
     total = section_count * data_count
     levels = list(range(total.bit_length() - 1))
     dp_levels = data_count.bit_length() - 1
-    for level in levels[dp_levels:] + levels[:dp_levels]:
+    for level in levels[:dp_levels] + levels[dp_levels:]:
         route = [(i, i ^ (1 << level)) for i in range(total)]
         scores = scores + lax.ppermute(scores, ("section", "dp"), route)
     return (panels_here[None], scores)

time: 457 us -> 457 us (level)
  no operation moved by 1% of the time
where the time goes in v13:
time: 457 us; the launch traced here: 449 us
  blocking collectives  172 us (38%)
  waiting for transfers between devices  146 us (32%)
  starting transfers between devices  68.8 us (15%)
  matrix products  35.4 us (8%)
  between operations  15.1 us (3%)
  local copies, waits for them, and re-layouts  6.17 us (1%)
  other arithmetic  5.9 us (1%)
    all_gather x17, blocking collectives, body(): grad_full = lax.all_gather(grad_piece, 'mp', axis=1, tiled=True)  122 us
    all_gather x1, waiting for transfers between devices, body(): w_cols = lax.all_gather(weights[0].T, 'dp', axis=0, tiled=True)  69.9 us
    ppermute x16, waiting for transfers between devices, body(): received = lax.ppermute(outgoing, 'section', [(k, k - 1) for k in senders])  55.6 us
    ppermute x7, starting transfers between devices, body(): scores = scores + lax.ppermute(scores, ('section', 'dp'), route)  55.6 us
    dot_general x16, matrix products, body(): back_term = jnp.dot(grad_full, w_cols, preferred_element_type=jnp.float32)  33 us
    all_gather x1, blocking collectives, body(): queries = lax.all_gather(queries, 'dp', axis=0, tiled=True)  24.8 us
    ppermute x7, waiting for transfers between devices, body(): scores = scores + lax.ppermute(scores, ('section', 'dp'), route)  20.6 us
    ppermute x16, starting transfers between devices, body(): received = lax.ppermute(outgoing, 'section', [(k, k - 1) for k in senders])  13.2 us
  transfers between devices with their start and end apart: 24, of which 11 were waited for; matrix products, arithmetic and copies ran while one was open for 2% of the time, Pallas kernels for 0%

profile of v13, /device:TPU:56, one launch (start us, length us, event | category | flops | bytes accessed | tf_op | source)
XLA Modules:
  0.0 449.3 jit_solution(11702636385224057571)
XLA Ops:
  12.2 12.5 %psum.7 = f32[4,32,64]{2,1,0:T(8,128)} all-reduce(f32[4,32,64]{2,1,0:T(8,128)S(1)} %bitcast.163), channel_id=1, replica_groups=mesh['section'=16,'dp'=8,'mp'=4] {'mp'}, use_global_device_ids=true, to_apply=%region_0.0 | all-reduce | flops 8192 | bytes 65536 | tf_op jit(solution)/shard_map/psum | solution.py:40
  33.4 7.5 %all-gather = bf16[1,4096,64]{1,2,0:T(8,128)(2,1)S(1)} all-gather(bf16[1,1024,64]{1,2,0:T(8,128)(2,1)} %param.13), channel_id=2, replica_groups=mesh['section'=16,'dp'=8,'mp'=4] {'mp'}, dimensions={1}, use_global_device_ids=true | all-gather | bytes 655360 | tf_op jit(solution)/shard_map/all_gather | solution.py:38
  41.9 69.9 %all-gather.5.cloned.1.call-done = bf16[4096,1024]{1,0:T(8,128)(2,1)} async-done(((bf16[512,1024]{1,0:T(8,128)(2,1)}), bf16[4096,1024]{1,0:T(8,128)(2,1)}) %all-gather.5.cloned.1.call-update) | async-done | bytes 8388624 | tf_op jit(solution)/shard_map/all_gather | solution.py:35
  123.4 24.8 %all-gather.2 = f32[1,16,4096]{2,0,1:T(1,128)S(1)} all-gather(f32[1,2,4096]{2,0,1:T(1,128)S(1)} %all-gather.1), channel_id=4, replica_groups=mesh['section'=16,'dp'=8,'mp'=4] {'dp'}, dimensions={1}, use_global_device_ids=true | all-gather | bytes 294912 | tf_op jit(solution)/shard_map/all_gather | solution.py:43
  148.2 7.3 %all_gather.65 = bf16[64,4096]{1,0:T(8,128)(2,1)S(1)} all-gather(bf16[64,1024]{1,0:T(8,128)(2,1)S(1)} %fusion.25), channel_id=1, replica_groups=mesh['section'=16,'dp'=8,'mp'=4] {'mp'}, dimensions={1}, use_global_device_ids=true | all-gather | bytes 655360 | tf_op jit(solution)/shard_map/all_gather | solution.py:66
  161.6 7.3 %all_gather.66 = bf16[64,4096]{1,0:T(8,128)(2,1)S(1)} all-gather(bf16[64,1024]{1,0:T(8,128)(2,1)S(1)} %fusion.26), channel_id=1, replica_groups=mesh['section'=16,'dp'=8,'mp'=4] {'mp'}, dimensions={1}, use_global_device_ids=true | all-gather | bytes 655360 | tf_op jit(solution)/shard_map/all_gather | solution.py:66
  171.4 7.3 %all_gather.67 = bf16[64,4096]{1,0:T(8,128)(2,1)S(1)} all-gather(bf16[64,1024]{1,0:T(8,128)(2,1)S(1)} %fusion.27), channel_id=1, replica_groups=mesh['section'=16,'dp'=8,'mp'=4] {'mp'}, dimensions={1}, use_global_device_ids=true | all-gather | bytes 655360 | tf_op jit(solution)/shard_map/all_gather | solution.py:66
  181.2 7.3 %all_gather.68 = bf16[64,4096]{1,0:T(8,128)(2,1)S(1)} all-gather(bf16[64,1024]{1,0:T(8,128)(2,1)S(1)} %fusion.28), channel_id=1, replica_groups=mesh['section'=16,'dp'=8,'mp'=4] {'mp'}, dimensions={1}, use_global_device_ids=true | all-gather | bytes 655360 | tf_op jit(solution)/shard_map/all_gather | solution.py:66
  191.1 7.5 %all_gather.69 = bf16[64,4096]{1,0:T(8,128)(2,1)S(1)} all-gather(bf16[64,1024]{1,0:T(8,128)(2,1)S(1)} %fusion.29), channel_id=1, replica_groups=mesh['section'=16,'dp'=8,'mp'=4] {'mp'}, dimensions={1}, use_global_device_ids=true | all-gather | bytes 655360 | tf_op jit(solution)/shard_map/all_gather | solution.py:66
  201.1 7.3 %all_gather.70 = bf16[64,4096]{1,0:T(8,128)(2,1)S(1)} all-gather(bf16[64,1024]{1,0:T(8,128)(2,1)S(1)} %fusion.30), channel_id=1, replica_groups=mesh['section'=16,'dp'=8,'mp'=4] {'mp'}, dimensions={1}, use_global_device_ids=true | all-gather | bytes 655360 | tf_op jit(solution)/shard_map/all_gather | solution.py:66
  210.9 7.3 %all_gather.71 = bf16[64,4096]{1,0:T(8,128)(2,1)S(1)} all-gather(bf16[64,1024]{1,0:T(8,128)(2,1)S(1)} %fusion.31), channel_id=1, replica_groups=mesh['section'=16,'dp'=8,'mp'=4] {'mp'}, dimensions={1}, use_global_device_ids=true | all-gather | bytes 655360 | tf_op jit(solution)/shard_map/all_gather | solution.py:66
  221.3 43.1 %collective-permute-done.7 = bf16[64,1024]{1,0:T(8,128)(2,1)S(1)} collective-permute-done((bf16[64,1024]{1,0:T(8,128)(2,1)S(1)}, bf16[64,1024]{1,0:T(8,128)(2,1)S(1)}, u32[]{:S(2)}, u32[]{:S(2)}) %collective-permute-start.7) | collective-permute-done | bytes 131104 | tf_op jit(solution)/shard_map/ppermute | solution.py:60
  274.8 9.1 %collective-permute-done.8 = bf16[64,1024]{1,0:T(8,128)(2,1)S(1)} collective-permute-done((bf16[64,1024]{1,0:T(8,128)(2,1)S(1)}, bf16[64,1024]{1,0:T(8,128)(2,1)S(1)}, u32[]{:S(2)}, u32[]{:S(2)}) %collective-permute-start.8) | collective-permute-done | bytes 131104 | tf_op jit(solution)/shard_map/ppermute | solution.py:60
  284.0 6.8 %all_gather.73 = bf16[64,4096]{1,0:T(8,128)(2,1)S(1)} all-gather(bf16[64,1024]{1,0:T(8,128)(2,1)S(1)} %fusion.33), channel_id=1, replica_groups=mesh['section'=16,'dp'=8,'mp'=4] {'mp'}, dimensions={1}, use_global_device_ids=true | all-gather | bytes 655360 | tf_op jit(solution)/shard_map/all_gather | solution.py:66
  297.3 6.7 %all_gather.74 = bf16[64,4096]{1,0:T(8,128)(2,1)S(1)} all-gather(bf16[64,1024]{1,0:T(8,128)(2,1)S(1)} %fusion.34), channel_id=1, replica_groups=mesh['section'=16,'dp'=8,'mp'=4] {'mp'}, dimensions={1}, use_global_device_ids=true | all-gather | bytes 655360 | tf_op jit(solution)/shard_map/all_gather | solution.py:66
  306.6 7.5 %all_gather.75 = bf16[64,4096]{1,0:T(8,128)(2,1)S(1)} all-gather(bf16[64,1024]{1,0:T(8,128)(2,1)S(1)} %fusion.35), channel_id=1, replica_groups=mesh['section'=16,'dp'=8,'mp'=4] {'mp'}, dimensions={1}, use_global_device_ids=true | all-gather | bytes 655360 | tf_op jit(solution)/shard_map/all_gather | solution.py:66
  316.6 7.3 %all_gather.76 = bf16[64,4096]{1,0:T(8,128)(2,1)S(1)} all-gather(bf16[64,1024]{1,0:T(8,128)(2,1)S(1)} %fusion.36), channel_id=1, replica_groups=mesh['section'=16,'dp'=8,'mp'=4] {'mp'}, dimensions={1}, use_global_device_ids=true | all-gather | bytes 655360 | tf_op jit(solution)/shard_map/all_gather | solution.py:66
  326.4 7.3 %all_gather.77 = bf16[64,4096]{1,0:T(8,128)(2,1)S(1)} all-gather(bf16[64,1024]{1,0:T(8,128)(2,1)S(1)} %fusion.37), channel_id=1, replica_groups=mesh['section'=16,'dp'=8,'mp'=4] {'mp'}, dimensions={1}, use_global_device_ids=true | all-gather | bytes 655360 | tf_op jit(solution)/shard_map/all_gather | solution.py:66
  336.3 7.3 %all_gather.78 = bf16[64,4096]{1,0:T(8,128)(2,1)S(1)} all-gather(bf16[64,1024]{1,0:T(8,128)(2,1)S(1)} %fusion.38), channel_id=1, replica_groups=mesh['section'=16,'dp'=8,'mp'=4] {'mp'}, dimensions={1}, use_global_device_ids=true | all-gather | bytes 655360 | tf_op jit(solution)/shard_map/all_gather | solution.py:66
  346.1 7.3 %all_gather.79 = bf16[64,4096]{1,0:T(8,128)(2,1)S(1)} all-gather(bf16[64,1024]{1,0:T(8,128)(2,1)S(1)} %fusion.39), channel_id=1, replica_groups=mesh['section'=16,'dp'=8,'mp'=4] {'mp'}, dimensions={1}, use_global_device_ids=true | all-gather | bytes 655360 | tf_op jit(solution)/shard_map/all_gather | solution.py:66
  355.9 7.3 %all_gather.80 = bf16[64,4096]{1,0:T(8,128)(2,1)S(1)} all-gather(bf16[64,1024]{1,0:T(8,128)(2,1)S(1)} %multiply_convert_fusion), channel_id=1, replica_groups=mesh['section'=16,'dp'=8,'mp'=4] {'mp'}, dimensions={1}, use_global_device_ids=true | all-gather | bytes 655360 | tf_op jit(solution)/shard_map/all_gather | solution.py:66
  386.6 7.7 %collective-permute-start.19 = (f32[16,8,4]{0,2,1:T(4,128)S(1)}, f32[16,8,4]{0,2,1:T(4,128)S(1)}, u32[]{:S(2)}, u32[]{:S(2)}) collective-permute-start(f32[16,8,4]{0,2,1:T(4,128)S(1)} %add.241), channel_id=1, source_target_pairs={{0,32},{4,36},{8,40},{12,44},{16,48},{20,52},{24,56},{28,60},{32,0... | collective-permute-start | bytes 6152 | tf_op jit(solution)/shard_map/ppermute | solution.py:99
  396.0 13.1 %collective-permute-start.20 = (f32[16,8,4]{0,2,1:T(4,128)S(1)}, f32[16,8,4]{0,2,1:T(4,128)S(1)}, u32[]{:S(2)}, u32[]{:S(2)}) collective-permute-start(f32[16,8,4]{0,2,1:T(4,128)S(1)} %add.242), channel_id=1, source_target_pairs={{0,64},{4,68},{8,72},{12,76},{16,80},{20,84},{24,88},{28,92},{32,9... | collective-permute-start | bytes 6152 | tf_op jit(solution)/shard_map/ppermute | solution.py:99
  410.8 22.1 %collective-permute-start.21 = (f32[16,8,4]{0,2,1:T(4,128)S(1)}, f32[16,8,4]{0,2,1:T(4,128)S(1)}, u32[]{:S(2)}, u32[]{:S(2)}) collective-permute-start(f32[16,8,4]{0,2,1:T(4,128)S(1)} %add.243), channel_id=1, source_target_pairs={{0,128},{4,132},{8,136},{12,140},{16,144},{20,148},{24,152},{28,15... | collective-permute-start | bytes 6152 | tf_op jit(solution)/shard_map/ppermute | solution.py:99
  (152 shorter events, 115.7 us)
Async XLA Ops:
  7.2 104.5 %all-gather.5.cloned.1.call-start = ((), (), s32[]{:S(2)}) async-start(), calls=%async_computation | async-start | bytes 9437184 | tf_op jit(solution)/shard_map/all_gather | solution.py:35
  117.3 30.8 %collective-permute-start = (bf16[64,1024]{1,0:T(8,128)(2,1)}, bf16[64,1024]{1,0:T(8,128)(2,1)S(1)}, u32[]{:S(2)}, u32[]{:S(2)}) collective-permute-start(bf16[64,1024]{1,0:T(8,128)(2,1)} %fusion), channel_id=1, source_target_pairs={{480,448},{481,449},{482,450},{483,451},{484,452},{485,453},{486,4... | collective-permute-start | bytes 393224 | tf_op jit(solution)/shard_map/ppermute | solution.py:60
  160.6 0.9 collective-permute-start.1
  170.5 0.9 collective-permute-start.2
  180.3 0.9 collective-permute-start.3
  190.1 0.9 collective-permute-start.4
  200.1 0.9 collective-permute-start.5
  210.0 0.9 collective-permute-start.6
  219.8 44.6 %collective-permute-start.7 = (bf16[64,1024]{1,0:T(8,128)(2,1)S(1)}, bf16[64,1024]{1,0:T(8,128)(2,1)S(1)}, u32[]{:S(2)}, u32[]{:S(2)}) collective-permute-start(bf16[64,1024]{1,0:T(8,128)(2,1)S(1)} %fusion.7), channel_id=1, source_target_pairs={{256,224},{288,256},{257,225},{289,257},{258,226},{290,258},{259,2... | collective-permute-start | bytes 393224 | tf_op jit(solution)/shard_map/ppermute | solution.py:60
  272.7 11.3 %collective-permute-start.8 = (bf16[64,1024]{1,0:T(8,128)(2,1)S(1)}, bf16[64,1024]{1,0:T(8,128)(2,1)S(1)}, u32[]{:S(2)}, u32[]{:S(2)}) collective-permute-start(bf16[64,1024]{1,0:T(8,128)(2,1)S(1)} %fusion.8), channel_id=1, source_target_pairs={{224,192},{256,224},{225,193},{257,225},{226,194},{258,226},{227,1... | collective-permute-start | bytes 393224 | tf_op jit(solution)/shard_map/ppermute | solution.py:60
  292.4 4.8 %collective-permute-start.9 = (bf16[64,1024]{1,0:T(8,128)(2,1)S(1)}, bf16[64,1024]{1,0:T(8,128)(2,1)S(1)}, u32[]{:S(2)}, u32[]{:S(2)}) collective-permute-start(bf16[64,1024]{1,0:T(8,128)(2,1)S(1)} %fusion.9), channel_id=1, source_target_pairs={{192,160},{224,192},{193,161},{225,193},{194,162},{226,194},{195,1... | collective-permute-start | bytes 393224 | tf_op jit(solution)/shard_map/ppermute | solution.py:60
  305.6 0.9 collective-permute-start.10
  315.7 0.9 collective-permute-start.11
  325.5 0.9 collective-permute-start.12
  335.3 0.9 collective-permute-start.13
  345.1 0.9 collective-permute-start.14
  355.0 0.9 collective-permute-start.15
  364.8 5.6 %collective-permute-start.16 = (f32[16,8,4]{0,2,1:T(4,128)S(1)}, f32[16,8,4]{0,2,1:T(4,128)S(1)}, u32[]{:S(2)}, u32[]{:S(2)}) collective-permute-start(f32[16,8,4]{0,2,1:T(4,128)S(1)} %broadcast_select_fusion), channel_id=1, source_target_pairs={{0,4},{4,0},{8,12},{12,8},{16,20},{20,16},{24,28},{28,24},{32,36},... | collective-permute-start | bytes 6152 | tf_op jit(solution)/shard_map/ppermute | solution.py:99
  370.5 6.5 %collective-permute-start.17 = (f32[16,8,4]{0,2,1:T(4,128)S(1)}, f32[16,8,4]{0,2,1:T(4,128)S(1)}, u32[]{:S(2)}, u32[]{:S(2)}) collective-permute-start(f32[16,8,4]{0,2,1:T(4,128)S(1)} %fusion.45), channel_id=1, source_target_pairs={{0,8},{4,12},{8,0},{12,4},{16,24},{20,28},{24,16},{28,20},{32,40},... | collective-permute-start | bytes 6152 | tf_op jit(solution)/shard_map/ppermute | solution.py:99
  377.0 9.5 %collective-permute-start.18 = (f32[16,8,4]{0,2,1:T(4,128)S(1)}, f32[16,8,4]{0,2,1:T(4,128)S(1)}, u32[]{:S(2)}, u32[]{:S(2)}) collective-permute-start(f32[16,8,4]{0,2,1:T(4,128)S(1)} %fusion.83), channel_id=1, source_target_pairs={{0,16},{4,20},{8,24},{12,28},{16,0},{20,4},{24,8},{28,12},{32,48},... | collective-permute-start | bytes 6152 | tf_op jit(solution)/shard_map/ppermute | solution.py:99
  386.6 9.5 %collective-permute-start.19 = (f32[16,8,4]{0,2,1:T(4,128)S(1)}, f32[16,8,4]{0,2,1:T(4,128)S(1)}, u32[]{:S(2)}, u32[]{:S(2)}) collective-permute-start(f32[16,8,4]{0,2,1:T(4,128)S(1)} %add.241), channel_id=1, source_target_pairs={{0,32},{4,36},{8,40},{12,44},{16,48},{20,52},{24,56},{28,60},{32,0... | collective-permute-start | bytes 6152 | tf_op jit(solution)/shard_map/ppermute | solution.py:99
  396.0 14.8 %collective-permute-start.20 = (f32[16,8,4]{0,2,1:T(4,128)S(1)}, f32[16,8,4]{0,2,1:T(4,128)S(1)}, u32[]{:S(2)}, u32[]{:S(2)}) collective-permute-start(f32[16,8,4]{0,2,1:T(4,128)S(1)} %add.242), channel_id=1, source_target_pairs={{0,64},{4,68},{8,72},{12,76},{16,80},{20,84},{24,88},{28,92},{32,9... | collective-permute-start | bytes 6152 | tf_op jit(solution)/shard_map/ppermute | solution.py:99
  410.8 23.9 %collective-permute-start.21 = (f32[16,8,4]{0,2,1:T(4,128)S(1)}, f32[16,8,4]{0,2,1:T(4,128)S(1)}, u32[]{:S(2)}, u32[]{:S(2)}) collective-permute-start(f32[16,8,4]{0,2,1:T(4,128)S(1)} %add.243), channel_id=1, source_target_pairs={{0,128},{4,132},{8,136},{12,140},{16,144},{20,148},{24,152},{28,15... | collective-permute-start | bytes 6152 | tf_op jit(solution)/shard_map/ppermute | solution.py:99
  434.7 7.1 %collective-permute-start.22 = (f32[16,8,4]{0,2,1:T(4,128)S(1)}, f32[16,8,4]{0,2,1:T(4,128)S(1)}, u32[]{:S(2)}, u32[]{:S(2)}) collective-permute-start(f32[16,8,4]{0,2,1:T(4,128)S(1)} %add.244), channel_id=1, source_target_pairs={{0,256},{4,260},{8,264},{12,268},{16,272},{20,276},{24,280},{28,28... | collective-permute-start | bytes 6152 | tf_op jit(solution)/shard_map/ppermute | solution.py:99
  (7 other events, 235.0 us)
Sparse Core Ops, SparseCore 0:
  10.1 101.5 all-gather.4
